TPU v7x, 32 devices: a whole 2x2x4 slice. The times are simulated.
32 devices in a mesh: groups: 2 (over y), rows: 4 (over z), cols: 4 (over x, core).
Axes of the slice: x: 2, y: 2, z: 4, core: 2. Of those that a mesh axis runs over, the one named last changes fastest.
Arguments:
- points: bfloat16 [6144, 128], P(('groups', 'rows', 'cols')), parts along dimension 0, as said below
- solution: float32 [6144, 128], P(('groups', 'rows', 'cols')), parts along dimension 0, may hold values from -6 to 6
- targets: float32 [6144, 128], P(('groups', 'rows', 'cols')), parts along dimension 0, may hold values from -40 to 40, as said below
- inducing: int32 [2048], P('groups'), parts along dimension 0, may hold values from 0 to 3071, as said below
- woodbury_inverse: float32 [2048, 1024], P('groups'), parts along dimension 0, may hold values from -1 to 7, as said below
Outputs:
- new_solution: float32 [6144, 128], P(('groups', 'rows', 'cols')), parts along dimension 0
- residual: float32 [6144, 128], P(('groups', 'rows', 'cols')), parts along dimension 0
- relative_norm: float32 [256], P('groups'), parts along dimension 0
There are 2 independent parts, one for each index of `groups`. A program takes and returns all parts, laid end to end along the dimension named above; each array names one. Nothing has to cross between parts.
Inputs may be any that keep to these rules, and one draw needn't show every extreme that they name: `points`: input locations. targets of each right-hand side have their own scale. `inducing`: indices into this problem's points. `woodbury_inverse`: symmetric.
All inputs are finite; a program needn't handle non-finite values.
Results may differ from a plain program's by a relative error of at most 0.0031.
Values may be sent and summed in bfloat16 or wider, within the bound.
No kernel may reach another device: no remote copies, remote signals or barrier semaphores. Data moves between devices by JAX's collectives and lax.ppermute only.
A program may use at most 64 MiB of HBM per device.

v0:
```python
import jax
import jax.numpy as jnp
from jax import lax
from jax.sharding import PartitionSpec as P

F = 128


noise_level = 0.5

COLUMN_CHUNK = 3072


def square_norms(values):
    return jnp.sum(jnp.square(values.astype(jnp.float32)), axis=1)


def rbf_tile(left_x, left_sq, right_x, right_sq, gamma):
    inner = lax.dot_general(
        left_x, right_x, (((1,), (1,)), ((), ())), preferred_element_type=jnp.float32
    )
    return jnp.exp(-gamma * (left_sq[:, None] + right_sq[None, :] - 2.0 * inner)).astype(
        jnp.bfloat16
    )


def kernel_product(own_x, own_sq, all_x, all_sq, all_v, gamma):
    total = all_x.shape[0]
    chunk = min(COLUMN_CHUNK, total)
    if total % chunk != 0:
        chunk = total
    steps = total // chunk

    def piece(start):
        x = lax.dynamic_slice_in_dim(all_x, start, chunk, 0)
        s = lax.dynamic_slice_in_dim(all_sq, start, chunk, 0)
        v = lax.dynamic_slice_in_dim(all_v, start, chunk, 0)
        k = rbf_tile(own_x, own_sq, x, s, gamma)
        return jnp.dot(k, v, preferred_element_type=jnp.float32)

    if steps == 1:
        return piece(0)

    def body(i, acc):
        return acc + piece(i * chunk)

    init = jnp.zeros((own_x.shape[0], all_v.shape[1]), jnp.float32)
    return lax.fori_loop(0, steps, body, init)


def split_bf16(values):
    hi = lax.reduce_precision(values, exponent_bits=8, mantissa_bits=7)
    lo = values - hi
    return hi.astype(jnp.bfloat16), lo.astype(jnp.bfloat16)


PERMUTE_GROUP_MAX = 16


def is_power_of_two(n):
    return n & (n - 1) == 0


RING_AXES = ("rows",)


def uses_ring(axis):
    return axis in RING_AXES or not is_power_of_two(lax.axis_size(axis))


def axis_gather(value, axis):
    n = lax.axis_size(axis)
    if uses_ring(axis):
        moved = [value]
        for k in range(1, n):
            perm = [(i, (i + k) % n) for i in range(n)]
            moved.append(lax.ppermute(value, axis, perm))
        return [jnp.concatenate(moved, axis=0)]
    parts = [value]
    bit = n // 2
    while bit >= 1:
        perm = [(i, i ^ bit) for i in range(n)]
        held = parts[0] if len(parts) == 1 else jnp.concatenate(parts, axis=0)
        parts.append(lax.ppermute(held, axis, perm))
        bit //= 2
    return parts


def axis_piece(axis, owner):
    n = lax.axis_size(axis)
    me = lax.axis_index(axis)
    if uses_ring(axis):
        return (me - owner) % n
    d = me ^ owner
    steps = n.bit_length() - 1
    piece = jnp.zeros_like(d)
    for j in range(steps):
        piece = piece + (((d >> (steps - 1 - j)) & 1) << j)
    return piece


def gather_blocks(block):
    n = lax.axis_size("rows") * lax.axis_size("cols")
    if n > PERMUTE_GROUP_MAX:
        got = lax.all_gather(block, ("rows", "cols"), axis=0, tiled=False)
        order = relative_order(jnp.arange(n, dtype=jnp.int32))
        return [jnp.take(got, jnp.argsort(order), axis=0).reshape(-1, block.shape[1])]
    if not uses_ring("rows") or uses_ring("cols"):
        return axis_gather(jnp.concatenate(axis_gather(block, "rows"), axis=0), "cols")
    n_rows = lax.axis_size("rows")
    ring = [lax.ppermute(block, "rows", [(i, (i + k) % n_rows) for i in range(n_rows)]) for k in range(1, n_rows)]
    return pipelined_xor_gather([block, jnp.concatenate(ring, axis=0)], "cols")


def pipelined_xor_gather(parts, axis):
    n = lax.axis_size(axis)
    bit = n // 2
    while bit >= 1:
        perm = [(i, i ^ bit) for i in range(n)]
        if len(parts) == 1:
            parts = parts + [lax.ppermute(parts[0], axis, perm)]
        else:
            held = lax.ppermute(jnp.concatenate(parts[:-1], axis=0), axis, perm)
            newest = lax.ppermute(parts[-1], axis, perm)
            parts = parts + [held, newest]
        bit //= 2
    return parts


def relative_order(owner):
    n_rows = lax.axis_size("rows")
    n_cols = lax.axis_size("cols")
    return axis_piece("cols", owner % n_cols) * n_rows + axis_piece("rows", owner // n_cols)


def projected_all(all_x, all_sq, centers, centers_sq, residual_parts, gamma):
    total = all_x.shape[0]
    chunk = min(COLUMN_CHUNK, total)
    if total % chunk != 0:
        chunk = total
    steps = total // chunk
    contract = (((0,), (0,)), ((), ()))

    if steps == 1:
        c = lax.optimization_barrier(rbf_tile(all_x, all_sq, centers, centers_sq, gamma))
        total_p = None
        begin = 0
        for r in residual_parts:
            piece = lax.slice_in_dim(c, begin, begin + r.shape[0], axis=0)
            term = lax.dot_general(piece, r, contract, preferred_element_type=jnp.float32)
            total_p = term if total_p is None else total_p + term
            begin += r.shape[0]
        return total_p

    residual_b_all = jnp.concatenate(residual_parts, axis=0)

    def piece(start):
        x = lax.dynamic_slice_in_dim(all_x, start, chunk, 0)
        s = lax.dynamic_slice_in_dim(all_sq, start, chunk, 0)
        r = lax.dynamic_slice_in_dim(residual_b_all, start, chunk, 0)
        c = rbf_tile(x, s, centers, centers_sq, gamma)
        return lax.dot_general(c, r, contract, preferred_element_type=jnp.float32)

    def body(i, acc):
        return acc + piece(i * chunk)

    init = jnp.zeros((centers.shape[0], residual_b_all.shape[1]), jnp.float32)
    return lax.fori_loop(0, steps, body, init)


def local(points, solution, targets, inducing, woodbury_inverse):
    gamma = 2.5 / F
    n_local = points.shape[0]
    solution_b = solution.astype(jnp.bfloat16)
    packed = jnp.concatenate([points, solution_b], axis=1)
    parts = gather_blocks(packed)
    own_sq = square_norms(points)
    kp = None
    for part in parts:
        part_x = part[:, :F]
        term = kernel_product(points, own_sq, part_x, square_norms(part_x), part[:, F:], gamma)
        kp = term if kp is None else kp + term
    residual = targets - kp - noise_level * solution
    all_x = jnp.concatenate([part[:, :F] for part in parts], axis=0)
    all_sq = square_norms(all_x)
    owner = inducing // n_local
    position = relative_order(owner) * n_local + inducing % n_local
    centers = jnp.take(all_x, position, axis=0)
    centers_sq = square_norms(centers)
    cross = rbf_tile(points, own_sq, centers, centers_sq, gamma)
    residual_b = residual.astype(jnp.bfloat16)
    res_local = jnp.sum(residual * residual, axis=0)
    tar_local = jnp.sum(targets * targets, axis=0)
    hi, lo = split_bf16(jnp.stack([res_local, tar_local]))
    extra = jnp.zeros((16, residual_b.shape[1]), jnp.bfloat16).at[0:2].set(hi).at[2:4].set(lo)
    sent = jnp.concatenate([residual_b, extra], axis=0)
    width = sent.shape[1]
    gathered_sent = gather_blocks(sent)
    got_parts = [g.reshape(-1, sent.shape[0], width) for g in gathered_sent]
    norms = sum(
        jnp.sum(g[:, n_local:n_local + 2].astype(jnp.float32) + g[:, n_local + 2:n_local + 4].astype(jnp.float32), axis=0)
        for g in got_parts
    )
    res_sq = norms[0]
    tar_sq = norms[1]
    residual_parts = [g[:, :n_local].reshape(-1, width) for g in got_parts]
    projected = projected_all(all_x, all_sq, centers, centers_sq, residual_parts, gamma)
    w_hi, w_lo = split_bf16(woodbury_inverse)
    p_hi, p_lo = split_bf16(projected)
    weights = (
        jnp.dot(w_hi, p_hi, preferred_element_type=jnp.float32)
        + jnp.dot(w_hi, p_lo, preferred_element_type=jnp.float32)
        + jnp.dot(w_lo, p_hi, preferred_element_type=jnp.float32)
    )
    correction = jnp.dot(cross, weights.astype(jnp.bfloat16), preferred_element_type=jnp.float32)
    new_solution = solution + (residual - correction) / noise_level
    relative_norm = jnp.sqrt(res_sq / (tar_sq + 1e-06))
    return (new_solution, residual, relative_norm)


def solution(mesh):
    return jax.shard_map(
        local,
        mesh=mesh,
        in_specs=(
            P(("groups", "rows", "cols"), None),
            P(("groups", "rows", "cols"), None),
            P(("groups", "rows", "cols"), None),
            P("groups"),
            P("groups", None),
        ),
        out_specs=(
            P(("groups", "rows", "cols"), None),
            P(("groups", "rows", "cols"), None),
            P("groups"),
        ),
        check_vma=False,
    )
```

profile of v0, /device:TPU:0, one launch (start us, length us, event | category | flops | bytes accessed | tf_op | source)
XLA Modules:
  0.0 53.7 jit_solution(5011625084991519385)
XLA Ops:
  0.6 0.9 %convert_element_type.114 = bf16[192,128]{1,0:T(8,128)(2,1)S(1)} convert(f32[192,128]{1,0:T(8,128)} %param.10) | non-fusion elementwise | flops 24576 | bytes 147456 | tf_op jit(solution)/shard_map/convert_element_type | solution.py:174
  1.6 0.8 %pad_maximum_fusion = (bf16[192,256]{1,0:T(8,128)(2,1)S(1)}, bf16[960,256]{1,0:T(8,128)(2,1)S(1)}) fusion(bf16[192,128]{1,0:T(8,128)(2,1)S(1)} %convert_element_type.114, bf16[192,128]{1,0:T(8,128)(2,1)} %param.9), kind=kLoop, calls=%fused_computation.129 | loop fusion | flops 196607 | bytes 294912 | tf_op jit(solution)/shard_map/concatenate | solution.py:175
  2.4 3.0 %collective-permute-start.3 = (bf16[192,256]{1,0:T(8,128)(2,1)S(1)}, bf16[192,256]{1,0:T(8,128)(2,1)S(1)}, u32[]{:S(2)}, u32[]{:S(2)}) collective-permute-start(bf16[192,256]{1,0:T(8,128)(2,1)S(1)} %get-tuple-element.37), channel_id=1, source_target_pairs={{0,2},{1,3},{2,0},{3,1},{4,6},{5,7},{6,4},{7,5},{8,10},{9,11},{10,... | collective-permute-start | bytes 294920 | tf_op jit(solution)/shard_map/ppermute | solution.py:123
  5.4 3.6 %collective-permute-start.2 = (bf16[192,256]{1,0:T(8,128)(2,1)S(1)}, bf16[192,256]{1,0:T(8,128)(2,1)S(1)}, u32[]{:S(2)}, u32[]{:S(2)}) collective-permute-start(bf16[192,256]{1,0:T(8,128)(2,1)S(1)} %get-tuple-element.37), channel_id=1, source_target_pairs={{0,12},{4,0},{8,4},{12,8},{1,13},{5,1},{9,5},{13,9},{2,14},{6,2},{... | collective-permute-start | bytes 294920 | tf_op jit(solution)/shard_map/ppermute | solution.py:111
  9.0 1.0 %collective-permute-start = (bf16[192,256]{1,0:T(8,128)(2,1)S(1)}, bf16[192,256]{1,0:T(8,128)(2,1)S(1)}, u32[]{:S(2)}, u32[]{:S(2)}) collective-permute-start(bf16[192,256]{1,0:T(8,128)(2,1)S(1)} %get-tuple-element.37), channel_id=1, source_target_pairs={{0,4},{4,8},{8,12},{12,0},{1,5},{5,9},{9,13},{13,1},{2,6},{6,10},{... | collective-permute-start | bytes 294920 | tf_op jit(solution)/shard_map/ppermute | solution.py:111
  10.0 0.9 %multiply_reduce_fusion.9 = f32[192]{0:T(256)S(1)} fusion(bf16[192,128]{1,0:T(8,128)(2,1)} %param.9), kind=kLoop, calls=%fused_computation.140 | loop fusion | flops 73536 | bytes 49920 | tf_op jit(solution)/shard_map/reduce_sum | solution.py:15
  10.9 0.9 %multiply_reduce_fusion.6 = f32[128]{0:T(128)S(1)} fusion(f32[192,128]{1,0:T(8,128)} %param.11), kind=kLoop, calls=%fused_computation.130 | loop fusion | flops 49024 | bytes 98816 | tf_op jit(solution)/shard_map/reduce_sum | solution.py:193
  11.9 0.7 %compare_and_fusion = (pred[1024]{0:T(1024)(128)(4,1)S(1)}, s32[1024]{0:T(1024)S(1)}) fusion(s32[]{:T(128)S(6)} %axis_index.25, s32[1024]{0:T(1024)} %param.12, s32[]{:T(128)S(6)} %axis_index.22), kind=kLoop, calls=%fused_computation.187 | loop fusion | flops 62464 | bytes 9224 | tf_op jit(solution)/shard_map/jit(_take)/and | solution.py:188
  12.6 1.2 %fusion.54 = f32[192,128]{1,0:T(8,128)S(1)} fusion(bf16[192,128]{1,0:T(8,128)(2,1)S(1)} %convert_element_type.114, bf16[192,128]{1,0:T(8,128)(2,1)} %param.9, f32[192]{0:T(256)S(1)} %multiply_reduce_fusion.9), kind=kOutput, calls=%fused_computation.64 | convolution fusion | flops 19058688 | bytes 197376 | tf_op jit(solution)/shard_map/dot_general | solution.py:39
  13.8 0.8 %constant_dynamic-update-slice_fusion.9 = bf16[3072,128]{1,0:T(8,128)(2,1)S(1)} fusion(bf16[192,128]{1,0:T(8,128)(2,1)} %param.9), kind=kLoop, calls=%fused_computation.154 | loop fusion | bytes 98304
  14.7 1.2 %collective-permute-done = bf16[192,256]{1,0:T(8,128)(2,1)S(1)} collective-permute-done((bf16[192,256]{1,0:T(8,128)(2,1)S(1)}, bf16[192,256]{1,0:T(8,128)(2,1)S(1)}, u32[]{:S(2)}, u32[]{:S(2)}) %collective-permute-start) | collective-permute-done | bytes 98336 | tf_op jit(solution)/shard_map/ppermute | solution.py:111
  15.9 1.4 %collective-permute-done.1 = bf16[192,256]{1,0:T(8,128)(2,1)S(1)} collective-permute-done((bf16[192,256]{1,0:T(8,128)(2,1)S(1)}, bf16[192,256]{1,0:T(8,128)(2,1)S(1)}, u32[]{:S(2)}, u32[]{:S(2)}) %collective-permute-start.1) | collective-permute-done | bytes 98336 | tf_op jit(solution)/shard_map/ppermute | solution.py:111
  17.4 0.6 %collective-permute-start.4 = (bf16[576,256]{1,0:T(8,128)(2,1)S(1)}, bf16[576,256]{1,0:T(8,128)(2,1)S(1)}, u32[]{:S(2)}, u32[]{:S(2)}) collective-permute-start(bf16[576,256]{1,0:T(8,128)(2,1)S(1)} %get-tuple-element.31), channel_id=1, source_target_pairs={{0,2},{1,3},{2,0},{3,1},{4,6},{5,7},{6,4},{7,5},{8,10},{9,11},{10,... | collective-permute-start | bytes 884744 | tf_op jit(solution)/shard_map/ppermute | solution.py:124
  18.0 0.2 multiply_reduce_fusion.5
  18.2 1.0 %fusion.49 = f32[192,192]{0,1:T(8,128)S(1)} fusion(bf16[192,128]{1,0:T(8,128)(2,1)} %param.9, bf16[192,256]{1,0:T(8,128)(2,1)S(1)} %collective-permute-done.3), kind=kOutput, calls=%fused_computation.58 | convolution fusion | flops 9474048 | bytes 245760 | tf_op jit(solution)/shard_map/dot_general | solution.py:19
  19.2 0.1 copy.8
  19.3 0.1 collective-permute-start.5
  19.5 0.1 multiply_reduce_fusion.8
  19.6 0.2 fusion.110
  19.8 6.0 %collective-permute-done.4 = bf16[576,256]{1,0:T(8,128)(2,1)S(1)} collective-permute-done((bf16[576,256]{1,0:T(8,128)(2,1)S(1)}, bf16[576,256]{1,0:T(8,128)(2,1)S(1)}, u32[]{:S(2)}, u32[]{:S(2)}) %collective-permute-start.4) | collective-permute-done | bytes 294944 | tf_op jit(solution)/shard_map/ppermute | solution.py:124
  25.8 0.2 multiply_reduce_fusion.4
  26.1 0.4 fusion.47
  26.6 0.2 multiply_reduce_fusion.2
  26.8 0.5 fusion.35
  27.3 0.4 fusion.61
  27.7 0.2 multiply_reduce_fusion.3
  27.9 0.4 multiply_reduce_fusion.7
  28.4 0.6 %collective-permute-start.9 = (bf16[208,128]{1,0:T(8,128)(2,1)S(1)}, bf16[208,128]{1,0:T(8,128)(2,1)S(1)}, u32[]{:S(2)}, u32[]{:S(2)}) collective-permute-start(bf16[208,128]{1,0:T(8,128)(2,1)S(1)} %get-tuple-element.40), channel_id=1, source_target_pairs={{0,12},{4,0},{8,4},{12,8},{1,13},{5,1},{9,5},{13,9},{2,14},{6,2},{... | collective-permute-start | bytes 159752 | tf_op jit(solution)/shard_map/ppermute | solution.py:111
  29.1 1.8 %collective-permute-start.8 = (bf16[208,128]{1,0:T(8,128)(2,1)S(1)}, bf16[208,128]{1,0:T(8,128)(2,1)S(1)}, u32[]{:S(2)}, u32[]{:S(2)}) collective-permute-start(bf16[208,128]{1,0:T(8,128)(2,1)S(1)} %get-tuple-element.40), channel_id=1, source_target_pairs={{0,8},{4,12},{8,0},{12,4},{1,9},{5,13},{9,1},{13,5},{2,10},{6,14},... | collective-permute-start | bytes 159752 | tf_op jit(solution)/shard_map/ppermute | solution.py:111
  30.8 1.9 %collective-permute-start.7 = (bf16[208,128]{1,0:T(8,128)(2,1)S(1)}, bf16[208,128]{1,0:T(8,128)(2,1)S(1)}, u32[]{:S(2)}, u32[]{:S(2)}) collective-permute-start(bf16[208,128]{1,0:T(8,128)(2,1)S(1)} %get-tuple-element.40), channel_id=1, source_target_pairs={{0,4},{4,8},{8,12},{12,0},{1,5},{5,9},{9,13},{13,1},{2,6},{6,10},{... | collective-permute-start | bytes 159752 | tf_op jit(solution)/shard_map/ppermute | solution.py:111
  32.8 0.5 %collective-permute-start.10 = (bf16[208,128]{1,0:T(8,128)(2,1)S(1)}, bf16[208,128]{1,0:T(8,128)(2,1)S(1)}, u32[]{:S(2)}, u32[]{:S(2)}) collective-permute-start(bf16[208,128]{1,0:T(8,128)(2,1)S(1)} %get-tuple-element.40), channel_id=1, source_target_pairs={{0,2},{1,3},{2,0},{3,1},{4,6},{5,7},{6,4},{7,5},{8,10},{9,11},{10,... | collective-permute-start | bytes 159752 | tf_op jit(solution)/shard_map/ppermute | solution.py:123
  33.3 0.5 multiply_reduce_fusion
  33.8 3.2 %gather_fusion = bf16[1024,128]{1,0:T(8,128)(2,1)S(1)} fusion(bf16[3072,128]{1,0:T(8,128)(2,1)S(1)} %slice_dynamic-update-slice_fusion.1, s32[1024]{0:T(1024)S(1)} %broadcast_clamp_fusion), kind=kCustom, calls=%fused_computation | custom fusion | bytes 528384 | tf_op jit(solution)/shard_map/jit(_take)/gather | solution.py:188
  37.0 0.4 multiply_reduce_fusion.1
  37.4 3.3 %exponential_convert_fusion = bf16[3072,1024]{1,0:T(8,128)(2,1)S(1)} fusion(bf16[3072,128]{1,0:T(8,128)(2,1)S(1)} %slice_dynamic-update-slice_fusion.1, f32[1024]{0:T(1024)S(1)} %multiply_reduce_fusion.1, f32[3072]{0:T(1024)S(1)} %multiply_reduce_fusion, bf16[1024,128]{1,0:T(8,128)(2,1)S(1)} %gather_fusion, pred[1024]{0:T(1024)(128)(4,1)S(1)} %get-tuple-element.27), kind=kOutput, calls=%fused_computation.1 | convolution fusion | flops 821166080 | bytes 7357440 | tf_op jit(solution)/shard_map/dot_general | solution.py:19
  40.8 0.4 fusion.74
  41.2 1.6 %collective-permute-start.11 = (bf16[624,128]{1,0:T(8,128)(2,1)S(1)}, bf16[624,128]{1,0:T(8,128)(2,1)S(1)}, u32[]{:S(2)}, u32[]{:S(2)}) collective-permute-start(bf16[624,128]{1,0:T(8,128)(2,1)S(1)} %get-tuple-element.41), channel_id=1, source_target_pairs={{0,2},{1,3},{2,0},{3,1},{4,6},{5,7},{6,4},{7,5},{8,10},{9,11},{10,... | collective-permute-start | bytes 479240 | tf_op jit(solution)/shard_map/ppermute | solution.py:124
  42.8 0.3 fusion.72
  43.3 3.4 %collective-permute-done.11 = bf16[624,128]{1,0:T(8,128)(2,1)S(1)} collective-permute-done((bf16[624,128]{1,0:T(8,128)(2,1)S(1)}, bf16[624,128]{1,0:T(8,128)(2,1)S(1)}, u32[]{:S(2)}, u32[]{:S(2)}) %collective-permute-start.11) | collective-permute-done | bytes 159776 | tf_op jit(solution)/shard_map/ppermute | solution.py:124
  46.8 0.6 %fusion.43 = f32[1024,128]{1,0:T(8,128)S(1)} fusion(bf16[576,128]{1,0:T(8,128)(2,1)S(1)} %bitcast.143, bf16[3072,1024]{1,0:T(8,128)(2,1)S(1)} %exponential_convert_fusion), kind=kOutput, calls=%fused_computation.51 | convolution fusion | flops 150994944 | bytes 1851392 | tf_op jit(solution)/shard_map/dot_general | solution.py:150
  47.4 0.8 %fusion.3 = f32[1024,128]{1,0:T(8,128)S(1)} fusion(bf16[960,128]{1,0:T(8,128)(2,1)S(1)} %bitcast.138, bf16[3072,1024]{1,0:T(8,128)(2,1)S(1)} %exponential_convert_fusion), kind=kOutput, calls=%fused_computation.6 | convolution fusion | flops 251658240 | bytes 2736128 | tf_op jit(solution)/shard_map/dot_general | solution.py:150
  48.2 0.6 %fusion.17 = f32[1024,128]{1,0:T(8,128)S(1)} fusion(f32[1024,128]{1,0:T(8,128)S(1)} %fusion.3, f32[1024,128]{1,0:T(8,128)S(1)} %fusion.43, f32[1024,128]{1,0:T(8,128)S(1)} %fusion.72, f32[1024,128]{1,0:T(8,128)S(1)} %fusion.74, bf16[576,128]{1,0:T(8,128)(2,1)S(1)} %bitcast.134, bf16[3072,1024]{1,0:T(8,128)(2,1)S(1)} %exponential_convert_fusion), kind=kOutput, calls=%fused_computation.25 | convolution fusion | flops 151519232 | bytes 3948544 | tf_op jit(solution)/shard_map/dot_general | solution.py:150
  48.8 0.5 sqrt_bitcast_fusion
  49.4 0.6 %convolution_add_fusion = f32[1024,128]{1,0:T(8,128)S(1)} fusion(f32[1024,128]{1,0:T(8,128)S(1)} %fusion.17, bf16[576,128]{1,0:T(8,128)(2,1)S(1)} %bitcast.135, bf16[3072,1024]{1,0:T(8,128)(2,1)S(1)} %exponential_convert_fusion), kind=kOutput, calls=%fused_computation.21 | convolution fusion | flops 151126016 | bytes 2375680 | tf_op jit(solution)/shard_map/dot_general | solution.py:150
  50.0 0.8 %fusion.65 = f32[128,1024]{1,0:T(8,128)S(1)} fusion(f32[1024,1024]{1,0:T(8,128)S(1)} %copy-done, f32[1024,128]{1,0:T(8,128)S(1)} %convolution_add_fusion), kind=kOutput, calls=%fused_computation.75 | convolution fusion | flops 270794752 | bytes 5242880 | tf_op jit(solution)/shard_map/dot_general | solution.py:211
  50.8 0.8 %fusion.21 = f32[1024,128]{0,1:T(8,128)S(1)} fusion(f32[128,1024]{1,0:T(8,128)S(1)} %fusion.65, f32[1024,1024]{1,0:T(8,128)S(1)} %copy-done, f32[1024,128]{1,0:T(8,128)S(1)} %convolution_add_fusion), kind=kOutput, calls=%fused_computation.28 | convolution fusion | flops 271056896 | bytes 5767168 | tf_op jit(solution)/shard_map/dot_general | solution.py:212
  51.6 0.8 %fusion.36 = bf16[1024,128]{0,1:T(8,128)(2,1)S(1)} fusion(f32[1024,128]{0,1:T(8,128)S(1)} %fusion.21, f32[1024,1024]{1,0:T(8,128)S(1)} %copy-done, f32[1024,128]{1,0:T(8,128)S(1)} %convolution_add_fusion), kind=kOutput, calls=%fused_computation.46 | convolution fusion | flops 272105472 | bytes 5505024 | tf_op jit(solution)/shard_map/dot_general | solution.py:213
  52.5 1.2 %fusion.64 = f32[192,128]{1,0:T(8,128)} fusion(f32[192,128]{1,0:T(8,128)S(1)} %copy-done.3, f32[192,128]{1,0:T(8,128)S(1)} %get-tuple-element.48, bf16[1024,128]{0,1:T(8,128)(2,1)S(1)} %fusion.36, bf16[192,128]{1,0:T(8,128)(2,1)S(1)} %copy-done.1, f32[1024]{0:T(1024)S(1)} %multiply_reduce_fusion.1, f32[192]{0:T(256)S(1)} %multiply_reduce_fusion.9, ...), kind=kOutput, calls=%fused_computation.74 | convolution fusion | flops 101851136 | bytes 874240 | tf_op jit(solution)/shard_map/dot_general | solution.py:215
  (53 shorter events, 0.7 us)
Async XLA Ops:
  0.6 25.5 %copy-start.1 = (bf16[192,128]{1,0:T(8,128)(2,1)S(1)}, bf16[192,128]{1,0:T(8,128)(2,1)}, u32[]{:S(2)}) copy-start(bf16[192,128]{1,0:T(8,128)(2,1)} %param.9) | copy-start | bytes 147460
  2.4 15.8 %collective-permute-start.3 = (bf16[192,256]{1,0:T(8,128)(2,1)S(1)}, bf16[192,256]{1,0:T(8,128)(2,1)S(1)}, u32[]{:S(2)}, u32[]{:S(2)}) collective-permute-start(bf16[192,256]{1,0:T(8,128)(2,1)S(1)} %get-tuple-element.37), channel_id=1, source_target_pairs={{0,2},{1,3},{2,0},{3,1},{4,6},{5,7},{6,4},{7,5},{8,10},{9,11},{10,... | collective-permute-start | bytes 294920 | tf_op jit(solution)/shard_map/ppermute | solution.py:123
  5.4 12.0 %collective-permute-start.2 = (bf16[192,256]{1,0:T(8,128)(2,1)S(1)}, bf16[192,256]{1,0:T(8,128)(2,1)S(1)}, u32[]{:S(2)}, u32[]{:S(2)}) collective-permute-start(bf16[192,256]{1,0:T(8,128)(2,1)S(1)} %get-tuple-element.37), channel_id=1, source_target_pairs={{0,12},{4,0},{8,4},{12,8},{1,13},{5,1},{9,5},{13,9},{2,14},{6,2},{... | collective-permute-start | bytes 294920 | tf_op jit(solution)/shard_map/ppermute | solution.py:111
  9.0 8.3 %collective-permute-start.1 = (bf16[192,256]{1,0:T(8,128)(2,1)S(1)}, bf16[192,256]{1,0:T(8,128)(2,1)S(1)}, u32[]{:S(2)}, u32[]{:S(2)}) collective-permute-start(bf16[192,256]{1,0:T(8,128)(2,1)S(1)} %get-tuple-element.37), channel_id=1, source_target_pairs={{0,8},{4,12},{8,0},{12,4},{1,9},{5,13},{9,1},{13,5},{2,10},{6,14},... | collective-permute-start | bytes 294920 | tf_op jit(solution)/shard_map/ppermute | solution.py:111
  9.0 6.9 %collective-permute-start = (bf16[192,256]{1,0:T(8,128)(2,1)S(1)}, bf16[192,256]{1,0:T(8,128)(2,1)S(1)}, u32[]{:S(2)}, u32[]{:S(2)}) collective-permute-start(bf16[192,256]{1,0:T(8,128)(2,1)S(1)} %get-tuple-element.37), channel_id=1, source_target_pairs={{0,4},{4,8},{8,12},{12,0},{1,5},{5,9},{9,13},{13,1},{2,6},{6,10},{... | collective-permute-start | bytes 294920 | tf_op jit(solution)/shard_map/ppermute | solution.py:111
  12.6 15.3 %copy-start.2 = (f32[192,128]{1,0:T(8,128)S(1)}, f32[192,128]{1,0:T(8,128)}, u32[]{:S(2)}) copy-start(f32[192,128]{1,0:T(8,128)} %param.11) | copy-start | bytes 294916
  12.6 15.3 %copy-start.3 = (f32[192,128]{1,0:T(8,128)S(1)}, f32[192,128]{1,0:T(8,128)}, u32[]{:S(2)}) copy-start(f32[192,128]{1,0:T(8,128)} %param.10) | copy-start | bytes 294916
  17.4 8.4 %collective-permute-start.4 = (bf16[576,256]{1,0:T(8,128)(2,1)S(1)}, bf16[576,256]{1,0:T(8,128)(2,1)S(1)}, u32[]{:S(2)}, u32[]{:S(2)}) collective-permute-start(bf16[576,256]{1,0:T(8,128)(2,1)S(1)} %get-tuple-element.31), channel_id=1, source_target_pairs={{0,2},{1,3},{2,0},{3,1},{4,6},{5,7},{6,4},{7,5},{8,10},{9,11},{10,... | collective-permute-start | bytes 884744 | tf_op jit(solution)/shard_map/ppermute | solution.py:124
  19.3 7.2 %collective-permute-start.5 = (bf16[960,256]{1,0:T(8,128)(2,1)S(1)}, bf16[960,256]{1,0:T(8,128)(2,1)S(1)}, u32[]{:S(2)}, u32[]{:S(2)}) collective-permute-start(bf16[960,256]{1,0:T(8,128)(2,1)S(1)} %constant_dynamic-update-slice_fusion.3), channel_id=1, source_target_pairs={{0,1},{1,0},{2,3},{3,2},{4,5},{5,4},{6,7},{7,6},{8,9},{9,8},{10,11... | collective-permute-start | bytes 1474568 | tf_op jit(solution)/shard_map/ppermute | solution.py:123
  26.0 1.7 %collective-permute-start.6 = (bf16[576,256]{1,0:T(8,128)(2,1)S(1)}, bf16[576,256]{1,0:T(8,128)(2,1)S(1)}, u32[]{:S(2)}, u32[]{:S(2)}) collective-permute-start(bf16[576,256]{1,0:T(8,128)(2,1)S(1)} %collective-permute-done.4), channel_id=1, source_target_pairs={{0,1},{1,0},{2,3},{3,2},{4,5},{5,4},{6,7},{7,6},{8,9},{9,8},{10,11... | collective-permute-start | bytes 884744 | tf_op jit(solution)/shard_map/ppermute | solution.py:124
  28.3 24.1 %copy-start.4 = (f32[192,128]{1,0:T(8,128)}, f32[192,128]{1,0:T(8,128)S(1)}, u32[]{:S(2)}) copy-start(f32[192,128]{1,0:T(8,128)S(1)} %get-tuple-element.48) | copy-start | bytes 294916
  28.4 12.8 %collective-permute-start.9 = (bf16[208,128]{1,0:T(8,128)(2,1)S(1)}, bf16[208,128]{1,0:T(8,128)(2,1)S(1)}, u32[]{:S(2)}, u32[]{:S(2)}) collective-permute-start(bf16[208,128]{1,0:T(8,128)(2,1)S(1)} %get-tuple-element.40), channel_id=1, source_target_pairs={{0,12},{4,0},{8,4},{12,8},{1,13},{5,1},{9,5},{13,9},{2,14},{6,2},{... | collective-permute-start | bytes 159752 | tf_op jit(solution)/shard_map/ppermute | solution.py:111
  29.1 12.1 %collective-permute-start.8 = (bf16[208,128]{1,0:T(8,128)(2,1)S(1)}, bf16[208,128]{1,0:T(8,128)(2,1)S(1)}, u32[]{:S(2)}, u32[]{:S(2)}) collective-permute-start(bf16[208,128]{1,0:T(8,128)(2,1)S(1)} %get-tuple-element.40), channel_id=1, source_target_pairs={{0,8},{4,12},{8,0},{12,4},{1,9},{5,13},{9,1},{13,5},{2,10},{6,14},... | collective-permute-start | bytes 159752 | tf_op jit(solution)/shard_map/ppermute | solution.py:111
  30.8 10.3 %collective-permute-start.7 = (bf16[208,128]{1,0:T(8,128)(2,1)S(1)}, bf16[208,128]{1,0:T(8,128)(2,1)S(1)}, u32[]{:S(2)}, u32[]{:S(2)}) collective-permute-start(bf16[208,128]{1,0:T(8,128)(2,1)S(1)} %get-tuple-element.40), channel_id=1, source_target_pairs={{0,4},{4,8},{8,12},{12,0},{1,5},{5,9},{9,13},{13,1},{2,6},{6,10},{... | collective-permute-start | bytes 159752 | tf_op jit(solution)/shard_map/ppermute | solution.py:111
  32.8 10.0 %collective-permute-start.10 = (bf16[208,128]{1,0:T(8,128)(2,1)S(1)}, bf16[208,128]{1,0:T(8,128)(2,1)S(1)}, u32[]{:S(2)}, u32[]{:S(2)}) collective-permute-start(bf16[208,128]{1,0:T(8,128)(2,1)S(1)} %get-tuple-element.40), channel_id=1, source_target_pairs={{0,2},{1,3},{2,0},{3,1},{4,6},{5,7},{6,4},{7,5},{8,10},{9,11},{10,... | collective-permute-start | bytes 159752 | tf_op jit(solution)/shard_map/ppermute | solution.py:123
  41.2 5.4 %collective-permute-start.11 = (bf16[624,128]{1,0:T(8,128)(2,1)S(1)}, bf16[624,128]{1,0:T(8,128)(2,1)S(1)}, u32[]{:S(2)}, u32[]{:S(2)}) collective-permute-start(bf16[624,128]{1,0:T(8,128)(2,1)S(1)} %get-tuple-element.41), channel_id=1, source_target_pairs={{0,2},{1,3},{2,0},{3,1},{4,6},{5,7},{6,4},{7,5},{8,10},{9,11},{10,... | collective-permute-start | bytes 479240 | tf_op jit(solution)/shard_map/ppermute | solution.py:124
  43.2 4.2 %collective-permute-start.12 = (bf16[1040,128]{1,0:T(8,128)(2,1)S(1)}, bf16[1040,128]{1,0:T(8,128)(2,1)S(1)}, u32[]{:S(2)}, u32[]{:S(2)}) collective-permute-start(bf16[1040,128]{1,0:T(8,128)(2,1)S(1)} %constant_dynamic-update-slice_fusion.13), channel_id=1, source_target_pairs={{0,1},{1,0},{2,3},{3,2},{4,5},{5,4},{6,7},{7,6},{8,9},{9,8},{10,11... | collective-permute-start | bytes 798728 | tf_op jit(solution)/shard_map/ppermute | solution.py:123
  46.7 2.1 %collective-permute-start.13 = (bf16[624,128]{1,0:T(8,128)(2,1)S(1)}, bf16[624,128]{1,0:T(8,128)(2,1)S(1)}, u32[]{:S(2)}, u32[]{:S(2)}) collective-permute-start(bf16[624,128]{1,0:T(8,128)(2,1)S(1)} %collective-permute-done.11), channel_id=1, source_target_pairs={{0,1},{1,0},{2,3},{3,2},{4,5},{5,4},{6,7},{7,6},{8,9},{9,8},{10,11... | collective-permute-start | bytes 479240 | tf_op jit(solution)/shard_map/ppermute | solution.py:124
  47.4 2.6 %copy-start = (f32[1024,1024]{1,0:T(8,128)S(1)}, f32[1024,1024]{1,0:T(8,128)}, u32[]{:S(2)}) copy-start(f32[1024,1024]{1,0:T(8,128)} %param.13) | copy-start | bytes 12582916
where the time goes:
time: 54.1 us; the launch traced here: 53.7 us
  starting transfers between devices  15 us (28%)
  matrix products  14.4 us (27%)
  waiting for transfers between devices  12.2 us (23%)
  other arithmetic  6.64 us (12%)
  local copies, waits for them, and re-layouts  4.46 us (8%)
  between operations  1.11 us (2%)
    ppermute x4, waiting for transfers between devices, pipelined_xor_gather(): newest = lax.ppermute(parts[-1], axis, perm)  9.45 us
    ppermute x6, starting transfers between devices, gather_blocks(): lax.ppermute(block, 'rows', [(i, (i + k) % n_rows) for i in range(n_rows)])  8.95 us
    dot_general x2, matrix products, rbf_tile(): lax.dot_general(left_x, right_x, (((1,), (1,)), ((), ())), preferred_elem...  4.34 us
    ppermute x4, starting transfers between devices, pipelined_xor_gather(): held = lax.ppermute(jnp.concatenate(parts[:-1], axis=0), axis, perm)  3.72 us
    gather x1, local copies, waits for them, and re-layouts, local(): centers = jnp.take(all_x, position, axis=0)  3.21 us
    dot_general x6, matrix products, projected_all(): lax.dot_general(piece, r, contract, preferred_element_type=jnp.float32)  3.17 us
    dot_general x6, matrix products, piece(): return jnp.dot(k, v, preferred_element_type=jnp.float32)  3.15 us
    ppermute x6, waiting for transfers between devices, gather_blocks(): lax.ppermute(block, 'rows', [(i, (i + k) % n_rows) for i in range(n_rows)])  2.69 us
  transfers between devices with their start and end apart: 14, of which 4 were waited for; matrix products, arithmetic and copies ran while one was open for 34% of the time, Pallas kernels for 0%

commit v1 on v0

--- a/solution.py
+++ b/solution.py
@@ -185,7 +185,10 @@
     all_sq = square_norms(all_x)
     owner = inducing // n_local
     position = relative_order(owner) * n_local + inducing % n_local
-    centers = jnp.take(all_x, position, axis=0)
+    selector = (position[:, None] == jnp.arange(all_x.shape[0], dtype=position.dtype)[None, :]).astype(
+        jnp.bfloat16
+    )
+    centers = jnp.dot(selector, all_x, preferred_element_type=jnp.float32).astype(jnp.bfloat16)
     centers_sq = square_norms(centers)
     cross = rbf_tile(points, own_sq, centers, centers_sq, gamma)
     residual_b = residual.astype(jnp.bfloat16)

time: 54.1 us -> 52.9 us (0.978)
  local copies, waits for them, and re-layouts: 4.46 us -> 1.25 us
  matrix products: 14.4 us -> 16.7 us
    gather x1 -> x0, local copies, waits for them, and re-layouts: 3.21 us -> none  [local(): centers = jnp.take(all_x, position, axis=0)]
    dot_general x0 -> x1, matrix products: none -> 2.67 us  [local(): jnp.dot(selector, all_x, preferred_element_type=jnp.float32)]
    add x0 -> x1, other arithmetic: none -> 0.72 us  [local(): position = relative_order(owner) * n_local + inducing % n_local]
    and x1 -> x0, other arithmetic: 0.72 us -> none  [local(): centers = jnp.take(all_x, position, axis=0)]
    reduce_sum x8 -> x7, other arithmetic: 2.59 us -> 2.23 us  [square_norms(): return jnp.sum(jnp.square(values.astype(jnp.float32)), axis=1)]
  transfers between devices with their start and end apart: 14 -> 14, of which waited for: 4 -> 4; matrix products, arithmetic and copies ran while one was open for 34% -> 32% of each run, Pallas kernels for 0% -> 0%
where the time goes in v1:
time: 52.9 us; the launch traced here: 52.5 us
  matrix products  16.7 us (32%)
  starting transfers between devices  15 us (28%)
  waiting for transfers between devices  12.2 us (23%)
  other arithmetic  6.27 us (12%)
  local copies, waits for them, and re-layouts  1.25 us (2%)
  between operations  1.1 us (2%)
    ppermute x4, waiting for transfers between devices, pipelined_xor_gather(): newest = lax.ppermute(parts[-1], axis, perm)  9.45 us
    ppermute x6, starting transfers between devices, gather_blocks(): lax.ppermute(block, 'rows', [(i, (i + k) % n_rows) for i in range(n_rows)])  8.95 us
    dot_general x2, matrix products, rbf_tile(): lax.dot_general(left_x, right_x, (((1,), (1,)), ((), ())), preferred_elem...  4.08 us
    ppermute x4, starting transfers between devices, pipelined_xor_gather(): held = lax.ppermute(jnp.concatenate(parts[:-1], axis=0), axis, perm)  3.71 us
    dot_general x6, matrix products, projected_all(): lax.dot_general(piece, r, contract, preferred_element_type=jnp.float32)  3.18 us
    dot_general x6, matrix products, piece(): return jnp.dot(k, v, preferred_element_type=jnp.float32)  3.15 us
    ppermute x6, waiting for transfers between devices, gather_blocks(): lax.ppermute(block, 'rows', [(i, (i + k) % n_rows) for i in range(n_rows)])  2.72 us
    dot_general x1, matrix products, local(): jnp.dot(selector, all_x, preferred_element_type=jnp.float32)  2.67 us
  transfers between devices with their start and end apart: 14, of which 4 were waited for; matrix products, arithmetic and copies ran while one was open for 32% of the time, Pallas kernels for 0%

profile of v1, /device:TPU:0, one launch (start us, length us, event | category | flops | bytes accessed | tf_op | source)
XLA Modules:
  0.0 52.5 jit_solution(6152934858614170370)
XLA Ops:
  0.6 0.9 %convert_element_type.118 = bf16[192,128]{1,0:T(8,128)(2,1)S(1)} convert(f32[192,128]{1,0:T(8,128)} %param.10) | non-fusion elementwise | flops 24576 | bytes 147456 | tf_op jit(solution)/shard_map/convert_element_type | solution.py:174
  1.6 0.8 %pad_maximum_fusion = (bf16[192,256]{1,0:T(8,128)(2,1)S(1)}, bf16[960,256]{1,0:T(8,128)(2,1)S(1)}) fusion(bf16[192,128]{1,0:T(8,128)(2,1)S(1)} %convert_element_type.118, bf16[192,128]{1,0:T(8,128)(2,1)} %param.9), kind=kLoop, calls=%fused_computation.131 | loop fusion | flops 196607 | bytes 294912 | tf_op jit(solution)/shard_map/concatenate | solution.py:175
  2.4 3.0 %collective-permute-start.3 = (bf16[192,256]{1,0:T(8,128)(2,1)S(1)}, bf16[192,256]{1,0:T(8,128)(2,1)S(1)}, u32[]{:S(2)}, u32[]{:S(2)}) collective-permute-start(bf16[192,256]{1,0:T(8,128)(2,1)S(1)} %get-tuple-element.35), channel_id=1, source_target_pairs={{0,2},{1,3},{2,0},{3,1},{4,6},{5,7},{6,4},{7,5},{8,10},{9,11},{10,... | collective-permute-start | bytes 294920 | tf_op jit(solution)/shard_map/ppermute | solution.py:123
  5.4 3.6 %collective-permute-start.2 = (bf16[192,256]{1,0:T(8,128)(2,1)S(1)}, bf16[192,256]{1,0:T(8,128)(2,1)S(1)}, u32[]{:S(2)}, u32[]{:S(2)}) collective-permute-start(bf16[192,256]{1,0:T(8,128)(2,1)S(1)} %get-tuple-element.35), channel_id=1, source_target_pairs={{0,12},{4,0},{8,4},{12,8},{1,13},{5,1},{9,5},{13,9},{2,14},{6,2},{... | collective-permute-start | bytes 294920 | tf_op jit(solution)/shard_map/ppermute | solution.py:111
  9.0 1.0 %collective-permute-start = (bf16[192,256]{1,0:T(8,128)(2,1)S(1)}, bf16[192,256]{1,0:T(8,128)(2,1)S(1)}, u32[]{:S(2)}, u32[]{:S(2)}) collective-permute-start(bf16[192,256]{1,0:T(8,128)(2,1)S(1)} %get-tuple-element.35), channel_id=1, source_target_pairs={{0,4},{4,8},{8,12},{12,0},{1,5},{5,9},{9,13},{13,1},{2,6},{6,10},{... | collective-permute-start | bytes 294920 | tf_op jit(solution)/shard_map/ppermute | solution.py:111
  10.0 0.9 %multiply_reduce_fusion.9 = f32[192]{0:T(256)S(1)} fusion(bf16[192,128]{1,0:T(8,128)(2,1)} %param.9), kind=kLoop, calls=%fused_computation.142 | loop fusion | flops 73536 | bytes 49920 | tf_op jit(solution)/shard_map/reduce_sum | solution.py:15
  10.9 0.9 %multiply_reduce_fusion.6 = f32[128]{0:T(128)S(1)} fusion(f32[192,128]{1,0:T(8,128)} %param.11), kind=kLoop, calls=%fused_computation.132 | loop fusion | flops 49024 | bytes 98816 | tf_op jit(solution)/shard_map/reduce_sum | solution.py:196
  11.9 1.2 %fusion.57 = f32[192,128]{1,0:T(8,128)S(1)} fusion(bf16[192,128]{1,0:T(8,128)(2,1)S(1)} %convert_element_type.118, bf16[192,128]{1,0:T(8,128)(2,1)} %param.9, f32[192]{0:T(256)S(1)} %multiply_reduce_fusion.9), kind=kOutput, calls=%fused_computation.67 | convolution fusion | flops 19058688 | bytes 197376 | tf_op jit(solution)/shard_map/dot_general | solution.py:39
  13.1 0.7 %fusion.128 = s32[1024]{0:T(1024)S(1)} fusion(s32[1024]{0:T(1024)} %param.12, s32[]{:T(128)S(6)} %axis_index.25, s32[]{:T(128)S(6)} %axis_index.22), kind=kLoop, calls=%fused_computation.183 | loop fusion | flops 56320 | bytes 8200 | tf_op jit(solution)/shard_map/add | solution.py:187
  13.8 0.8 %constant_dynamic-update-slice_fusion.9 = bf16[3072,128]{1,0:T(8,128)(2,1)S(1)} fusion(bf16[192,128]{1,0:T(8,128)(2,1)} %param.9), kind=kLoop, calls=%fused_computation.156 | loop fusion | bytes 98304
  14.6 1.3 %collective-permute-done = bf16[192,256]{1,0:T(8,128)(2,1)S(1)} collective-permute-done((bf16[192,256]{1,0:T(8,128)(2,1)S(1)}, bf16[192,256]{1,0:T(8,128)(2,1)S(1)}, u32[]{:S(2)}, u32[]{:S(2)}) %collective-permute-start) | collective-permute-done | bytes 98336 | tf_op jit(solution)/shard_map/ppermute | solution.py:111
  15.9 1.4 %collective-permute-done.1 = bf16[192,256]{1,0:T(8,128)(2,1)S(1)} collective-permute-done((bf16[192,256]{1,0:T(8,128)(2,1)S(1)}, bf16[192,256]{1,0:T(8,128)(2,1)S(1)}, u32[]{:S(2)}, u32[]{:S(2)}) %collective-permute-start.1) | collective-permute-done | bytes 98336 | tf_op jit(solution)/shard_map/ppermute | solution.py:111
  17.4 0.6 %collective-permute-start.4 = (bf16[576,256]{1,0:T(8,128)(2,1)S(1)}, bf16[576,256]{1,0:T(8,128)(2,1)S(1)}, u32[]{:S(2)}, u32[]{:S(2)}) collective-permute-start(bf16[576,256]{1,0:T(8,128)(2,1)S(1)} %get-tuple-element.29), channel_id=1, source_target_pairs={{0,2},{1,3},{2,0},{3,1},{4,6},{5,7},{6,4},{7,5},{8,10},{9,11},{10,... | collective-permute-start | bytes 884744 | tf_op jit(solution)/shard_map/ppermute | solution.py:124
  18.0 0.2 multiply_reduce_fusion.5
  18.2 1.0 %fusion.52 = f32[192,192]{0,1:T(8,128)S(1)} fusion(bf16[192,128]{1,0:T(8,128)(2,1)} %param.9, bf16[192,256]{1,0:T(8,128)(2,1)S(1)} %collective-permute-done.3), kind=kOutput, calls=%fused_computation.61 | convolution fusion | flops 9474048 | bytes 245760 | tf_op jit(solution)/shard_map/dot_general | solution.py:19
  19.2 0.1 copy.8
  19.3 0.1 collective-permute-start.5
  19.5 0.1 multiply_reduce_fusion.8
  19.6 0.2 fusion.113
  19.8 6.0 %collective-permute-done.4 = bf16[576,256]{1,0:T(8,128)(2,1)S(1)} collective-permute-done((bf16[576,256]{1,0:T(8,128)(2,1)S(1)}, bf16[576,256]{1,0:T(8,128)(2,1)S(1)}, u32[]{:S(2)}, u32[]{:S(2)}) %collective-permute-start.4) | collective-permute-done | bytes 294944 | tf_op jit(solution)/shard_map/ppermute | solution.py:124
  25.8 0.2 multiply_reduce_fusion.4
  26.1 0.4 fusion.50
  26.6 0.2 multiply_reduce_fusion.2
  26.8 0.5 fusion.37
  27.3 0.4 fusion.64
  27.7 0.2 multiply_reduce_fusion.3
  27.9 0.4 multiply_reduce_fusion.7
  28.4 0.6 %collective-permute-start.9 = (bf16[208,128]{1,0:T(8,128)(2,1)S(1)}, bf16[208,128]{1,0:T(8,128)(2,1)S(1)}, u32[]{:S(2)}, u32[]{:S(2)}) collective-permute-start(bf16[208,128]{1,0:T(8,128)(2,1)S(1)} %get-tuple-element.38), channel_id=1, source_target_pairs={{0,12},{4,0},{8,4},{12,8},{1,13},{5,1},{9,5},{13,9},{2,14},{6,2},{... | collective-permute-start | bytes 159752 | tf_op jit(solution)/shard_map/ppermute | solution.py:111
  29.1 1.8 %collective-permute-start.8 = (bf16[208,128]{1,0:T(8,128)(2,1)S(1)}, bf16[208,128]{1,0:T(8,128)(2,1)S(1)}, u32[]{:S(2)}, u32[]{:S(2)}) collective-permute-start(bf16[208,128]{1,0:T(8,128)(2,1)S(1)} %get-tuple-element.38), channel_id=1, source_target_pairs={{0,8},{4,12},{8,0},{12,4},{1,9},{5,13},{9,1},{13,5},{2,10},{6,14},... | collective-permute-start | bytes 159752 | tf_op jit(solution)/shard_map/ppermute | solution.py:111
  30.8 1.9 %collective-permute-start.7 = (bf16[208,128]{1,0:T(8,128)(2,1)S(1)}, bf16[208,128]{1,0:T(8,128)(2,1)S(1)}, u32[]{:S(2)}, u32[]{:S(2)}) collective-permute-start(bf16[208,128]{1,0:T(8,128)(2,1)S(1)} %get-tuple-element.38), channel_id=1, source_target_pairs={{0,4},{4,8},{8,12},{12,0},{1,5},{5,9},{9,13},{13,1},{2,6},{6,10},{... | collective-permute-start | bytes 159752 | tf_op jit(solution)/shard_map/ppermute | solution.py:111
  32.8 0.5 %collective-permute-start.10 = (bf16[208,128]{1,0:T(8,128)(2,1)S(1)}, bf16[208,128]{1,0:T(8,128)(2,1)S(1)}, u32[]{:S(2)}, u32[]{:S(2)}) collective-permute-start(bf16[208,128]{1,0:T(8,128)(2,1)S(1)} %get-tuple-element.38), channel_id=1, source_target_pairs={{0,2},{1,3},{2,0},{3,1},{4,6},{5,7},{6,4},{7,5},{8,10},{9,11},{10,... | collective-permute-start | bytes 159752 | tf_op jit(solution)/shard_map/ppermute | solution.py:123
  33.3 0.5 multiply_reduce_fusion
  33.8 2.7 %multiply_reduce_fusion.1 = (f32[1024]{0:T(1024)S(1)}, bf16[1024,128]{0,1:T(8,128)(2,1)S(1)}) fusion(bf16[3072,128]{1,0:T(8,128)(2,1)S(1)} %slice_dynamic-update-slice_fusion.1, s32[1024]{0:T(1024)S(1)} %fusion.128), kind=kOutput, calls=%fused_computation.84 | convolution fusion | flops 808975360 | bytes 1056768 | tf_op jit(solution)/shard_map/dot_general | solution.py:191
  36.5 3.1 %exponential_convert_fusion = bf16[3072,1024]{1,0:T(8,128)(2,1)S(1)} fusion(bf16[3072,128]{1,0:T(8,128)(2,1)S(1)} %slice_dynamic-update-slice_fusion.1, bf16[1024,128]{0,1:T(8,128)(2,1)S(1)} %get-tuple-element.48, f32[1024]{0:T(1024)S(1)} %get-tuple-element.47, f32[3072]{0:T(1024)S(1)} %multiply_reduce_fusion), kind=kOutput, calls=%fused_computation | convolution fusion | flops 821035008 | bytes 7356416 | tf_op jit(solution)/shard_map/dot_general | solution.py:19
  39.6 0.4 fusion.77
  40.1 1.6 %collective-permute-start.11 = (bf16[624,128]{1,0:T(8,128)(2,1)S(1)}, bf16[624,128]{1,0:T(8,128)(2,1)S(1)}, u32[]{:S(2)}, u32[]{:S(2)}) collective-permute-start(bf16[624,128]{1,0:T(8,128)(2,1)S(1)} %get-tuple-element.39), channel_id=1, source_target_pairs={{0,2},{1,3},{2,0},{3,1},{4,6},{5,7},{6,4},{7,5},{8,10},{9,11},{10,... | collective-permute-start | bytes 479240 | tf_op jit(solution)/shard_map/ppermute | solution.py:124
  41.6 0.3 fusion.75
  42.0 0.1 collective-permute-start.12
  42.1 3.4 %collective-permute-done.11 = bf16[624,128]{1,0:T(8,128)(2,1)S(1)} collective-permute-done((bf16[624,128]{1,0:T(8,128)(2,1)S(1)}, bf16[624,128]{1,0:T(8,128)(2,1)S(1)}, u32[]{:S(2)}, u32[]{:S(2)}) %collective-permute-start.11) | collective-permute-done | bytes 159776 | tf_op jit(solution)/shard_map/ppermute | solution.py:124
  45.6 0.6 %fusion.46 = f32[1024,128]{1,0:T(8,128)S(1)} fusion(bf16[576,128]{1,0:T(8,128)(2,1)S(1)} %bitcast.146, bf16[3072,1024]{1,0:T(8,128)(2,1)S(1)} %exponential_convert_fusion), kind=kOutput, calls=%fused_computation.54 | convolution fusion | flops 150994944 | bytes 1851392 | tf_op jit(solution)/shard_map/dot_general | solution.py:150
  46.3 0.8 %fusion.5 = f32[1024,128]{1,0:T(8,128)S(1)} fusion(bf16[960,128]{1,0:T(8,128)(2,1)S(1)} %bitcast.141, bf16[3072,1024]{1,0:T(8,128)(2,1)S(1)} %exponential_convert_fusion), kind=kOutput, calls=%fused_computation.8 | convolution fusion | flops 251658240 | bytes 2736128 | tf_op jit(solution)/shard_map/dot_general | solution.py:150
  47.0 0.6 %fusion.19 = f32[1024,128]{1,0:T(8,128)S(1)} fusion(f32[1024,128]{1,0:T(8,128)S(1)} %fusion.5, f32[1024,128]{1,0:T(8,128)S(1)} %fusion.46, f32[1024,128]{1,0:T(8,128)S(1)} %fusion.75, f32[1024,128]{1,0:T(8,128)S(1)} %fusion.77, bf16[576,128]{1,0:T(8,128)(2,1)S(1)} %bitcast.137, bf16[3072,1024]{1,0:T(8,128)(2,1)S(1)} %exponential_convert_fusion), kind=kOutput, calls=%fused_computation.27 | convolution fusion | flops 151519232 | bytes 3948544 | tf_op jit(solution)/shard_map/dot_general | solution.py:150
  47.7 0.5 %sqrt_bitcast_fusion = f32[128]{0:T(128)} fusion(f32[2,128]{1,0:T(2,128)S(1)} %fusion.135), kind=kLoop, calls=%fused_computation.202 | loop fusion | flops 256 | bytes 1536 | tf_op jit(solution)/shard_map/sqrt | solution.py:220
  48.2 0.6 %convolution_add_fusion = f32[1024,128]{1,0:T(8,128)S(1)} fusion(f32[1024,128]{1,0:T(8,128)S(1)} %fusion.19, bf16[576,128]{1,0:T(8,128)(2,1)S(1)} %bitcast.138, bf16[3072,1024]{1,0:T(8,128)(2,1)S(1)} %exponential_convert_fusion), kind=kOutput, calls=%fused_computation.23 | convolution fusion | flops 151126016 | bytes 2375680 | tf_op jit(solution)/shard_map/dot_general | solution.py:150
  48.8 0.8 %fusion.68 = f32[128,1024]{1,0:T(8,128)S(1)} fusion(f32[1024,1024]{1,0:T(8,128)S(1)} %copy-done, f32[1024,128]{1,0:T(8,128)S(1)} %convolution_add_fusion), kind=kOutput, calls=%fused_computation.78 | convolution fusion | flops 270794752 | bytes 5242880 | tf_op jit(solution)/shard_map/dot_general | solution.py:214
  49.6 0.8 %fusion.23 = f32[1024,128]{0,1:T(8,128)S(1)} fusion(f32[128,1024]{1,0:T(8,128)S(1)} %fusion.68, f32[1024,1024]{1,0:T(8,128)S(1)} %copy-done, f32[1024,128]{1,0:T(8,128)S(1)} %convolution_add_fusion), kind=kOutput, calls=%fused_computation.30 | convolution fusion | flops 271056896 | bytes 5767168 | tf_op jit(solution)/shard_map/dot_general | solution.py:215
  50.5 0.8 %fusion.39 = bf16[1024,128]{0,1:T(8,128)(2,1)S(1)} fusion(f32[1024,128]{0,1:T(8,128)S(1)} %fusion.23, f32[1024,1024]{1,0:T(8,128)S(1)} %copy-done, f32[1024,128]{1,0:T(8,128)S(1)} %convolution_add_fusion), kind=kOutput, calls=%fused_computation.49 | convolution fusion | flops 272105472 | bytes 5505024 | tf_op jit(solution)/shard_map/dot_general | solution.py:216
  51.3 1.1 %fusion.67 = f32[192,128]{1,0:T(8,128)} fusion(f32[192,128]{1,0:T(8,128)S(1)} %copy-done.3, f32[192,128]{1,0:T(8,128)S(1)} %get-tuple-element.46, bf16[1024,128]{0,1:T(8,128)(2,1)S(1)} %fusion.39, bf16[192,128]{1,0:T(8,128)(2,1)S(1)} %copy-done.1, bf16[1024,128]{0,1:T(8,128)(2,1)S(1)} %get-tuple-element.48, f32[1024]{0:T(1024)S(1)} %get-tuple-element.47, ...), kind=kOutput, calls=%fused_computation.77 | convolution fusion | flops 101720064 | bytes 873216 | tf_op jit(solution)/shard_map/dot_general | solution.py:218
  (51 shorter events, 0.6 us)
Async XLA Ops:
  0.6 25.5 %copy-start.1 = (bf16[192,128]{1,0:T(8,128)(2,1)S(1)}, bf16[192,128]{1,0:T(8,128)(2,1)}, u32[]{:S(2)}) copy-start(bf16[192,128]{1,0:T(8,128)(2,1)} %param.9) | copy-start | bytes 147460
  2.4 15.8 %collective-permute-start.3 = (bf16[192,256]{1,0:T(8,128)(2,1)S(1)}, bf16[192,256]{1,0:T(8,128)(2,1)S(1)}, u32[]{:S(2)}, u32[]{:S(2)}) collective-permute-start(bf16[192,256]{1,0:T(8,128)(2,1)S(1)} %get-tuple-element.35), channel_id=1, source_target_pairs={{0,2},{1,3},{2,0},{3,1},{4,6},{5,7},{6,4},{7,5},{8,10},{9,11},{10,... | collective-permute-start | bytes 294920 | tf_op jit(solution)/shard_map/ppermute | solution.py:123
  5.4 12.0 %collective-permute-start.2 = (bf16[192,256]{1,0:T(8,128)(2,1)S(1)}, bf16[192,256]{1,0:T(8,128)(2,1)S(1)}, u32[]{:S(2)}, u32[]{:S(2)}) collective-permute-start(bf16[192,256]{1,0:T(8,128)(2,1)S(1)} %get-tuple-element.35), channel_id=1, source_target_pairs={{0,12},{4,0},{8,4},{12,8},{1,13},{5,1},{9,5},{13,9},{2,14},{6,2},{... | collective-permute-start | bytes 294920 | tf_op jit(solution)/shard_map/ppermute | solution.py:111
  9.0 8.3 %collective-permute-start.1 = (bf16[192,256]{1,0:T(8,128)(2,1)S(1)}, bf16[192,256]{1,0:T(8,128)(2,1)S(1)}, u32[]{:S(2)}, u32[]{:S(2)}) collective-permute-start(bf16[192,256]{1,0:T(8,128)(2,1)S(1)} %get-tuple-element.35), channel_id=1, source_target_pairs={{0,8},{4,12},{8,0},{12,4},{1,9},{5,13},{9,1},{13,5},{2,10},{6,14},... | collective-permute-start | bytes 294920 | tf_op jit(solution)/shard_map/ppermute | solution.py:111
  9.0 6.9 %collective-permute-start = (bf16[192,256]{1,0:T(8,128)(2,1)S(1)}, bf16[192,256]{1,0:T(8,128)(2,1)S(1)}, u32[]{:S(2)}, u32[]{:S(2)}) collective-permute-start(bf16[192,256]{1,0:T(8,128)(2,1)S(1)} %get-tuple-element.35), channel_id=1, source_target_pairs={{0,4},{4,8},{8,12},{12,0},{1,5},{5,9},{9,13},{13,1},{2,6},{6,10},{... | collective-permute-start | bytes 294920 | tf_op jit(solution)/shard_map/ppermute | solution.py:111
  11.9 16.0 %copy-start.2 = (f32[192,128]{1,0:T(8,128)S(1)}, f32[192,128]{1,0:T(8,128)}, u32[]{:S(2)}) copy-start(f32[192,128]{1,0:T(8,128)} %param.11) | copy-start | bytes 294916
  11.9 16.0 %copy-start.3 = (f32[192,128]{1,0:T(8,128)S(1)}, f32[192,128]{1,0:T(8,128)}, u32[]{:S(2)}) copy-start(f32[192,128]{1,0:T(8,128)} %param.10) | copy-start | bytes 294916
  17.4 8.4 %collective-permute-start.4 = (bf16[576,256]{1,0:T(8,128)(2,1)S(1)}, bf16[576,256]{1,0:T(8,128)(2,1)S(1)}, u32[]{:S(2)}, u32[]{:S(2)}) collective-permute-start(bf16[576,256]{1,0:T(8,128)(2,1)S(1)} %get-tuple-element.29), channel_id=1, source_target_pairs={{0,2},{1,3},{2,0},{3,1},{4,6},{5,7},{6,4},{7,5},{8,10},{9,11},{10,... | collective-permute-start | bytes 884744 | tf_op jit(solution)/shard_map/ppermute | solution.py:124
  19.3 7.2 %collective-permute-start.5 = (bf16[960,256]{1,0:T(8,128)(2,1)S(1)}, bf16[960,256]{1,0:T(8,128)(2,1)S(1)}, u32[]{:S(2)}, u32[]{:S(2)}) collective-permute-start(bf16[960,256]{1,0:T(8,128)(2,1)S(1)} %constant_dynamic-update-slice_fusion.3), channel_id=1, source_target_pairs={{0,1},{1,0},{2,3},{3,2},{4,5},{5,4},{6,7},{7,6},{8,9},{9,8},{10,11... | collective-permute-start | bytes 1474568 | tf_op jit(solution)/shard_map/ppermute | solution.py:123
  26.0 1.7 %collective-permute-start.6 = (bf16[576,256]{1,0:T(8,128)(2,1)S(1)}, bf16[576,256]{1,0:T(8,128)(2,1)S(1)}, u32[]{:S(2)}, u32[]{:S(2)}) collective-permute-start(bf16[576,256]{1,0:T(8,128)(2,1)S(1)} %collective-permute-done.4), channel_id=1, source_target_pairs={{0,1},{1,0},{2,3},{3,2},{4,5},{5,4},{6,7},{7,6},{8,9},{9,8},{10,11... | collective-permute-start | bytes 884744 | tf_op jit(solution)/shard_map/ppermute | solution.py:124
  28.3 23.0 %copy-start.4 = (f32[192,128]{1,0:T(8,128)}, f32[192,128]{1,0:T(8,128)S(1)}, u32[]{:S(2)}) copy-start(f32[192,128]{1,0:T(8,128)S(1)} %get-tuple-element.46) | copy-start | bytes 294916
  28.4 11.6 %collective-permute-start.9 = (bf16[208,128]{1,0:T(8,128)(2,1)S(1)}, bf16[208,128]{1,0:T(8,128)(2,1)S(1)}, u32[]{:S(2)}, u32[]{:S(2)}) collective-permute-start(bf16[208,128]{1,0:T(8,128)(2,1)S(1)} %get-tuple-element.38), channel_id=1, source_target_pairs={{0,12},{4,0},{8,4},{12,8},{1,13},{5,1},{9,5},{13,9},{2,14},{6,2},{... | collective-permute-start | bytes 159752 | tf_op jit(solution)/shard_map/ppermute | solution.py:111
  29.1 10.9 %collective-permute-start.8 = (bf16[208,128]{1,0:T(8,128)(2,1)S(1)}, bf16[208,128]{1,0:T(8,128)(2,1)S(1)}, u32[]{:S(2)}, u32[]{:S(2)}) collective-permute-start(bf16[208,128]{1,0:T(8,128)(2,1)S(1)} %get-tuple-element.38), channel_id=1, source_target_pairs={{0,8},{4,12},{8,0},{12,4},{1,9},{5,13},{9,1},{13,5},{2,10},{6,14},... | collective-permute-start | bytes 159752 | tf_op jit(solution)/shard_map/ppermute | solution.py:111
  30.8 9.1 %collective-permute-start.7 = (bf16[208,128]{1,0:T(8,128)(2,1)S(1)}, bf16[208,128]{1,0:T(8,128)(2,1)S(1)}, u32[]{:S(2)}, u32[]{:S(2)}) collective-permute-start(bf16[208,128]{1,0:T(8,128)(2,1)S(1)} %get-tuple-element.38), channel_id=1, source_target_pairs={{0,4},{4,8},{8,12},{12,0},{1,5},{5,9},{9,13},{13,1},{2,6},{6,10},{... | collective-permute-start | bytes 159752 | tf_op jit(solution)/shard_map/ppermute | solution.py:111
  32.8 8.9 %collective-permute-start.10 = (bf16[208,128]{1,0:T(8,128)(2,1)S(1)}, bf16[208,128]{1,0:T(8,128)(2,1)S(1)}, u32[]{:S(2)}, u32[]{:S(2)}) collective-permute-start(bf16[208,128]{1,0:T(8,128)(2,1)S(1)} %get-tuple-element.38), channel_id=1, source_target_pairs={{0,2},{1,3},{2,0},{3,1},{4,6},{5,7},{6,4},{7,5},{8,10},{9,11},{10,... | collective-permute-start | bytes 159752 | tf_op jit(solution)/shard_map/ppermute | solution.py:123
  40.1 5.5 %collective-permute-start.11 = (bf16[624,128]{1,0:T(8,128)(2,1)S(1)}, bf16[624,128]{1,0:T(8,128)(2,1)S(1)}, u32[]{:S(2)}, u32[]{:S(2)}) collective-permute-start(bf16[624,128]{1,0:T(8,128)(2,1)S(1)} %get-tuple-element.39), channel_id=1, source_target_pairs={{0,2},{1,3},{2,0},{3,1},{4,6},{5,7},{6,4},{7,5},{8,10},{9,11},{10,... | collective-permute-start | bytes 479240 | tf_op jit(solution)/shard_map/ppermute | solution.py:124
  42.0 4.2 %collective-permute-start.12 = (bf16[1040,128]{1,0:T(8,128)(2,1)S(1)}, bf16[1040,128]{1,0:T(8,128)(2,1)S(1)}, u32[]{:S(2)}, u32[]{:S(2)}) collective-permute-start(bf16[1040,128]{1,0:T(8,128)(2,1)S(1)} %constant_dynamic-update-slice_fusion.13), channel_id=1, source_target_pairs={{0,1},{1,0},{2,3},{3,2},{4,5},{5,4},{6,7},{7,6},{8,9},{9,8},{10,11... | collective-permute-start | bytes 798728 | tf_op jit(solution)/shard_map/ppermute | solution.py:123
  45.5 2.1 %collective-permute-start.13 = (bf16[624,128]{1,0:T(8,128)(2,1)S(1)}, bf16[624,128]{1,0:T(8,128)(2,1)S(1)}, u32[]{:S(2)}, u32[]{:S(2)}) collective-permute-start(bf16[624,128]{1,0:T(8,128)(2,1)S(1)} %collective-permute-done.11), channel_id=1, source_target_pairs={{0,1},{1,0},{2,3},{3,2},{4,5},{5,4},{6,7},{7,6},{8,9},{9,8},{10,11... | collective-permute-start | bytes 479240 | tf_op jit(solution)/shard_map/ppermute | solution.py:124
  46.2 2.6 %copy-start = (f32[1024,1024]{1,0:T(8,128)S(1)}, f32[1024,1024]{1,0:T(8,128)}, u32[]{:S(2)}) copy-start(f32[1024,1024]{1,0:T(8,128)} %param.13) | copy-start | bytes 12582916

commit v2 on v0

--- a/solution.py
+++ b/solution.py
@@ -99,7 +99,7 @@
     return piece
 
 
-def gather_blocks(block):
+def gather_blocks(block, split_pieces=False):
     n = lax.axis_size("rows") * lax.axis_size("cols")
     if n > PERMUTE_GROUP_MAX:
         got = lax.all_gather(block, ("rows", "cols"), axis=0, tiled=False)
@@ -109,16 +109,18 @@
         return axis_gather(jnp.concatenate(axis_gather(block, "rows"), axis=0), "cols")
     n_rows = lax.axis_size("rows")
     ring = [lax.ppermute(block, "rows", [(i, (i + k) % n_rows) for i in range(n_rows)]) for k in range(1, n_rows)]
+    if split_pieces:
+        return pipelined_xor_gather([block] + ring, "cols", split_first=True)
     return pipelined_xor_gather([block, jnp.concatenate(ring, axis=0)], "cols")
 
 
-def pipelined_xor_gather(parts, axis):
+def pipelined_xor_gather(parts, axis, split_first=False):
     n = lax.axis_size(axis)
     bit = n // 2
     while bit >= 1:
         perm = [(i, i ^ bit) for i in range(n)]
-        if len(parts) == 1:
-            parts = parts + [lax.ppermute(parts[0], axis, perm)]
+        if len(parts) == 1 or (split_first and bit == n // 2):
+            parts = parts + [lax.ppermute(p, axis, perm) for p in parts]
         else:
             held = lax.ppermute(jnp.concatenate(parts[:-1], axis=0), axis, perm)
             newest = lax.ppermute(parts[-1], axis, perm)
@@ -173,7 +175,7 @@
     n_local = points.shape[0]
     solution_b = solution.astype(jnp.bfloat16)
     packed = jnp.concatenate([points, solution_b], axis=1)
-    parts = gather_blocks(packed)
+    parts = gather_blocks(packed, split_pieces=True)
     own_sq = square_norms(points)
     kp = None
     for part in parts:

time: 54.1 us -> 54 us (level)
  waiting for transfers between devices: 12.2 us -> 6.8 us
  matrix products: 14.4 us -> 18 us
  starting transfers between devices: 15 us -> 16 us
    ppermute x0 -> x4, starting transfers between devices: none -> 5.72 us  [pipelined_xor_gather(): parts = parts + [lax.ppermute(p, axis, perm) for p in parts]]
    dot_general x6 -> x10, matrix products: 3.15 us -> 7.74 us  [piece(): return jnp.dot(k, v, preferred_element_type=jnp.float32)]
    ppermute x4 -> x3, waiting for transfers between devices: 9.45 us -> 4.87 us  [pipelined_xor_gather(): newest = lax.ppermute(parts[-1], axis, perm)]
    ppermute x4 -> x3, starting transfers between devices: 3.72 us -> 1.64 us  [pipelined_xor_gather(): held = lax.ppermute(jnp.concatenate(parts[:-1], axis=0), axis, perm)]
    ppermute x6, starting transfers between devices: 8.95 us -> 7.41 us  [gather_blocks(): lax.ppermute(block, 'rows', [(i, (i + k) % n_rows) for i in range(n_rows)])]
    ppermute x4 -> x3, starting transfers between devices: 2.29 us -> 1.23 us  [pipelined_xor_gather(): newest = lax.ppermute(parts[-1], axis, perm)]
    dot_general x2 -> x1, matrix products: 4.34 us -> 3.36 us  [rbf_tile(): lax.dot_general(left_x, right_x, (((1,), (1,)), ((), ())), preferred_elem...]
    ppermute x6, waiting for transfers between devices: 2.69 us -> 1.92 us  [gather_blocks(): lax.ppermute(block, 'rows', [(i, (i + k) % n_rows) for i in range(n_rows)])]
  transfers between devices with their start and end apart: 14 -> 16, of which waited for: 4 -> 3; matrix products, arithmetic and copies ran while one was open for 34% -> 40% of each run, Pallas kernels for 0% -> 0%
where the time goes in v2:
time: 54 us; the launch traced here: 53.3 us
  matrix products  18 us (33%)
  starting transfers between devices  16 us (30%)
  other arithmetic  6.97 us (13%)
  waiting for transfers between devices  6.8 us (13%)
  local copies, waits for them, and re-layouts  4.37 us (8%)
  between operations  1.2 us (2%)
    dot_general x10, matrix products, piece(): return jnp.dot(k, v, preferred_element_type=jnp.float32)  7.74 us
    ppermute x6, starting transfers between devices, gather_blocks(): lax.ppermute(block, 'rows', [(i, (i + k) % n_rows) for i in range(n_rows)])  7.41 us
    ppermute x4, starting transfers between devices, pipelined_xor_gather(): parts = parts + [lax.ppermute(p, axis, perm) for p in parts]  5.72 us
    ppermute x3, waiting for transfers between devices, pipelined_xor_gather(): newest = lax.ppermute(parts[-1], axis, perm)  4.87 us
    dot_general x1, matrix products, rbf_tile(): lax.dot_general(left_x, right_x, (((1,), (1,)), ((), ())), preferred_elem...  3.36 us
    gather x1, local copies, waits for them, and re-layouts, local(): centers = jnp.take(all_x, position, axis=0)  3.21 us
    dot_general x6, matrix products, projected_all(): lax.dot_general(piece, r, contract, preferred_element_type=jnp.float32)  3.17 us
    reduce_sum x12, other arithmetic, square_norms(): return jnp.sum(jnp.square(values.astype(jnp.float32)), axis=1)  2.93 us
  transfers between devices with their start and end apart: 16, of which 3 were waited for; matrix products, arithmetic and copies ran while one was open for 40% of the time, Pallas kernels for 0%

profile of v2, /device:TPU:0, one launch (start us, length us, event | category | flops | bytes accessed | tf_op | source)
XLA Modules:
  0.0 53.3 jit_solution(16474536357854220698)
XLA Ops:
  0.6 0.9 %convert_element_type.138 = bf16[192,128]{1,0:T(8,128)(2,1)S(1)} convert(f32[192,128]{1,0:T(8,128)} %param.10) | non-fusion elementwise | flops 24576 | bytes 147456 | tf_op jit(solution)/shard_map/convert_element_type | solution.py:176
  1.6 0.8 %pad_maximum_fusion = (bf16[192,256]{1,0:T(8,128)(2,1)S(1)}, bf16[1344,256]{1,0:T(8,128)(2,1)S(1)}) fusion(bf16[192,128]{1,0:T(8,128)(2,1)S(1)} %convert_element_type.138, bf16[192,128]{1,0:T(8,128)(2,1)} %param.9), kind=kLoop, calls=%fused_computation.145 | loop fusion | flops 196607 | bytes 294912 | tf_op jit(solution)/shard_map/concatenate | solution.py:177
  2.4 3.0 %collective-permute-start.3 = (bf16[192,256]{1,0:T(8,128)(2,1)S(1)}, bf16[192,256]{1,0:T(8,128)(2,1)S(1)}, u32[]{:S(2)}, u32[]{:S(2)}) collective-permute-start(bf16[192,256]{1,0:T(8,128)(2,1)S(1)} %get-tuple-element.31), channel_id=1, source_target_pairs={{0,2},{1,3},{2,0},{3,1},{4,6},{5,7},{6,4},{7,5},{8,10},{9,11},{10,... | collective-permute-start | bytes 294920 | tf_op jit(solution)/shard_map/ppermute | solution.py:123
  5.4 3.6 %collective-permute-start.2 = (bf16[192,256]{1,0:T(8,128)(2,1)S(1)}, bf16[192,256]{1,0:T(8,128)(2,1)S(1)}, u32[]{:S(2)}, u32[]{:S(2)}) collective-permute-start(bf16[192,256]{1,0:T(8,128)(2,1)S(1)} %get-tuple-element.31), channel_id=1, source_target_pairs={{0,12},{4,0},{8,4},{12,8},{1,13},{5,1},{9,5},{13,9},{2,14},{6,2},{... | collective-permute-start | bytes 294920 | tf_op jit(solution)/shard_map/ppermute | solution.py:111
  9.0 1.0 %collective-permute-start = (bf16[192,256]{1,0:T(8,128)(2,1)S(1)}, bf16[192,256]{1,0:T(8,128)(2,1)S(1)}, u32[]{:S(2)}, u32[]{:S(2)}) collective-permute-start(bf16[192,256]{1,0:T(8,128)(2,1)S(1)} %get-tuple-element.31), channel_id=1, source_target_pairs={{0,4},{4,8},{8,12},{12,0},{1,5},{5,9},{9,13},{13,1},{2,6},{6,10},{... | collective-permute-start | bytes 294920 | tf_op jit(solution)/shard_map/ppermute | solution.py:111
  10.0 0.9 %multiply_reduce_fusion.13 = f32[192]{0:T(256)S(1)} fusion(bf16[192,128]{1,0:T(8,128)(2,1)} %param.9), kind=kLoop, calls=%fused_computation.192 | loop fusion | flops 73536 | bytes 49920 | tf_op jit(solution)/shard_map/reduce_sum | solution.py:15
  10.9 0.9 %multiply_reduce_fusion.3 = f32[128]{0:T(128)S(1)} fusion(f32[192,128]{1,0:T(8,128)} %param.11), kind=kLoop, calls=%fused_computation.148 | loop fusion | flops 49024 | bytes 98816 | tf_op jit(solution)/shard_map/reduce_sum | solution.py:195
  11.9 0.7 %compare_and_fusion = (pred[1024]{0:T(1024)(128)(4,1)S(1)}, s32[1024]{0:T(1024)S(1)}) fusion(s32[]{:T(128)S(6)} %axis_index.25, s32[1024]{0:T(1024)} %param.12, s32[]{:T(128)S(6)} %axis_index.22), kind=kLoop, calls=%fused_computation.259 | loop fusion | flops 62464 | bytes 9224 | tf_op jit(solution)/shard_map/jit(_take)/and | solution.py:190
  12.6 1.3 %fusion.94 = f32[192,128]{1,0:T(8,128)S(1)} fusion(bf16[192,128]{1,0:T(8,128)(2,1)S(1)} %convert_element_type.138, bf16[192,128]{1,0:T(8,128)(2,1)} %param.9, f32[192]{0:T(256)S(1)} %multiply_reduce_fusion.13), kind=kOutput, calls=%fused_computation.108 | convolution fusion | flops 19058688 | bytes 197376 | tf_op jit(solution)/shard_map/dot_general | solution.py:39
  13.9 0.8 %constant_dynamic-update-slice_fusion.15 = bf16[3072,128]{1,0:T(8,128)(2,1)S(1)} fusion(bf16[192,128]{1,0:T(8,128)(2,1)} %param.9), kind=kLoop, calls=%fused_computation.209 | loop fusion | bytes 98304
  14.7 0.6 %collective-permute-start.6 = (bf16[192,256]{1,0:T(8,128)(2,1)S(1)}, bf16[192,256]{1,0:T(8,128)(2,1)S(1)}, u32[]{:S(2)}, u32[]{:S(2)}) collective-permute-start(bf16[192,256]{1,0:T(8,128)(2,1)S(1)} %collective-permute-done.2), channel_id=1, source_target_pairs={{0,2},{1,3},{2,0},{3,1},{4,6},{5,7},{6,4},{7,5},{8,10},{9,11},{10,... | collective-permute-start | bytes 294920 | tf_op jit(solution)/shard_map/ppermute | solution.py:123
  15.4 1.9 %collective-permute-done.1 = bf16[192,256]{1,0:T(8,128)(2,1)S(1)} collective-permute-done((bf16[192,256]{1,0:T(8,128)(2,1)S(1)}, bf16[192,256]{1,0:T(8,128)(2,1)S(1)}, u32[]{:S(2)}, u32[]{:S(2)}) %collective-permute-start.1) | collective-permute-done | bytes 98336 | tf_op jit(solution)/shard_map/ppermute | solution.py:111
  17.4 0.5 %collective-permute-start.5 = (bf16[192,256]{1,0:T(8,128)(2,1)S(1)}, bf16[192,256]{1,0:T(8,128)(2,1)S(1)}, u32[]{:S(2)}, u32[]{:S(2)}) collective-permute-start(bf16[192,256]{1,0:T(8,128)(2,1)S(1)} %collective-permute-done.1), channel_id=1, source_target_pairs={{0,2},{1,3},{2,0},{3,1},{4,6},{5,7},{6,4},{7,5},{8,10},{9,11},{10,... | collective-permute-start | bytes 294920 | tf_op jit(solution)/shard_map/ppermute | solution.py:123
  18.0 1.6 %collective-permute-start.4 = (bf16[192,256]{1,0:T(8,128)(2,1)S(1)}, bf16[192,256]{1,0:T(8,128)(2,1)S(1)}, u32[]{:S(2)}, u32[]{:S(2)}) collective-permute-start(bf16[192,256]{1,0:T(8,128)(2,1)S(1)} %collective-permute-done), channel_id=1, source_target_pairs={{0,2},{1,3},{2,0},{3,1},{4,6},{5,7},{6,4},{7,5},{8,10},{9,11},{10,... | collective-permute-start | bytes 294920 | tf_op jit(solution)/shard_map/ppermute | solution.py:123
  19.8 1.1 %fusion.86 = f32[192,128]{1,0:T(8,128)S(1)} fusion(bf16[192,128]{1,0:T(8,128)(2,1)} %param.9, f32[192]{0:T(256)S(1)} %multiply_reduce_fusion.9, f32[192]{0:T(256)S(1)} %multiply_reduce_fusion.13, bf16[192,256]{1,0:T(8,128)(2,1)S(1)} %collective-permute-done.3), kind=kOutput, calls=%fused_computation.100 | convolution fusion | flops 19058688 | bytes 247296 | tf_op jit(solution)/shard_map/dot_general | solution.py:39
  21.0 1.1 %fusion.87 = f32[192,128]{1,0:T(8,128)S(1)} fusion(bf16[192,128]{1,0:T(8,128)(2,1)} %param.9, f32[192]{0:T(256)S(1)} %multiply_reduce_fusion.10, f32[192]{0:T(256)S(1)} %multiply_reduce_fusion.13, bf16[192,256]{1,0:T(8,128)(2,1)S(1)} %collective-permute-done.2), kind=kOutput, calls=%fused_computation.101 | convolution fusion | flops 19058688 | bytes 247296 | tf_op jit(solution)/shard_map/dot_general | solution.py:39
  22.2 1.1 %fusion.93 = f32[192,128]{1,0:T(8,128)S(1)} fusion(f32[192,128]{1,0:T(8,128)S(1)} %fusion.94, bf16[192,128]{1,0:T(8,128)(2,1)} %param.9, f32[192]{0:T(256)S(1)} %multiply_reduce_fusion.12, f32[192]{0:T(256)S(1)} %multiply_reduce_fusion.13, bf16[192,256]{1,0:T(8,128)(2,1)S(1)} %collective-permute-done), kind=kOutput, calls=%fused_computation.107 | convolution fusion | flops 19083264 | bytes 345600 | tf_op jit(solution)/shard_map/dot_general | solution.py:39
  23.4 1.1 %fusion.91 = f32[192,128]{1,0:T(8,128)S(1)} fusion(f32[192,128]{1,0:T(8,128)S(1)} %fusion.86, f32[192,128]{1,0:T(8,128)S(1)} %fusion.87, f32[192,128]{1,0:T(8,128)S(1)} %fusion.93, bf16[192,128]{1,0:T(8,128)(2,1)} %param.9, f32[192]{0:T(256)S(1)} %multiply_reduce_fusion.11, f32[192]{0:T(256)S(1)} %multiply_reduce_fusion.13, ...), kind=kOutput, calls=%fused_computation.105 | convolution fusion | flops 19132416 | bytes 542208 | tf_op jit(solution)/shard_map/dot_general | solution.py:39
  24.7 0.1 multiply_reduce_fusion.6
  24.8 0.6 %collective-permute-start.8 = (bf16[192,256]{1,0:T(8,128)(2,1)S(1)}, bf16[192,256]{1,0:T(8,128)(2,1)S(1)}, u32[]{:S(2)}, u32[]{:S(2)}) collective-permute-start(bf16[192,256]{1,0:T(8,128)(2,1)S(1)} %collective-permute-done.6), channel_id=1, source_target_pairs={{0,1},{1,0},{2,3},{3,2},{4,5},{5,4},{6,7},{7,6},{8,9},{9,8},{10,11... | collective-permute-start | bytes 294920 | tf_op jit(solution)/shard_map/ppermute | solution.py:126
  25.5 0.3 fusion.79
  25.9 0.3 fusion.80
  26.2 0.1 multiply_reduce_fusion.8
  26.3 0.6 %collective-permute-done.8 = bf16[192,256]{1,0:T(8,128)(2,1)S(1)} collective-permute-done((bf16[192,256]{1,0:T(8,128)(2,1)S(1)}, bf16[192,256]{1,0:T(8,128)(2,1)S(1)}, u32[]{:S(2)}, u32[]{:S(2)}) %collective-permute-start.8) | collective-permute-done | bytes 98336 | tf_op jit(solution)/shard_map/ppermute | solution.py:126
  27.1 0.3 multiply_reduce_fusion.1
  27.3 0.5 fusion.15
  27.9 0.3 fusion.85
  28.2 0.4 multiply_reduce_fusion.4
  28.7 2.1 %collective-permute-start.11 = (bf16[208,128]{1,0:T(8,128)(2,1)S(1)}, bf16[208,128]{1,0:T(8,128)(2,1)S(1)}, u32[]{:S(2)}, u32[]{:S(2)}) collective-permute-start(bf16[208,128]{1,0:T(8,128)(2,1)S(1)} %get-tuple-element.34), channel_id=1, source_target_pairs={{0,12},{4,0},{8,4},{12,8},{1,13},{5,1},{9,5},{13,9},{2,14},{6,2},{... | collective-permute-start | bytes 159752 | tf_op jit(solution)/shard_map/ppermute | solution.py:111
  30.9 0.6 %collective-permute-start.9 = (bf16[208,128]{1,0:T(8,128)(2,1)S(1)}, bf16[208,128]{1,0:T(8,128)(2,1)S(1)}, u32[]{:S(2)}, u32[]{:S(2)}) collective-permute-start(bf16[208,128]{1,0:T(8,128)(2,1)S(1)} %get-tuple-element.34), channel_id=1, source_target_pairs={{0,4},{4,8},{8,12},{12,0},{1,5},{5,9},{9,13},{13,1},{2,6},{6,10},{... | collective-permute-start | bytes 159752 | tf_op jit(solution)/shard_map/ppermute | solution.py:111
  31.5 1.5 %collective-permute-start.12 = (bf16[208,128]{1,0:T(8,128)(2,1)S(1)}, bf16[208,128]{1,0:T(8,128)(2,1)S(1)}, u32[]{:S(2)}, u32[]{:S(2)}) collective-permute-start(bf16[208,128]{1,0:T(8,128)(2,1)S(1)} %get-tuple-element.34), channel_id=1, source_target_pairs={{0,2},{1,3},{2,0},{3,1},{4,6},{5,7},{6,4},{7,5},{8,10},{9,11},{10,... | collective-permute-start | bytes 159752 | tf_op jit(solution)/shard_map/ppermute | solution.py:125
  33.1 0.5 multiply_reduce_fusion
  33.5 3.2 %gather_fusion = bf16[1024,128]{1,0:T(8,128)(2,1)S(1)} fusion(bf16[3072,128]{1,0:T(8,128)(2,1)S(1)} %constant_dynamic-update-slice_fusion.7, s32[1024]{0:T(1024)S(1)} %broadcast_clamp_fusion), kind=kCustom, calls=%fused_computation | custom fusion | bytes 528384 | tf_op jit(solution)/shard_map/jit(_take)/gather | solution.py:190
  36.8 0.4 multiply_reduce_fusion.2
  37.1 3.4 %exponential_convert_fusion = bf16[3072,1024]{1,0:T(8,128)(2,1)S(1)} fusion(bf16[3072,128]{1,0:T(8,128)(2,1)S(1)} %constant_dynamic-update-slice_fusion.7, f32[1024]{0:T(1024)S(1)} %multiply_reduce_fusion.2, f32[3072]{0:T(1024)S(1)} %multiply_reduce_fusion, bf16[1024,128]{1,0:T(8,128)(2,1)S(1)} %gather_fusion, pred[1024]{0:T(1024)(128)(4,1)S(1)} %get-tuple-element.27), kind=kOutput, calls=%fused_computation.1 | convolution fusion | flops 821166080 | bytes 7357440 | tf_op jit(solution)/shard_map/dot_general | solution.py:19
  40.5 0.4 fusion.108
  41.0 0.6 %collective-permute-start.13 = (bf16[624,128]{1,0:T(8,128)(2,1)S(1)}, bf16[624,128]{1,0:T(8,128)(2,1)S(1)}, u32[]{:S(2)}, u32[]{:S(2)}) collective-permute-start(bf16[624,128]{1,0:T(8,128)(2,1)S(1)} %get-tuple-element.35), channel_id=1, source_target_pairs={{0,2},{1,3},{2,0},{3,1},{4,6},{5,7},{6,4},{7,5},{8,10},{9,11},{10,... | collective-permute-start | bytes 479240 | tf_op jit(solution)/shard_map/ppermute | solution.py:126
  41.6 0.3 fusion.106
  42.0 4.3 %collective-permute-done.13 = bf16[624,128]{1,0:T(8,128)(2,1)S(1)} collective-permute-done((bf16[624,128]{1,0:T(8,128)(2,1)S(1)}, bf16[624,128]{1,0:T(8,128)(2,1)S(1)}, u32[]{:S(2)}, u32[]{:S(2)}) %collective-permute-start.13) | collective-permute-done | bytes 159776 | tf_op jit(solution)/shard_map/ppermute | solution.py:126
  46.4 0.6 %fusion.28 = f32[1024,128]{1,0:T(8,128)S(1)} fusion(bf16[576,128]{1,0:T(8,128)(2,1)S(1)} %bitcast.213, bf16[3072,1024]{1,0:T(8,128)(2,1)S(1)} %exponential_convert_fusion), kind=kOutput, calls=%fused_computation.33 | convolution fusion | flops 150994944 | bytes 1851392 | tf_op jit(solution)/shard_map/dot_general | solution.py:152
  47.0 0.8 %fusion.8 = f32[1024,128]{1,0:T(8,128)S(1)} fusion(bf16[960,128]{1,0:T(8,128)(2,1)S(1)} %bitcast.208, bf16[3072,1024]{1,0:T(8,128)(2,1)S(1)} %exponential_convert_fusion), kind=kOutput, calls=%fused_computation.12 | convolution fusion | flops 251658240 | bytes 2736128 | tf_op jit(solution)/shard_map/dot_general | solution.py:152
  47.8 0.6 %fusion.18 = f32[1024,128]{1,0:T(8,128)S(1)} fusion(f32[1024,128]{1,0:T(8,128)S(1)} %fusion.8, f32[1024,128]{1,0:T(8,128)S(1)} %fusion.28, f32[1024,128]{1,0:T(8,128)S(1)} %fusion.106, f32[1024,128]{1,0:T(8,128)S(1)} %fusion.108, bf16[576,128]{1,0:T(8,128)(2,1)S(1)} %bitcast.204, bf16[3072,1024]{1,0:T(8,128)(2,1)S(1)} %exponential_convert_fusion), kind=kOutput, calls=%fused_computation.26 | convolution fusion | flops 151519232 | bytes 3948544 | tf_op jit(solution)/shard_map/dot_general | solution.py:152
  48.5 0.5 sqrt_bitcast_fusion
  49.0 0.6 %convolution_add_fusion = f32[1024,128]{1,0:T(8,128)S(1)} fusion(f32[1024,128]{1,0:T(8,128)S(1)} %fusion.18, bf16[576,128]{1,0:T(8,128)(2,1)S(1)} %bitcast.205, bf16[3072,1024]{1,0:T(8,128)(2,1)S(1)} %exponential_convert_fusion), kind=kOutput, calls=%fused_computation.22 | convolution fusion | flops 151126016 | bytes 2375680 | tf_op jit(solution)/shard_map/dot_general | solution.py:152
  49.6 0.8 %fusion.99 = f32[128,1024]{1,0:T(8,128)S(1)} fusion(f32[1024,1024]{1,0:T(8,128)S(1)} %copy-done, f32[1024,128]{1,0:T(8,128)S(1)} %convolution_add_fusion), kind=kOutput, calls=%fused_computation.113 | convolution fusion | flops 270794752 | bytes 5242880 | tf_op jit(solution)/shard_map/dot_general | solution.py:213
  50.4 0.8 %fusion.22 = f32[1024,128]{0,1:T(8,128)S(1)} fusion(f32[128,1024]{1,0:T(8,128)S(1)} %fusion.99, f32[1024,1024]{1,0:T(8,128)S(1)} %copy-done, f32[1024,128]{1,0:T(8,128)S(1)} %convolution_add_fusion), kind=kOutput, calls=%fused_computation.29 | convolution fusion | flops 271056896 | bytes 5767168 | tf_op jit(solution)/shard_map/dot_general | solution.py:214
  51.3 0.8 %fusion.24 = bf16[1024,128]{0,1:T(8,128)(2,1)S(1)} fusion(f32[1024,128]{0,1:T(8,128)S(1)} %fusion.22, f32[1024,1024]{1,0:T(8,128)S(1)} %copy-done, f32[1024,128]{1,0:T(8,128)S(1)} %convolution_add_fusion), kind=kOutput, calls=%fused_computation.31 | convolution fusion | flops 272105472 | bytes 5505024 | tf_op jit(solution)/shard_map/dot_general | solution.py:215
  52.1 1.2 %fusion.97 = f32[192,128]{1,0:T(8,128)} fusion(f32[192,128]{1,0:T(8,128)S(1)} %copy-done.3, f32[192,128]{1,0:T(8,128)S(1)} %get-tuple-element.42, bf16[1024,128]{0,1:T(8,128)(2,1)S(1)} %fusion.24, bf16[192,128]{1,0:T(8,128)(2,1)S(1)} %copy-done.1, f32[1024]{0:T(1024)S(1)} %multiply_reduce_fusion.2, f32[192]{0:T(256)S(1)} %multiply_reduce_fusion.13, ...), kind=kOutput, calls=%fused_computation.111 | convolution fusion | flops 101851136 | bytes 874240 | tf_op jit(solution)/shard_map/dot_general | solution.py:217
  (69 shorter events, 1.5 us)
Async XLA Ops:
  0.6 24.8 %copy-start.1 = (bf16[192,128]{1,0:T(8,128)(2,1)S(1)}, bf16[192,128]{1,0:T(8,128)(2,1)}, u32[]{:S(2)}) copy-start(bf16[192,128]{1,0:T(8,128)(2,1)} %param.9) | copy-start | bytes 147460
  2.4 17.3 %collective-permute-start.3 = (bf16[192,256]{1,0:T(8,128)(2,1)S(1)}, bf16[192,256]{1,0:T(8,128)(2,1)S(1)}, u32[]{:S(2)}, u32[]{:S(2)}) collective-permute-start(bf16[192,256]{1,0:T(8,128)(2,1)S(1)} %get-tuple-element.31), channel_id=1, source_target_pairs={{0,2},{1,3},{2,0},{3,1},{4,6},{5,7},{6,4},{7,5},{8,10},{9,11},{10,... | collective-permute-start | bytes 294920 | tf_op jit(solution)/shard_map/ppermute | solution.py:123
  5.4 9.3 %collective-permute-start.2 = (bf16[192,256]{1,0:T(8,128)(2,1)S(1)}, bf16[192,256]{1,0:T(8,128)(2,1)S(1)}, u32[]{:S(2)}, u32[]{:S(2)}) collective-permute-start(bf16[192,256]{1,0:T(8,128)(2,1)S(1)} %get-tuple-element.31), channel_id=1, source_target_pairs={{0,12},{4,0},{8,4},{12,8},{1,13},{5,1},{9,5},{13,9},{2,14},{6,2},{... | collective-permute-start | bytes 294920 | tf_op jit(solution)/shard_map/ppermute | solution.py:111
  9.0 8.3 %collective-permute-start.1 = (bf16[192,256]{1,0:T(8,128)(2,1)S(1)}, bf16[192,256]{1,0:T(8,128)(2,1)S(1)}, u32[]{:S(2)}, u32[]{:S(2)}) collective-permute-start(bf16[192,256]{1,0:T(8,128)(2,1)S(1)} %get-tuple-element.31), channel_id=1, source_target_pairs={{0,8},{4,12},{8,0},{12,4},{1,9},{5,13},{9,1},{13,5},{2,10},{6,14},... | collective-permute-start | bytes 294920 | tf_op jit(solution)/shard_map/ppermute | solution.py:111
  9.0 9.0 %collective-permute-start = (bf16[192,256]{1,0:T(8,128)(2,1)S(1)}, bf16[192,256]{1,0:T(8,128)(2,1)S(1)}, u32[]{:S(2)}, u32[]{:S(2)}) collective-permute-start(bf16[192,256]{1,0:T(8,128)(2,1)S(1)} %get-tuple-element.31), channel_id=1, source_target_pairs={{0,4},{4,8},{8,12},{12,0},{1,5},{5,9},{9,13},{13,1},{2,6},{6,10},{... | collective-permute-start | bytes 294920 | tf_op jit(solution)/shard_map/ppermute | solution.py:111
  14.7 13.5 %copy-start.2 = (f32[192,128]{1,0:T(8,128)S(1)}, f32[192,128]{1,0:T(8,128)}, u32[]{:S(2)}) copy-start(f32[192,128]{1,0:T(8,128)} %param.11) | copy-start | bytes 294916
  14.7 13.5 %copy-start.3 = (f32[192,128]{1,0:T(8,128)S(1)}, f32[192,128]{1,0:T(8,128)}, u32[]{:S(2)}) copy-start(f32[192,128]{1,0:T(8,128)} %param.10) | copy-start | bytes 294916
  14.7 9.9 %collective-permute-start.6 = (bf16[192,256]{1,0:T(8,128)(2,1)S(1)}, bf16[192,256]{1,0:T(8,128)(2,1)S(1)}, u32[]{:S(2)}, u32[]{:S(2)}) collective-permute-start(bf16[192,256]{1,0:T(8,128)(2,1)S(1)} %collective-permute-done.2), channel_id=1, source_target_pairs={{0,2},{1,3},{2,0},{3,1},{4,6},{5,7},{6,4},{7,5},{8,10},{9,11},{10,... | collective-permute-start | bytes 294920 | tf_op jit(solution)/shard_map/ppermute | solution.py:123
  17.4 7.2 %collective-permute-start.5 = (bf16[192,256]{1,0:T(8,128)(2,1)S(1)}, bf16[192,256]{1,0:T(8,128)(2,1)S(1)}, u32[]{:S(2)}, u32[]{:S(2)}) collective-permute-start(bf16[192,256]{1,0:T(8,128)(2,1)S(1)} %collective-permute-done.1), channel_id=1, source_target_pairs={{0,2},{1,3},{2,0},{3,1},{4,6},{5,7},{6,4},{7,5},{8,10},{9,11},{10,... | collective-permute-start | bytes 294920 | tf_op jit(solution)/shard_map/ppermute | solution.py:123
  18.0 6.5 %collective-permute-start.4 = (bf16[192,256]{1,0:T(8,128)(2,1)S(1)}, bf16[192,256]{1,0:T(8,128)(2,1)S(1)}, u32[]{:S(2)}, u32[]{:S(2)}) collective-permute-start(bf16[192,256]{1,0:T(8,128)(2,1)S(1)} %collective-permute-done), channel_id=1, source_target_pairs={{0,2},{1,3},{2,0},{3,1},{4,6},{5,7},{6,4},{7,5},{8,10},{9,11},{10,... | collective-permute-start | bytes 294920 | tf_op jit(solution)/shard_map/ppermute | solution.py:123
  24.6 2.5 %collective-permute-start.7 = (bf16[1344,256]{1,0:T(8,128)(2,1)S(1)}, bf16[1344,256]{1,0:T(8,128)(2,1)S(1)}, u32[]{:S(2)}, u32[]{:S(2)}) collective-permute-start(bf16[1344,256]{1,0:T(8,128)(2,1)S(1)} %constant_dynamic-update-slice_fusion), channel_id=1, source_target_pairs={{0,1},{1,0},{2,3},{3,2},{4,5},{5,4},{6,7},{7,6},{8,9},{9,8},{10,11... | collective-permute-start | bytes 2064392 | tf_op jit(solution)/shard_map/ppermute | solution.py:125
  24.8 2.1 %collective-permute-start.8 = (bf16[192,256]{1,0:T(8,128)(2,1)S(1)}, bf16[192,256]{1,0:T(8,128)(2,1)S(1)}, u32[]{:S(2)}, u32[]{:S(2)}) collective-permute-start(bf16[192,256]{1,0:T(8,128)(2,1)S(1)} %collective-permute-done.6), channel_id=1, source_target_pairs={{0,1},{1,0},{2,3},{3,2},{4,5},{5,4},{6,7},{7,6},{8,9},{9,8},{10,11... | collective-permute-start | bytes 294920 | tf_op jit(solution)/shard_map/ppermute | solution.py:126
  28.6 23.5 %copy-start.4 = (f32[192,128]{1,0:T(8,128)}, f32[192,128]{1,0:T(8,128)S(1)}, u32[]{:S(2)}) copy-start(f32[192,128]{1,0:T(8,128)S(1)} %get-tuple-element.42) | copy-start | bytes 294916
  28.7 12.2 %collective-permute-start.11 = (bf16[208,128]{1,0:T(8,128)(2,1)S(1)}, bf16[208,128]{1,0:T(8,128)(2,1)S(1)}, u32[]{:S(2)}, u32[]{:S(2)}) collective-permute-start(bf16[208,128]{1,0:T(8,128)(2,1)S(1)} %get-tuple-element.34), channel_id=1, source_target_pairs={{0,12},{4,0},{8,4},{12,8},{1,13},{5,1},{9,5},{13,9},{2,14},{6,2},{... | collective-permute-start | bytes 159752 | tf_op jit(solution)/shard_map/ppermute | solution.py:111
  30.8 10.1 %collective-permute-start.10 = (bf16[208,128]{1,0:T(8,128)(2,1)S(1)}, bf16[208,128]{1,0:T(8,128)(2,1)S(1)}, u32[]{:S(2)}, u32[]{:S(2)}) collective-permute-start(bf16[208,128]{1,0:T(8,128)(2,1)S(1)} %get-tuple-element.34), channel_id=1, source_target_pairs={{0,8},{4,12},{8,0},{12,4},{1,9},{5,13},{9,1},{13,5},{2,10},{6,14},... | collective-permute-start | bytes 159752 | tf_op jit(solution)/shard_map/ppermute | solution.py:111
  30.9 10.0 %collective-permute-start.9 = (bf16[208,128]{1,0:T(8,128)(2,1)S(1)}, bf16[208,128]{1,0:T(8,128)(2,1)S(1)}, u32[]{:S(2)}, u32[]{:S(2)}) collective-permute-start(bf16[208,128]{1,0:T(8,128)(2,1)S(1)} %get-tuple-element.34), channel_id=1, source_target_pairs={{0,4},{4,8},{8,12},{12,0},{1,5},{5,9},{9,13},{13,1},{2,6},{6,10},{... | collective-permute-start | bytes 159752 | tf_op jit(solution)/shard_map/ppermute | solution.py:111
  31.5 10.1 %collective-permute-start.12 = (bf16[208,128]{1,0:T(8,128)(2,1)S(1)}, bf16[208,128]{1,0:T(8,128)(2,1)S(1)}, u32[]{:S(2)}, u32[]{:S(2)}) collective-permute-start(bf16[208,128]{1,0:T(8,128)(2,1)S(1)} %get-tuple-element.34), channel_id=1, source_target_pairs={{0,2},{1,3},{2,0},{3,1},{4,6},{5,7},{6,4},{7,5},{8,10},{9,11},{10,... | collective-permute-start | bytes 159752 | tf_op jit(solution)/shard_map/ppermute | solution.py:125
  41.0 5.3 %collective-permute-start.13 = (bf16[624,128]{1,0:T(8,128)(2,1)S(1)}, bf16[624,128]{1,0:T(8,128)(2,1)S(1)}, u32[]{:S(2)}, u32[]{:S(2)}) collective-permute-start(bf16[624,128]{1,0:T(8,128)(2,1)S(1)} %get-tuple-element.35), channel_id=1, source_target_pairs={{0,2},{1,3},{2,0},{3,1},{4,6},{5,7},{6,4},{7,5},{8,10},{9,11},{10,... | collective-permute-start | bytes 479240 | tf_op jit(solution)/shard_map/ppermute | solution.py:126
  42.0 5.0 %collective-permute-start.14 = (bf16[1040,128]{1,0:T(8,128)(2,1)S(1)}, bf16[1040,128]{1,0:T(8,128)(2,1)S(1)}, u32[]{:S(2)}, u32[]{:S(2)}) collective-permute-start(bf16[1040,128]{1,0:T(8,128)(2,1)S(1)} %constant_dynamic-update-slice_fusion.19), channel_id=1, source_target_pairs={{0,1},{1,0},{2,3},{3,2},{4,5},{5,4},{6,7},{7,6},{8,9},{9,8},{10,11... | collective-permute-start | bytes 798728 | tf_op jit(solution)/shard_map/ppermute | solution.py:125
  46.3 2.1 %collective-permute-start.15 = (bf16[624,128]{1,0:T(8,128)(2,1)S(1)}, bf16[624,128]{1,0:T(8,128)(2,1)S(1)}, u32[]{:S(2)}, u32[]{:S(2)}) collective-permute-start(bf16[624,128]{1,0:T(8,128)(2,1)S(1)} %collective-permute-done.13), channel_id=1, source_target_pairs={{0,1},{1,0},{2,3},{3,2},{4,5},{5,4},{6,7},{7,6},{8,9},{9,8},{10,11... | collective-permute-start | bytes 479240 | tf_op jit(solution)/shard_map/ppermute | solution.py:126
  47.0 2.5 %copy-start = (f32[1024,1024]{1,0:T(8,128)S(1)}, f32[1024,1024]{1,0:T(8,128)}, u32[]{:S(2)}) copy-start(f32[1024,1024]{1,0:T(8,128)} %param.13) | copy-start | bytes 12582916

commit v3 on v2

--- a/solution.py
+++ b/solution.py
@@ -152,7 +152,7 @@
             term = lax.dot_general(piece, r, contract, preferred_element_type=jnp.float32)
             total_p = term if total_p is None else total_p + term
             begin += r.shape[0]
-        return total_p
+        return total_p, c
 
     residual_b_all = jnp.concatenate(residual_parts, axis=0)
 
@@ -167,7 +167,7 @@
         return acc + piece(i * chunk)
 
     init = jnp.zeros((centers.shape[0], residual_b_all.shape[1]), jnp.float32)
-    return lax.fori_loop(0, steps, body, init)
+    return lax.fori_loop(0, steps, body, init), None
 
 
 def local(points, solution, targets, inducing, woodbury_inverse):
@@ -206,7 +206,9 @@
     res_sq = norms[0]
     tar_sq = norms[1]
     residual_parts = [g[:, :n_local].reshape(-1, width) for g in got_parts]
-    projected = projected_all(all_x, all_sq, centers, centers_sq, residual_parts, gamma)
+    projected, cross_all = projected_all(all_x, all_sq, centers, centers_sq, residual_parts, gamma)
+    if cross_all is not None:
+        cross = lax.slice_in_dim(cross_all, 0, n_local, axis=0)
     w_hi, w_lo = split_bf16(woodbury_inverse)
     p_hi, p_lo = split_bf16(projected)
     weights = (

time: 54 us -> 56 us (1.037)
  matrix products: 18 us -> 20 us
    dot_general x1, matrix products: 1.2 us -> 4.03 us  [local(): jnp.dot(cross, weights.astype(jnp.bfloat16), preferred_element_type=jnp.f...]
    dot_general x1 -> x0, matrix products: 0.84 us -> none  [local(): jnp.dot(w_lo, p_hi, preferred_element_type=jnp.float32)]
  transfers between devices with their start and end apart: 16 -> 16, of which waited for: 3 -> 3; matrix products, arithmetic and copies ran while one was open for 40% -> 38% of each run, Pallas kernels for 0% -> 0%
where the time goes in v3:
time: 56 us; the launch traced here: 55.3 us
  matrix products  20 us (36%)
  starting transfers between devices  16 us (29%)
  other arithmetic  6.97 us (12%)
  waiting for transfers between devices  6.8 us (12%)
  local copies, waits for them, and re-layouts  4.38 us (8%)
  between operations  1.2 us (2%)
    dot_general x10, matrix products, piece(): return jnp.dot(k, v, preferred_element_type=jnp.float32)  7.74 us
    ppermute x6, starting transfers between devices, gather_blocks(): lax.ppermute(block, 'rows', [(i, (i + k) % n_rows) for i in range(n_rows)])  7.41 us
    ppermute x4, starting transfers between devices, pipelined_xor_gather(): parts = parts + [lax.ppermute(p, axis, perm) for p in parts]  5.72 us
    ppermute x3, waiting for transfers between devices, pipelined_xor_gather(): newest = lax.ppermute(parts[-1], axis, perm)  4.86 us
    dot_general x1, matrix products, local(): jnp.dot(cross, weights.astype(jnp.bfloat16), preferred_element_type=jnp.f...  4.03 us
    dot_general x1, matrix products, rbf_tile(): lax.dot_general(left_x, right_x, (((1,), (1,)), ((), ())), preferred_elem...  3.36 us
    gather x1, local copies, waits for them, and re-layouts, local(): centers = jnp.take(all_x, position, axis=0)  3.21 us
    dot_general x6, matrix products, projected_all(): lax.dot_general(piece, r, contract, preferred_element_type=jnp.float32)  3.17 us
  transfers between devices with their start and end apart: 16, of which 3 were waited for; matrix products, arithmetic and copies ran while one was open for 38% of the time, Pallas kernels for 0%

profile of v3, /device:TPU:0, one launch (start us, length us, event | category | flops | bytes accessed | tf_op | source)
XLA Modules:
  0.0 55.3 jit_solution(2479333466740194188)
XLA Ops:
  0.6 0.9 %convert_element_type.135 = bf16[192,128]{1,0:T(8,128)(2,1)S(1)} convert(f32[192,128]{1,0:T(8,128)} %param.10) | non-fusion elementwise | flops 24576 | bytes 147456 | tf_op jit(solution)/shard_map/convert_element_type | solution.py:176
  1.6 0.8 %pad_maximum_fusion = (bf16[192,256]{1,0:T(8,128)(2,1)S(1)}, bf16[1344,256]{1,0:T(8,128)(2,1)S(1)}) fusion(bf16[192,128]{1,0:T(8,128)(2,1)S(1)} %convert_element_type.135, bf16[192,128]{1,0:T(8,128)(2,1)} %param.9), kind=kLoop, calls=%fused_computation.135 | loop fusion | flops 196607 | bytes 294912 | tf_op jit(solution)/shard_map/concatenate | solution.py:177
  2.4 3.0 %collective-permute-start.3 = (bf16[192,256]{1,0:T(8,128)(2,1)S(1)}, bf16[192,256]{1,0:T(8,128)(2,1)S(1)}, u32[]{:S(2)}, u32[]{:S(2)}) collective-permute-start(bf16[192,256]{1,0:T(8,128)(2,1)S(1)} %get-tuple-element.31), channel_id=1, source_target_pairs={{0,2},{1,3},{2,0},{3,1},{4,6},{5,7},{6,4},{7,5},{8,10},{9,11},{10,... | collective-permute-start | bytes 294920 | tf_op jit(solution)/shard_map/ppermute | solution.py:123
  5.4 3.6 %collective-permute-start.2 = (bf16[192,256]{1,0:T(8,128)(2,1)S(1)}, bf16[192,256]{1,0:T(8,128)(2,1)S(1)}, u32[]{:S(2)}, u32[]{:S(2)}) collective-permute-start(bf16[192,256]{1,0:T(8,128)(2,1)S(1)} %get-tuple-element.31), channel_id=1, source_target_pairs={{0,12},{4,0},{8,4},{12,8},{1,13},{5,1},{9,5},{13,9},{2,14},{6,2},{... | collective-permute-start | bytes 294920 | tf_op jit(solution)/shard_map/ppermute | solution.py:111
  9.0 1.0 %collective-permute-start = (bf16[192,256]{1,0:T(8,128)(2,1)S(1)}, bf16[192,256]{1,0:T(8,128)(2,1)S(1)}, u32[]{:S(2)}, u32[]{:S(2)}) collective-permute-start(bf16[192,256]{1,0:T(8,128)(2,1)S(1)} %get-tuple-element.31), channel_id=1, source_target_pairs={{0,4},{4,8},{8,12},{12,0},{1,5},{5,9},{9,13},{13,1},{2,6},{6,10},{... | collective-permute-start | bytes 294920 | tf_op jit(solution)/shard_map/ppermute | solution.py:111
  10.0 0.9 %multiply_reduce_fusion.13 = f32[192]{0:T(256)S(1)} fusion(bf16[192,128]{1,0:T(8,128)(2,1)} %param.9), kind=kLoop, calls=%fused_computation.182 | loop fusion | flops 73536 | bytes 49920 | tf_op jit(solution)/shard_map/reduce_sum | solution.py:15
  10.9 0.9 %multiply_reduce_fusion.3 = f32[128]{0:T(128)S(1)} fusion(f32[192,128]{1,0:T(8,128)} %param.11), kind=kLoop, calls=%fused_computation.138 | loop fusion | flops 49024 | bytes 98816 | tf_op jit(solution)/shard_map/reduce_sum | solution.py:195
  11.9 0.7 %compare_and_fusion = (pred[1024]{0:T(1024)(128)(4,1)S(1)}, s32[1024]{0:T(1024)S(1)}) fusion(s32[]{:T(128)S(6)} %axis_index.25, s32[1024]{0:T(1024)} %param.12, s32[]{:T(128)S(6)} %axis_index.22), kind=kLoop, calls=%fused_computation.249 | loop fusion | flops 62464 | bytes 9224 | tf_op jit(solution)/shard_map/jit(_take)/and | solution.py:190
  12.6 1.3 %fusion.100 = f32[192,128]{1,0:T(8,128)S(1)} fusion(bf16[192,128]{1,0:T(8,128)(2,1)S(1)} %convert_element_type.135, bf16[192,128]{1,0:T(8,128)(2,1)} %param.9, f32[192]{0:T(256)S(1)} %multiply_reduce_fusion.13), kind=kOutput, calls=%fused_computation.105 | convolution fusion | flops 19058688 | bytes 197376 | tf_op jit(solution)/shard_map/dot_general | solution.py:39
  13.9 0.8 %constant_dynamic-update-slice_fusion.15 = bf16[3072,128]{1,0:T(8,128)(2,1)S(1)} fusion(bf16[192,128]{1,0:T(8,128)(2,1)} %param.9), kind=kLoop, calls=%fused_computation.199 | loop fusion | bytes 98304
  14.7 0.6 %collective-permute-start.6 = (bf16[192,256]{1,0:T(8,128)(2,1)S(1)}, bf16[192,256]{1,0:T(8,128)(2,1)S(1)}, u32[]{:S(2)}, u32[]{:S(2)}) collective-permute-start(bf16[192,256]{1,0:T(8,128)(2,1)S(1)} %collective-permute-done.2), channel_id=1, source_target_pairs={{0,2},{1,3},{2,0},{3,1},{4,6},{5,7},{6,4},{7,5},{8,10},{9,11},{10,... | collective-permute-start | bytes 294920 | tf_op jit(solution)/shard_map/ppermute | solution.py:123
  15.4 1.9 %collective-permute-done.1 = bf16[192,256]{1,0:T(8,128)(2,1)S(1)} collective-permute-done((bf16[192,256]{1,0:T(8,128)(2,1)S(1)}, bf16[192,256]{1,0:T(8,128)(2,1)S(1)}, u32[]{:S(2)}, u32[]{:S(2)}) %collective-permute-start.1) | collective-permute-done | bytes 98336 | tf_op jit(solution)/shard_map/ppermute | solution.py:111
  17.4 0.5 collective-permute-start.5
  18.0 1.6 %collective-permute-start.4 = (bf16[192,256]{1,0:T(8,128)(2,1)S(1)}, bf16[192,256]{1,0:T(8,128)(2,1)S(1)}, u32[]{:S(2)}, u32[]{:S(2)}) collective-permute-start(bf16[192,256]{1,0:T(8,128)(2,1)S(1)} %collective-permute-done), channel_id=1, source_target_pairs={{0,2},{1,3},{2,0},{3,1},{4,6},{5,7},{6,4},{7,5},{8,10},{9,11},{10,... | collective-permute-start | bytes 294920 | tf_op jit(solution)/shard_map/ppermute | solution.py:123
  19.7 0.1 multiply_reduce_fusion.9
  19.8 1.1 %fusion.92 = f32[192,128]{1,0:T(8,128)S(1)} fusion(bf16[192,128]{1,0:T(8,128)(2,1)} %param.9, f32[192]{0:T(256)S(1)} %multiply_reduce_fusion.9, f32[192]{0:T(256)S(1)} %multiply_reduce_fusion.13, bf16[192,256]{1,0:T(8,128)(2,1)S(1)} %collective-permute-done.3), kind=kOutput, calls=%fused_computation.97 | convolution fusion | flops 19058688 | bytes 247296 | tf_op jit(solution)/shard_map/dot_general | solution.py:39
  21.0 1.1 %fusion.93 = f32[192,128]{1,0:T(8,128)S(1)} fusion(bf16[192,128]{1,0:T(8,128)(2,1)} %param.9, f32[192]{0:T(256)S(1)} %multiply_reduce_fusion.10, f32[192]{0:T(256)S(1)} %multiply_reduce_fusion.13, bf16[192,256]{1,0:T(8,128)(2,1)S(1)} %collective-permute-done.2), kind=kOutput, calls=%fused_computation.98 | convolution fusion | flops 19058688 | bytes 247296 | tf_op jit(solution)/shard_map/dot_general | solution.py:39
  22.2 1.1 %fusion.99 = f32[192,128]{1,0:T(8,128)S(1)} fusion(f32[192,128]{1,0:T(8,128)S(1)} %fusion.100, bf16[192,128]{1,0:T(8,128)(2,1)} %param.9, f32[192]{0:T(256)S(1)} %multiply_reduce_fusion.12, f32[192]{0:T(256)S(1)} %multiply_reduce_fusion.13, bf16[192,256]{1,0:T(8,128)(2,1)S(1)} %collective-permute-done), kind=kOutput, calls=%fused_computation.104 | convolution fusion | flops 19083264 | bytes 345600 | tf_op jit(solution)/shard_map/dot_general | solution.py:39
  23.4 1.1 %fusion.97 = f32[192,128]{1,0:T(8,128)S(1)} fusion(f32[192,128]{1,0:T(8,128)S(1)} %fusion.92, f32[192,128]{1,0:T(8,128)S(1)} %fusion.93, f32[192,128]{1,0:T(8,128)S(1)} %fusion.99, bf16[192,128]{1,0:T(8,128)(2,1)} %param.9, f32[192]{0:T(256)S(1)} %multiply_reduce_fusion.11, f32[192]{0:T(256)S(1)} %multiply_reduce_fusion.13, ...), kind=kOutput, calls=%fused_computation.102 | convolution fusion | flops 19132416 | bytes 542208 | tf_op jit(solution)/shard_map/dot_general | solution.py:39
  24.7 0.1 multiply_reduce_fusion.6
  24.8 0.6 %collective-permute-start.8 = (bf16[192,256]{1,0:T(8,128)(2,1)S(1)}, bf16[192,256]{1,0:T(8,128)(2,1)S(1)}, u32[]{:S(2)}, u32[]{:S(2)}) collective-permute-start(bf16[192,256]{1,0:T(8,128)(2,1)S(1)} %collective-permute-done.6), channel_id=1, source_target_pairs={{0,1},{1,0},{2,3},{3,2},{4,5},{5,4},{6,7},{7,6},{8,9},{9,8},{10,11... | collective-permute-start | bytes 294920 | tf_op jit(solution)/shard_map/ppermute | solution.py:126
  25.5 0.3 fusion.85
  25.9 0.3 fusion.86
  26.2 0.1 multiply_reduce_fusion.8
  26.3 0.6 %collective-permute-done.8 = bf16[192,256]{1,0:T(8,128)(2,1)S(1)} collective-permute-done((bf16[192,256]{1,0:T(8,128)(2,1)S(1)}, bf16[192,256]{1,0:T(8,128)(2,1)S(1)}, u32[]{:S(2)}, u32[]{:S(2)}) %collective-permute-start.8) | collective-permute-done | bytes 98336 | tf_op jit(solution)/shard_map/ppermute | solution.py:126
  27.1 0.3 multiply_reduce_fusion.1
  27.3 0.5 fusion.10
  27.9 0.3 fusion.91
  28.2 0.4 multiply_reduce_fusion.4
  28.7 2.1 %collective-permute-start.11 = (bf16[208,128]{1,0:T(8,128)(2,1)S(1)}, bf16[208,128]{1,0:T(8,128)(2,1)S(1)}, u32[]{:S(2)}, u32[]{:S(2)}) collective-permute-start(bf16[208,128]{1,0:T(8,128)(2,1)S(1)} %get-tuple-element.34), channel_id=1, source_target_pairs={{0,12},{4,0},{8,4},{12,8},{1,13},{5,1},{9,5},{13,9},{2,14},{6,2},{... | collective-permute-start | bytes 159752 | tf_op jit(solution)/shard_map/ppermute | solution.py:111
  30.9 0.6 %collective-permute-start.9 = (bf16[208,128]{1,0:T(8,128)(2,1)S(1)}, bf16[208,128]{1,0:T(8,128)(2,1)S(1)}, u32[]{:S(2)}, u32[]{:S(2)}) collective-permute-start(bf16[208,128]{1,0:T(8,128)(2,1)S(1)} %get-tuple-element.34), channel_id=1, source_target_pairs={{0,4},{4,8},{8,12},{12,0},{1,5},{5,9},{9,13},{13,1},{2,6},{6,10},{... | collective-permute-start | bytes 159752 | tf_op jit(solution)/shard_map/ppermute | solution.py:111
  31.5 1.5 %collective-permute-start.12 = (bf16[208,128]{1,0:T(8,128)(2,1)S(1)}, bf16[208,128]{1,0:T(8,128)(2,1)S(1)}, u32[]{:S(2)}, u32[]{:S(2)}) collective-permute-start(bf16[208,128]{1,0:T(8,128)(2,1)S(1)} %get-tuple-element.34), channel_id=1, source_target_pairs={{0,2},{1,3},{2,0},{3,1},{4,6},{5,7},{6,4},{7,5},{8,10},{9,11},{10,... | collective-permute-start | bytes 159752 | tf_op jit(solution)/shard_map/ppermute | solution.py:125
  33.0 0.5 multiply_reduce_fusion
  33.5 3.2 %gather_fusion = bf16[1024,128]{1,0:T(8,128)(2,1)S(1)} fusion(bf16[3072,128]{1,0:T(8,128)(2,1)S(1)} %constant_dynamic-update-slice_fusion.7, s32[1024]{0:T(1024)S(1)} %broadcast_clamp_fusion), kind=kCustom, calls=%fused_computation | custom fusion | bytes 528384 | tf_op jit(solution)/shard_map/jit(_take)/gather | solution.py:190
  36.7 0.4 multiply_reduce_fusion.2
  37.1 3.4 %exponential_convert_fusion = bf16[3072,1024]{1,0:T(8,128)(2,1)S(1)} fusion(bf16[3072,128]{1,0:T(8,128)(2,1)S(1)} %constant_dynamic-update-slice_fusion.7, f32[1024]{0:T(1024)S(1)} %multiply_reduce_fusion.2, f32[3072]{0:T(1024)S(1)} %multiply_reduce_fusion, bf16[1024,128]{1,0:T(8,128)(2,1)S(1)} %gather_fusion, pred[1024]{0:T(1024)(128)(4,1)S(1)} %get-tuple-element.27), kind=kOutput, calls=%fused_computation.1 | convolution fusion | flops 821166080 | bytes 7357440 | tf_op jit(solution)/shard_map/dot_general | solution.py:19
  40.5 0.4 fusion.111
  41.0 0.6 %collective-permute-start.13 = (bf16[624,128]{1,0:T(8,128)(2,1)S(1)}, bf16[624,128]{1,0:T(8,128)(2,1)S(1)}, u32[]{:S(2)}, u32[]{:S(2)}) collective-permute-start(bf16[624,128]{1,0:T(8,128)(2,1)S(1)} %get-tuple-element.35), channel_id=1, source_target_pairs={{0,2},{1,3},{2,0},{3,1},{4,6},{5,7},{6,4},{7,5},{8,10},{9,11},{10,... | collective-permute-start | bytes 479240 | tf_op jit(solution)/shard_map/ppermute | solution.py:126
  41.6 0.4 fusion.108
  42.1 4.2 %collective-permute-done.13 = bf16[624,128]{1,0:T(8,128)(2,1)S(1)} collective-permute-done((bf16[624,128]{1,0:T(8,128)(2,1)S(1)}, bf16[624,128]{1,0:T(8,128)(2,1)S(1)}, u32[]{:S(2)}, u32[]{:S(2)}) %collective-permute-start.13) | collective-permute-done | bytes 159776 | tf_op jit(solution)/shard_map/ppermute | solution.py:126
  46.4 0.6 %fusion.22 = f32[1024,128]{1,0:T(8,128)S(1)} fusion(bf16[576,128]{1,0:T(8,128)(2,1)S(1)} %bitcast.193, bf16[3072,1024]{1,0:T(8,128)(2,1)S(1)} %exponential_convert_fusion), kind=kOutput, calls=%fused_computation.26 | convolution fusion | flops 150994944 | bytes 1851392 | tf_op jit(solution)/shard_map/dot_general | solution.py:152
  47.0 0.8 %fusion.8 = f32[1024,128]{1,0:T(8,128)S(1)} fusion(bf16[960,128]{1,0:T(8,128)(2,1)S(1)} %bitcast.188, bf16[3072,1024]{1,0:T(8,128)(2,1)S(1)} %exponential_convert_fusion), kind=kOutput, calls=%fused_computation.12 | convolution fusion | flops 251658240 | bytes 2736128 | tf_op jit(solution)/shard_map/dot_general | solution.py:152
  47.8 0.6 %fusion.13 = f32[1024,128]{1,0:T(8,128)S(1)} fusion(f32[1024,128]{1,0:T(8,128)S(1)} %fusion.8, f32[1024,128]{1,0:T(8,128)S(1)} %fusion.22, f32[1024,128]{1,0:T(8,128)S(1)} %fusion.108, f32[1024,128]{1,0:T(8,128)S(1)} %fusion.111, bf16[576,128]{1,0:T(8,128)(2,1)S(1)} %bitcast.184, bf16[3072,1024]{1,0:T(8,128)(2,1)S(1)} %exponential_convert_fusion), kind=kOutput, calls=%fused_computation.20 | convolution fusion | flops 151519232 | bytes 3948544 | tf_op jit(solution)/shard_map/dot_general | solution.py:152
  48.5 0.5 sqrt_bitcast_fusion
  49.0 0.6 %convolution_add_fusion = f32[1024,128]{1,0:T(8,128)S(1)} fusion(f32[1024,128]{1,0:T(8,128)S(1)} %fusion.13, bf16[576,128]{1,0:T(8,128)(2,1)S(1)} %bitcast.185, bf16[3072,1024]{1,0:T(8,128)(2,1)S(1)} %exponential_convert_fusion), kind=kOutput, calls=%fused_computation.16 | convolution fusion | flops 151126016 | bytes 2375680 | tf_op jit(solution)/shard_map/dot_general | solution.py:152
  49.6 0.8 %fusion.102 = f32[128,1024]{1,0:T(8,128)S(1)} fusion(f32[1024,1024]{1,0:T(8,128)S(1)} %copy-done, f32[1024,128]{1,0:T(8,128)S(1)} %convolution_add_fusion), kind=kOutput, calls=%fused_computation.107 | convolution fusion | flops 270794752 | bytes 5242880 | tf_op jit(solution)/shard_map/dot_general | solution.py:215
  50.4 0.8 %fusion.17 = f32[1024,128]{0,1:T(8,128)S(1)} fusion(f32[128,1024]{1,0:T(8,128)S(1)} %fusion.102, f32[1024,1024]{1,0:T(8,128)S(1)} %copy-done, f32[1024,128]{1,0:T(8,128)S(1)} %convolution_add_fusion), kind=kOutput, calls=%fused_computation.23 | convolution fusion | flops 271056896 | bytes 5767168 | tf_op jit(solution)/shard_map/dot_general | solution.py:216
  51.3 4.0 %fusion.78 = f32[192,128]{1,0:T(8,128)} fusion(f32[192,128]{1,0:T(8,128)S(1)} %copy-done.3, f32[192,128]{1,0:T(8,128)S(1)} %get-tuple-element.42, f32[1024,128]{0,1:T(8,128)S(1)} %fusion.17, f32[1024,1024]{1,0:T(8,128)} %param.13, bf16[3072,1024]{1,0:T(8,128)(2,1)} %copy-done.1, f32[1024,128]{1,0:T(8,128)S(1)} %convolution_add_fusion), kind=kOutput, calls=%fused_computation.85 | convolution fusion | flops 322510848 | bytes 5931008 | tf_op jit(solution)/shard_map/dot_general | solution.py:219
  (70 shorter events, 1.4 us)
Async XLA Ops:
  0.6 24.8 %copy-start.2 = (bf16[192,128]{1,0:T(8,128)(2,1)S(1)}, bf16[192,128]{1,0:T(8,128)(2,1)}, u32[]{:S(2)}) copy-start(bf16[192,128]{1,0:T(8,128)(2,1)} %param.9) | copy-start | bytes 147460
  2.4 17.3 %collective-permute-start.3 = (bf16[192,256]{1,0:T(8,128)(2,1)S(1)}, bf16[192,256]{1,0:T(8,128)(2,1)S(1)}, u32[]{:S(2)}, u32[]{:S(2)}) collective-permute-start(bf16[192,256]{1,0:T(8,128)(2,1)S(1)} %get-tuple-element.31), channel_id=1, source_target_pairs={{0,2},{1,3},{2,0},{3,1},{4,6},{5,7},{6,4},{7,5},{8,10},{9,11},{10,... | collective-permute-start | bytes 294920 | tf_op jit(solution)/shard_map/ppermute | solution.py:123
  5.4 9.3 %collective-permute-start.2 = (bf16[192,256]{1,0:T(8,128)(2,1)S(1)}, bf16[192,256]{1,0:T(8,128)(2,1)S(1)}, u32[]{:S(2)}, u32[]{:S(2)}) collective-permute-start(bf16[192,256]{1,0:T(8,128)(2,1)S(1)} %get-tuple-element.31), channel_id=1, source_target_pairs={{0,12},{4,0},{8,4},{12,8},{1,13},{5,1},{9,5},{13,9},{2,14},{6,2},{... | collective-permute-start | bytes 294920 | tf_op jit(solution)/shard_map/ppermute | solution.py:111
  9.0 8.3 %collective-permute-start.1 = (bf16[192,256]{1,0:T(8,128)(2,1)S(1)}, bf16[192,256]{1,0:T(8,128)(2,1)S(1)}, u32[]{:S(2)}, u32[]{:S(2)}) collective-permute-start(bf16[192,256]{1,0:T(8,128)(2,1)S(1)} %get-tuple-element.31), channel_id=1, source_target_pairs={{0,8},{4,12},{8,0},{12,4},{1,9},{5,13},{9,1},{13,5},{2,10},{6,14},... | collective-permute-start | bytes 294920 | tf_op jit(solution)/shard_map/ppermute | solution.py:111
  9.0 9.0 %collective-permute-start = (bf16[192,256]{1,0:T(8,128)(2,1)S(1)}, bf16[192,256]{1,0:T(8,128)(2,1)S(1)}, u32[]{:S(2)}, u32[]{:S(2)}) collective-permute-start(bf16[192,256]{1,0:T(8,128)(2,1)S(1)} %get-tuple-element.31), channel_id=1, source_target_pairs={{0,4},{4,8},{8,12},{12,0},{1,5},{5,9},{9,13},{13,1},{2,6},{6,10},{... | collective-permute-start | bytes 294920 | tf_op jit(solution)/shard_map/ppermute | solution.py:111
  14.7 13.5 %copy-start.3 = (f32[192,128]{1,0:T(8,128)S(1)}, f32[192,128]{1,0:T(8,128)}, u32[]{:S(2)}) copy-start(f32[192,128]{1,0:T(8,128)} %param.10) | copy-start | bytes 294916
  14.7 13.5 %copy-start.5 = (f32[192,128]{1,0:T(8,128)S(1)}, f32[192,128]{1,0:T(8,128)}, u32[]{:S(2)}) copy-start(f32[192,128]{1,0:T(8,128)} %param.11) | copy-start | bytes 294916
  14.7 9.9 %collective-permute-start.6 = (bf16[192,256]{1,0:T(8,128)(2,1)S(1)}, bf16[192,256]{1,0:T(8,128)(2,1)S(1)}, u32[]{:S(2)}, u32[]{:S(2)}) collective-permute-start(bf16[192,256]{1,0:T(8,128)(2,1)S(1)} %collective-permute-done.2), channel_id=1, source_target_pairs={{0,2},{1,3},{2,0},{3,1},{4,6},{5,7},{6,4},{7,5},{8,10},{9,11},{10,... | collective-permute-start | bytes 294920 | tf_op jit(solution)/shard_map/ppermute | solution.py:123
  17.4 7.2 %collective-permute-start.5 = (bf16[192,256]{1,0:T(8,128)(2,1)S(1)}, bf16[192,256]{1,0:T(8,128)(2,1)S(1)}, u32[]{:S(2)}, u32[]{:S(2)}) collective-permute-start(bf16[192,256]{1,0:T(8,128)(2,1)S(1)} %collective-permute-done.1), channel_id=1, source_target_pairs={{0,2},{1,3},{2,0},{3,1},{4,6},{5,7},{6,4},{7,5},{8,10},{9,11},{10,... | collective-permute-start | bytes 294920 | tf_op jit(solution)/shard_map/ppermute | solution.py:123
  18.0 6.5 %collective-permute-start.4 = (bf16[192,256]{1,0:T(8,128)(2,1)S(1)}, bf16[192,256]{1,0:T(8,128)(2,1)S(1)}, u32[]{:S(2)}, u32[]{:S(2)}) collective-permute-start(bf16[192,256]{1,0:T(8,128)(2,1)S(1)} %collective-permute-done), channel_id=1, source_target_pairs={{0,2},{1,3},{2,0},{3,1},{4,6},{5,7},{6,4},{7,5},{8,10},{9,11},{10,... | collective-permute-start | bytes 294920 | tf_op jit(solution)/shard_map/ppermute | solution.py:123
  24.6 2.5 %collective-permute-start.7 = (bf16[1344,256]{1,0:T(8,128)(2,1)S(1)}, bf16[1344,256]{1,0:T(8,128)(2,1)S(1)}, u32[]{:S(2)}, u32[]{:S(2)}) collective-permute-start(bf16[1344,256]{1,0:T(8,128)(2,1)S(1)} %constant_dynamic-update-slice_fusion), channel_id=1, source_target_pairs={{0,1},{1,0},{2,3},{3,2},{4,5},{5,4},{6,7},{7,6},{8,9},{9,8},{10,11... | collective-permute-start | bytes 2064392 | tf_op jit(solution)/shard_map/ppermute | solution.py:125
  24.8 2.1 %collective-permute-start.8 = (bf16[192,256]{1,0:T(8,128)(2,1)S(1)}, bf16[192,256]{1,0:T(8,128)(2,1)S(1)}, u32[]{:S(2)}, u32[]{:S(2)}) collective-permute-start(bf16[192,256]{1,0:T(8,128)(2,1)S(1)} %collective-permute-done.6), channel_id=1, source_target_pairs={{0,1},{1,0},{2,3},{3,2},{4,5},{5,4},{6,7},{7,6},{8,9},{9,8},{10,11... | collective-permute-start | bytes 294920 | tf_op jit(solution)/shard_map/ppermute | solution.py:126
  28.6 22.7 %copy-start.4 = (f32[192,128]{1,0:T(8,128)}, f32[192,128]{1,0:T(8,128)S(1)}, u32[]{:S(2)}) copy-start(f32[192,128]{1,0:T(8,128)S(1)} %get-tuple-element.42) | copy-start | bytes 294916
  28.7 12.2 %collective-permute-start.11 = (bf16[208,128]{1,0:T(8,128)(2,1)S(1)}, bf16[208,128]{1,0:T(8,128)(2,1)S(1)}, u32[]{:S(2)}, u32[]{:S(2)}) collective-permute-start(bf16[208,128]{1,0:T(8,128)(2,1)S(1)} %get-tuple-element.34), channel_id=1, source_target_pairs={{0,12},{4,0},{8,4},{12,8},{1,13},{5,1},{9,5},{13,9},{2,14},{6,2},{... | collective-permute-start | bytes 159752 | tf_op jit(solution)/shard_map/ppermute | solution.py:111
  30.8 10.1 %collective-permute-start.10 = (bf16[208,128]{1,0:T(8,128)(2,1)S(1)}, bf16[208,128]{1,0:T(8,128)(2,1)S(1)}, u32[]{:S(2)}, u32[]{:S(2)}) collective-permute-start(bf16[208,128]{1,0:T(8,128)(2,1)S(1)} %get-tuple-element.34), channel_id=1, source_target_pairs={{0,8},{4,12},{8,0},{12,4},{1,9},{5,13},{9,1},{13,5},{2,10},{6,14},... | collective-permute-start | bytes 159752 | tf_op jit(solution)/shard_map/ppermute | solution.py:111
  30.9 10.0 %collective-permute-start.9 = (bf16[208,128]{1,0:T(8,128)(2,1)S(1)}, bf16[208,128]{1,0:T(8,128)(2,1)S(1)}, u32[]{:S(2)}, u32[]{:S(2)}) collective-permute-start(bf16[208,128]{1,0:T(8,128)(2,1)S(1)} %get-tuple-element.34), channel_id=1, source_target_pairs={{0,4},{4,8},{8,12},{12,0},{1,5},{5,9},{9,13},{13,1},{2,6},{6,10},{... | collective-permute-start | bytes 159752 | tf_op jit(solution)/shard_map/ppermute | solution.py:111
  31.5 10.1 %collective-permute-start.12 = (bf16[208,128]{1,0:T(8,128)(2,1)S(1)}, bf16[208,128]{1,0:T(8,128)(2,1)S(1)}, u32[]{:S(2)}, u32[]{:S(2)}) collective-permute-start(bf16[208,128]{1,0:T(8,128)(2,1)S(1)} %get-tuple-element.34), channel_id=1, source_target_pairs={{0,2},{1,3},{2,0},{3,1},{4,6},{5,7},{6,4},{7,5},{8,10},{9,11},{10,... | collective-permute-start | bytes 159752 | tf_op jit(solution)/shard_map/ppermute | solution.py:125
  40.5 8.5 %copy-start.1 = (bf16[3072,1024]{1,0:T(8,128)(2,1)}, bf16[3072,1024]{1,0:T(8,128)(2,1)S(1)}, u32[]{:S(2)}) copy-start(bf16[3072,1024]{1,0:T(8,128)(2,1)S(1)} %exponential_convert_fusion) | copy-start | bytes 18874372
  41.0 5.3 %collective-permute-start.13 = (bf16[624,128]{1,0:T(8,128)(2,1)S(1)}, bf16[624,128]{1,0:T(8,128)(2,1)S(1)}, u32[]{:S(2)}, u32[]{:S(2)}) collective-permute-start(bf16[624,128]{1,0:T(8,128)(2,1)S(1)} %get-tuple-element.35), channel_id=1, source_target_pairs={{0,2},{1,3},{2,0},{3,1},{4,6},{5,7},{6,4},{7,5},{8,10},{9,11},{10,... | collective-permute-start | bytes 479240 | tf_op jit(solution)/shard_map/ppermute | solution.py:126
  42.0 5.0 %collective-permute-start.14 = (bf16[1040,128]{1,0:T(8,128)(2,1)S(1)}, bf16[1040,128]{1,0:T(8,128)(2,1)S(1)}, u32[]{:S(2)}, u32[]{:S(2)}) collective-permute-start(bf16[1040,128]{1,0:T(8,128)(2,1)S(1)} %constant_dynamic-update-slice_fusion.19), channel_id=1, source_target_pairs={{0,1},{1,0},{2,3},{3,2},{4,5},{5,4},{6,7},{7,6},{8,9},{9,8},{10,11... | collective-permute-start | bytes 798728 | tf_op jit(solution)/shard_map/ppermute | solution.py:125
  46.3 2.1 %collective-permute-start.15 = (bf16[624,128]{1,0:T(8,128)(2,1)S(1)}, bf16[624,128]{1,0:T(8,128)(2,1)S(1)}, u32[]{:S(2)}, u32[]{:S(2)}) collective-permute-start(bf16[624,128]{1,0:T(8,128)(2,1)S(1)} %collective-permute-done.13), channel_id=1, source_target_pairs={{0,1},{1,0},{2,3},{3,2},{4,5},{5,4},{6,7},{7,6},{8,9},{9,8},{10,11... | collective-permute-start | bytes 479240 | tf_op jit(solution)/shard_map/ppermute | solution.py:126
  47.0 2.6 %copy-start = (f32[1024,1024]{1,0:T(8,128)S(1)}, f32[1024,1024]{1,0:T(8,128)}, u32[]{:S(2)}) copy-start(f32[1024,1024]{1,0:T(8,128)} %param.13) | copy-start | bytes 12582916

commit v4 on v2

--- a/solution.py
+++ b/solution.py
@@ -209,11 +209,13 @@
     projected = projected_all(all_x, all_sq, centers, centers_sq, residual_parts, gamma)
     w_hi, w_lo = split_bf16(woodbury_inverse)
     p_hi, p_lo = split_bf16(projected)
-    weights = (
-        jnp.dot(w_hi, p_hi, preferred_element_type=jnp.float32)
-        + jnp.dot(w_hi, p_lo, preferred_element_type=jnp.float32)
-        + jnp.dot(w_lo, p_hi, preferred_element_type=jnp.float32)
-    )
+    w_both = jnp.concatenate([w_hi, w_lo], axis=1)
+    p_both = jnp.concatenate(
+        [jnp.concatenate([p_hi, p_lo], axis=1), jnp.concatenate([p_hi, jnp.zeros_like(p_lo)], axis=1)], axis=0
+    )
+    both = jnp.dot(w_both, p_both, preferred_element_type=jnp.float32)
+    r = p_hi.shape[1]
+    weights = both[:, :r] + both[:, r:]
     correction = jnp.dot(cross, weights.astype(jnp.bfloat16), preferred_element_type=jnp.float32)
     new_solution = solution + (residual - correction) / noise_level
     relative_norm = jnp.sqrt(res_sq / (tar_sq + 1e-06))

time: 54 us -> 75.3 us (1.39)
  other arithmetic: 6.97 us -> 14.5 us
  local copies, waits for them, and re-layouts: 4.37 us -> 11.6 us
  matrix products: 18 us -> 23.7 us
  starting transfers between devices: 16 us -> 17.9 us
  waiting for transfers between devices: 6.8 us -> 5.57 us
    unnamed x27 -> x31, local copies, waits for them, and re-layouts: 1.05 us -> 6.8 us
    dot_general x10, matrix products: 7.74 us -> 12.5 us  [piece(): return jnp.dot(k, v, preferred_element_type=jnp.float32)]
    convert_element_type x1 -> x2, other arithmetic: 0.01 us -> 4.49 us  [split_bf16(): return (hi.astype(jnp.bfloat16), lo.astype(jnp.bfloat16))]
    ppermute x6, starting transfers between devices: 7.41 us -> 10.9 us  [gather_blocks(): lax.ppermute(block, 'rows', [(i, (i + k) % n_rows) for i in range(n_rows)])]
    ppermute x6, waiting for transfers between devices: 1.92 us -> 0.02 us  [gather_blocks(): lax.ppermute(block, 'rows', [(i, (i + k) % n_rows) for i in range(n_rows)])]
    reduce_sum x12, other arithmetic: 2.93 us -> 4.71 us  [square_norms(): return jnp.sum(jnp.square(values.astype(jnp.float32)), axis=1)]
    ppermute x4, starting transfers between devices: 5.72 us -> 4.25 us  [pipelined_xor_gather(): parts = parts + [lax.ppermute(p, axis, perm) for p in parts]]
    dot_general x1, matrix products: 1.2 us -> 2.42 us  [local(): jnp.dot(cross, weights.astype(jnp.bfloat16), preferred_element_type=jnp.f...]
  transfers between devices with their start and end apart: 16 -> 16, of which waited for: 3 -> 1; matrix products, arithmetic and copies ran while one was open for 40% -> 49% of each run, Pallas kernels for 0% -> 0%
where the time goes in v4:
time: 75.3 us; the launch traced here: 74.3 us
  matrix products  23.7 us (31%)
  starting transfers between devices  17.9 us (24%)
  other arithmetic  14.5 us (19%)
  local copies, waits for them, and re-layouts  11.6 us (15%)
  waiting for transfers between devices  5.57 us (7%)
  between operations  1.07 us (1%)
    dot_general x10, matrix products, piece(): return jnp.dot(k, v, preferred_element_type=jnp.float32)  12.5 us
    ppermute x6, starting transfers between devices, gather_blocks(): lax.ppermute(block, 'rows', [(i, (i + k) % n_rows) for i in range(n_rows)])  10.9 us
    unnamed x31, local copies, waits for them, and re-layouts  6.8 us
    ppermute x3, waiting for transfers between devices, pipelined_xor_gather(): newest = lax.ppermute(parts[-1], axis, perm)  5.53 us
    reduce_sum x12, other arithmetic, square_norms(): return jnp.sum(jnp.square(values.astype(jnp.float32)), axis=1)  4.71 us
    convert_element_type x2, other arithmetic, split_bf16(): return (hi.astype(jnp.bfloat16), lo.astype(jnp.bfloat16))  4.49 us
    ppermute x4, starting transfers between devices, pipelined_xor_gather(): parts = parts + [lax.ppermute(p, axis, perm) for p in parts]  4.25 us
    dot_general x1, matrix products, rbf_tile(): lax.dot_general(left_x, right_x, (((1,), (1,)), ((), ())), preferred_elem...  3.36 us
  transfers between devices with their start and end apart: 16, of which 1 were waited for; matrix products, arithmetic and copies ran while one was open for 49% of the time, Pallas kernels for 0%

profile of v4, /device:TPU:0, one launch (start us, length us, event | category | flops | bytes accessed | tf_op | source)
XLA Modules:
  0.0 74.3 jit_solution(7076180207251115496)
XLA Ops:
  0.6 0.9 %convert_element_type.138 = bf16[192,128]{1,0:T(8,128)(2,1)S(1)} convert(f32[192,128]{1,0:T(8,128)} %param.10) | non-fusion elementwise | flops 24576 | bytes 147456 | tf_op jit(solution)/shard_map/convert_element_type | solution.py:176
  1.5 1.5 %pad_maximum_fusion = (bf16[192,256]{1,0:T(8,128)(2,1)}, bf16[1344,256]{1,0:T(8,128)(2,1)}) fusion(bf16[192,128]{1,0:T(8,128)(2,1)S(1)} %convert_element_type.138, bf16[192,128]{1,0:T(8,128)(2,1)} %param.9), kind=kLoop, calls=%fused_computation.154 | loop fusion | flops 196607 | bytes 294912 | tf_op jit(solution)/shard_map/concatenate | solution.py:177
  3.0 3.1 %collective-permute-start = (bf16[192,256]{1,0:T(8,128)(2,1)}, bf16[192,256]{1,0:T(8,128)(2,1)S(1)}, u32[]{:S(2)}, u32[]{:S(2)}) collective-permute-start(bf16[192,256]{1,0:T(8,128)(2,1)} %get-tuple-element.35), channel_id=1, source_target_pairs={{0,4},{4,8},{8,12},{12,0},{1,5},{5,9},{9,13},{13,1},{2,6},{6,10},{... | collective-permute-start | bytes 294920 | tf_op jit(solution)/shard_map/ppermute | solution.py:111
  6.1 2.6 %collective-permute-start.1 = (bf16[192,256]{1,0:T(8,128)(2,1)}, bf16[192,256]{1,0:T(8,128)(2,1)S(1)}, u32[]{:S(2)}, u32[]{:S(2)}) collective-permute-start(bf16[192,256]{1,0:T(8,128)(2,1)} %get-tuple-element.35), channel_id=1, source_target_pairs={{0,8},{4,12},{8,0},{12,4},{1,9},{5,13},{9,1},{13,5},{2,10},{6,14},... | collective-permute-start | bytes 294920 | tf_op jit(solution)/shard_map/ppermute | solution.py:111
  8.7 1.3 %collective-permute-start.2 = (bf16[192,256]{1,0:T(8,128)(2,1)}, bf16[192,256]{1,0:T(8,128)(2,1)S(1)}, u32[]{:S(2)}, u32[]{:S(2)}) collective-permute-start(bf16[192,256]{1,0:T(8,128)(2,1)} %get-tuple-element.35), channel_id=1, source_target_pairs={{0,12},{4,0},{8,4},{12,8},{1,13},{5,1},{9,5},{13,9},{2,14},{6,2},{... | collective-permute-start | bytes 294920 | tf_op jit(solution)/shard_map/ppermute | solution.py:111
  10.0 1.5 %collective-permute-start.3 = (bf16[192,256]{1,0:T(8,128)(2,1)}, bf16[192,256]{1,0:T(8,128)(2,1)S(1)}, u32[]{:S(2)}, u32[]{:S(2)}) collective-permute-start(bf16[192,256]{1,0:T(8,128)(2,1)} %get-tuple-element.35), channel_id=1, source_target_pairs={{0,2},{1,3},{2,0},{3,1},{4,6},{5,7},{6,4},{7,5},{8,10},{9,11},{10,... | collective-permute-start | bytes 294920 | tf_op jit(solution)/shard_map/ppermute | solution.py:123
  11.5 0.9 %multiply_reduce_fusion.13 = f32[192]{0:T(256)S(1)} fusion(bf16[192,128]{1,0:T(8,128)(2,1)} %param.9), kind=kLoop, calls=%fused_computation.201 | loop fusion | flops 73536 | bytes 49920 | tf_op jit(solution)/shard_map/reduce_sum | solution.py:15
  12.4 1.9 %fusion.90 = f32[192,128]{1,0:T(8,128)} fusion(bf16[192,128]{1,0:T(8,128)(2,1)S(1)} %convert_element_type.138, bf16[192,128]{1,0:T(8,128)(2,1)} %param.9, f32[192]{0:T(256)S(1)} %multiply_reduce_fusion.13), kind=kOutput, calls=%fused_computation.109 | convolution fusion | flops 19058688 | bytes 197376 | tf_op jit(solution)/shard_map/dot_general | solution.py:39
  14.4 0.9 %multiply_reduce_fusion.3 = f32[128]{0:T(128)S(1)} fusion(f32[192,128]{1,0:T(8,128)} %param.11), kind=kLoop, calls=%fused_computation.157 | loop fusion | flops 49024 | bytes 98816 | tf_op jit(solution)/shard_map/reduce_sum | solution.py:195
  15.3 0.7 compare_and_fusion
  16.0 4.5 %reduce-precision_convert_fusion = (bf16[1024,1024]{1,0:T(8,128)(2,1)S(1)}, bf16[1024,1024]{1,0:T(8,128)(2,1)}) fusion(f32[1024,1024]{1,0:T(8,128)} %param.13), kind=kLoop, calls=%fused_computation.3 | loop fusion | flops 4194304 | bytes 8388608 | tf_op jit(solution)/shard_map/convert_element_type | solution.py:54
  20.5 0.6 collective-permute-start.4
  21.3 1.6 %collective-permute-start.5 = (bf16[192,256]{1,0:T(8,128)(2,1)S(1)}, bf16[192,256]{1,0:T(8,128)(2,1)S(1)}, u32[]{:S(2)}, u32[]{:S(2)}) collective-permute-start(bf16[192,256]{1,0:T(8,128)(2,1)S(1)} %collective-permute-done.1), channel_id=1, source_target_pairs={{0,2},{1,3},{2,0},{3,1},{4,6},{5,7},{6,4},{7,5},{8,10},{9,11},{10,... | collective-permute-start | bytes 294920 | tf_op jit(solution)/shard_map/ppermute | solution.py:123
  23.1 0.6 collective-permute-start.6
  23.7 0.6 constant_dynamic-update-slice_fusion.5
  24.3 0.6 constant_dynamic-update-slice_fusion.4
  24.9 1.0 %fusion.83 = f32[192,128]{1,0:T(8,128)} fusion(bf16[192,128]{1,0:T(8,128)(2,1)S(1)} %copy-done.1, f32[192]{0:T(256)S(1)} %multiply_reduce_fusion.10, f32[192]{0:T(256)S(1)} %multiply_reduce_fusion.13, bf16[192,256]{1,0:T(8,128)(2,1)S(1)} %collective-permute-done.2), kind=kOutput, calls=%fused_computation.102 | convolution fusion | flops 19058688 | bytes 247296 | tf_op jit(solution)/shard_map/dot_general | solution.py:39
  25.9 0.6 constant_dynamic-update-slice_fusion.3
  26.7 1.0 %fusion.82 = f32[192,128]{1,0:T(8,128)} fusion(bf16[192,128]{1,0:T(8,128)(2,1)S(1)} %copy-done.1, f32[192]{0:T(256)S(1)} %multiply_reduce_fusion.9, f32[192]{0:T(256)S(1)} %multiply_reduce_fusion.13, bf16[192,256]{1,0:T(8,128)(2,1)S(1)} %collective-permute-done.3), kind=kOutput, calls=%fused_computation.101 | convolution fusion | flops 19058688 | bytes 247296 | tf_op jit(solution)/shard_map/dot_general | solution.py:39
  27.7 1.9 %fusion.89 = f32[192,128]{1,0:T(8,128)} fusion(f32[192,128]{1,0:T(8,128)} %fusion.90, bf16[192,128]{1,0:T(8,128)(2,1)S(1)} %copy-done.1, f32[192]{0:T(256)S(1)} %multiply_reduce_fusion.12, f32[192]{0:T(256)S(1)} %multiply_reduce_fusion.13, bf16[192,256]{1,0:T(8,128)(2,1)S(1)} %collective-permute-done), kind=kOutput, calls=%fused_computation.108 | convolution fusion | flops 19083264 | bytes 345600 | tf_op jit(solution)/shard_map/dot_general | solution.py:39
  29.6 2.0 %fusion.87 = f32[192,128]{1,0:T(8,128)} fusion(f32[192,128]{1,0:T(8,128)} %fusion.82, f32[192,128]{1,0:T(8,128)} %fusion.83, f32[192,128]{1,0:T(8,128)} %fusion.89, bf16[192,128]{1,0:T(8,128)(2,1)S(1)} %copy-done.1, f32[192]{0:T(256)S(1)} %multiply_reduce_fusion.11, f32[192]{0:T(256)S(1)} %multiply_reduce_fusion.13, ...), kind=kOutput, calls=%fused_computation.106 | convolution fusion | flops 19132416 | bytes 542208 | tf_op jit(solution)/shard_map/dot_general | solution.py:39
  31.6 0.6 constant_dynamic-update-slice_fusion.2
  32.2 0.6 constant_dynamic-update-slice_fusion.1
  32.9 0.6 constant_dynamic-update-slice_fusion
  33.6 0.9 %multiply_reduce_fusion.6 = f32[192]{0:T(256)S(1)} fusion(bf16[192,256]{1,0:T(8,128)(2,1)} %collective-permute-done.6), kind=kLoop, calls=%fused_computation.162 | loop fusion | flops 73536 | bytes 49920 | tf_op jit(solution)/shard_map/reduce_sum | solution.py:15
  34.6 0.6 collective-permute-start.8
  35.1 1.2 %fusion.75 = f32[192,128]{1,0:T(8,128)S(1)} fusion(bf16[192,128]{1,0:T(8,128)(2,1)S(1)} %copy-done.1, f32[192]{0:T(256)S(1)} %multiply_reduce_fusion.6, f32[192]{0:T(256)S(1)} %multiply_reduce_fusion.13, bf16[192,256]{1,0:T(8,128)(2,1)} %collective-permute-done.6), kind=kOutput, calls=%fused_computation.94 | convolution fusion | flops 19058688 | bytes 247296 | tf_op jit(solution)/shard_map/dot_general | solution.py:39
  36.3 0.8 %constant_dynamic-update-slice_fusion.8 = bf16[3072,128]{1,0:T(8,128)(2,1)S(1)} fusion(bf16[3072,128]{1,0:T(8,128)(2,1)S(1)} %constant_dynamic-update-slice_fusion.9, bf16[192,256]{1,0:T(8,128)(2,1)} %collective-permute-done.6), kind=kLoop, calls=%fused_computation.211 | loop fusion | bytes 98304
  37.7 1.3 %multiply_reduce_fusion.1 = f32[1344]{0:T(1024)S(1)} fusion(bf16[1344,256]{1,0:T(8,128)(2,1)} %collective-permute-done.7), kind=kLoop, calls=%fused_computation.123 | loop fusion | flops 514752 | bytes 349440 | tf_op jit(solution)/shard_map/reduce_sum | solution.py:15
  39.0 1.6 %fusion.18 = f32[192,128]{1,0:T(8,128)S(1)} fusion(bf16[192,128]{1,0:T(8,128)(2,1)S(1)} %copy-done.1, f32[1344]{0:T(1024)S(1)} %multiply_reduce_fusion.1, f32[192]{0:T(256)S(1)} %multiply_reduce_fusion.13, bf16[1344,256]{1,0:T(8,128)(2,1)} %collective-permute-done.7), kind=kOutput, calls=%fused_computation.26 | convolution fusion | flops 133410816 | bytes 841728 | tf_op jit(solution)/shard_map/dot_general | solution.py:39
  41.0 1.4 %multiply_reduce_fusion.4 = (f32[128]{0:T(128)S(1)}, f32[192,128]{1,0:T(8,128)S(1)}) fusion(f32[192,128]{1,0:T(8,128)} %param.10, f32[192,128]{1,0:T(8,128)} %param.11, f32[192,128]{1,0:T(8,128)S(1)} %fusion.81, bf16[192,256]{1,0:T(8,128)(2,1)} %copy-done.5, bf16[192,128]{1,0:T(8,128)(2,1)S(1)} %copy-done.1, f32[192]{0:T(256)S(1)} %multiply_reduce_fusion.5, ...), kind=kOutput, calls=%fused_computation.158 | convolution fusion | flops 19206016 | bytes 542720 | tf_op jit(solution)/shard_map/dot_general | solution.py:39
  42.4 0.6 constant_dynamic-update-slice_fusion.24
  43.0 0.7 collective-permute-start.9
  44.1 2.8 %collective-permute-start.11 = (bf16[208,128]{1,0:T(8,128)(2,1)S(1)}, bf16[208,128]{1,0:T(8,128)(2,1)S(1)}, u32[]{:S(2)}, u32[]{:S(2)}) collective-permute-start(bf16[208,128]{1,0:T(8,128)(2,1)S(1)} %get-tuple-element.38), channel_id=1, source_target_pairs={{0,12},{4,0},{8,4},{12,8},{1,13},{5,1},{9,5},{13,9},{2,14},{6,2},{... | collective-permute-start | bytes 159752 | tf_op jit(solution)/shard_map/ppermute | solution.py:111
  46.9 1.5 %collective-permute-start.12 = (bf16[208,128]{1,0:T(8,128)(2,1)S(1)}, bf16[208,128]{1,0:T(8,128)(2,1)S(1)}, u32[]{:S(2)}, u32[]{:S(2)}) collective-permute-start(bf16[208,128]{1,0:T(8,128)(2,1)S(1)} %get-tuple-element.38), channel_id=1, source_target_pairs={{0,2},{1,3},{2,0},{3,1},{4,6},{5,7},{6,4},{7,5},{8,10},{9,11},{10,... | collective-permute-start | bytes 159752 | tf_op jit(solution)/shard_map/ppermute | solution.py:125
  48.4 1.0 %slice_dynamic-update-slice_fusion = bf16[3072,128]{1,0:T(8,128)(2,1)S(1)} fusion(bf16[3072,128]{1,0:T(8,128)(2,1)S(1)} %constant_dynamic-update-slice_fusion.8, bf16[1344,256]{1,0:T(8,128)(2,1)} %collective-permute-done.7), kind=kLoop, calls=%fused_computation.142 | loop fusion | bytes 688128
  49.4 0.8 %constant_dynamic-update-slice_fusion.7 = bf16[3072,128]{1,0:T(8,128)(2,1)S(1)} fusion(bf16[3072,128]{1,0:T(8,128)(2,1)S(1)} %slice_dynamic-update-slice_fusion, bf16[192,256]{1,0:T(8,128)(2,1)} %copy-done.5), kind=kLoop, calls=%fused_computation.210 | loop fusion | bytes 98304 | tf_op jit(solution)/shard_map/concatenate | solution.py:186
  50.7 3.2 %gather_fusion = bf16[1024,128]{1,0:T(8,128)(2,1)S(1)} fusion(bf16[3072,128]{1,0:T(8,128)(2,1)S(1)} %constant_dynamic-update-slice_fusion.7, s32[1024]{0:T(1024)S(1)} %broadcast_clamp_fusion), kind=kCustom, calls=%fused_computation | custom fusion | bytes 528384 | tf_op jit(solution)/shard_map/jit(_take)/gather | solution.py:190
  54.3 3.4 %exponential_convert_fusion = bf16[3072,1024]{1,0:T(8,128)(2,1)S(1)} fusion(bf16[3072,128]{1,0:T(8,128)(2,1)S(1)} %constant_dynamic-update-slice_fusion.7, f32[1024]{0:T(1024)S(1)} %multiply_reduce_fusion.2, f32[3072]{0:T(1024)S(1)} %multiply_reduce_fusion, bf16[1024,128]{1,0:T(8,128)(2,1)S(1)} %gather_fusion, pred[1024]{0:T(1024)(128)(4,1)S(1)} %get-tuple-element.29), kind=kOutput, calls=%fused_computation.1 | convolution fusion | flops 821166080 | bytes 7357440 | tf_op jit(solution)/shard_map/dot_general | solution.py:19
  58.1 0.8 %constant_dynamic-update-slice_fusion.18 = (bf16[624,128]{1,0:T(8,128)(2,1)S(1)}, bf16[1040,128]{1,0:T(8,128)(2,1)S(1)}) fusion(bf16[208,128]{1,0:T(8,128)(2,1)} %collective-permute-done.9, bf16[1040,128]{1,0:T(8,128)(2,1)S(1)} %constant_dynamic-update-slice_fusion.23), kind=kLoop, calls=%fused_computation.221 | loop fusion | bytes 159744
  58.9 0.8 %constant_dynamic-update-slice_fusion.17 = (bf16[624,128]{1,0:T(8,128)(2,1)S(1)}, bf16[1040,128]{1,0:T(8,128)(2,1)S(1)}) fusion(bf16[624,128]{1,0:T(8,128)(2,1)S(1)} %get-tuple-element.43, bf16[208,128]{1,0:T(8,128)(2,1)} %collective-permute-done.10, bf16[1040,128]{1,0:T(8,128)(2,1)S(1)} %get-tuple-element.44), kind=kLoop, calls=%fused_computation.220 | loop fusion | bytes 159744
  59.9 0.6 collective-permute-start.13
  60.9 5.5 %collective-permute-done.13 = bf16[624,128]{1,0:T(8,128)(2,1)S(1)} collective-permute-done((bf16[624,128]{1,0:T(8,128)(2,1)S(1)}, bf16[624,128]{1,0:T(8,128)(2,1)S(1)}, u32[]{:S(2)}, u32[]{:S(2)}) %collective-permute-start.13) | collective-permute-done | bytes 159776 | tf_op jit(solution)/shard_map/ppermute | solution.py:126
  66.5 0.6 fusion.24
  67.1 0.8 %fusion.11 = f32[1024,128]{1,0:T(8,128)S(1)} fusion(bf16[960,128]{1,0:T(8,128)(2,1)S(1)} %bitcast.204, bf16[3072,1024]{1,0:T(8,128)(2,1)S(1)} %exponential_convert_fusion), kind=kOutput, calls=%fused_computation.17 | convolution fusion | flops 251658240 | bytes 2736128 | tf_op jit(solution)/shard_map/dot_general | solution.py:152
  69.1 0.6 fusion.107
  69.7 2.2 %fusion.1 = f32[1024,256]{1,0:T(8,128)} fusion(bf16[1024,1024]{1,0:T(8,128)(2,1)S(1)} %copy-done, bf16[1024,1024]{1,0:T(8,128)(2,1)S(1)} %get-tuple-element.31, bf16[1024,128]{1,0:T(8,128)(2,1)S(1)} %get-tuple-element.34, bf16[1024,128]{1,0:T(8,128)(2,1)S(1)} %get-tuple-element.33), kind=kOutput, calls=%fused_computation.5 | convolution fusion | flops 1086324736 | bytes 5767168 | tf_op jit(solution)/shard_map/dot_general | solution.py:216
  71.9 2.4 %fusion.93 = f32[192,128]{1,0:T(8,128)} fusion(f32[192,128]{1,0:T(8,128)S(1)} %copy-done.3, f32[192,128]{1,0:T(8,128)S(1)} %get-tuple-element.46, bf16[192,128]{1,0:T(8,128)(2,1)S(1)} %copy-done.1, f32[1024]{0:T(1024)S(1)} %multiply_reduce_fusion.2, f32[192]{0:T(256)S(1)} %multiply_reduce_fusion.13, f32[1024,256]{1,0:T(8,128)} %fusion.1, ...), kind=kOutput, calls=%fused_computation.112 | convolution fusion | flops 102113280 | bytes 1660672 | tf_op jit(solution)/shard_map/dot_general | solution.py:219
  (72 shorter events, 4.9 us)
Async XLA Ops:
  3.0 17.5 %collective-permute-start = (bf16[192,256]{1,0:T(8,128)(2,1)}, bf16[192,256]{1,0:T(8,128)(2,1)S(1)}, u32[]{:S(2)}, u32[]{:S(2)}) collective-permute-start(bf16[192,256]{1,0:T(8,128)(2,1)} %get-tuple-element.35), channel_id=1, source_target_pairs={{0,4},{4,8},{8,12},{12,0},{1,5},{5,9},{9,13},{13,1},{2,6},{6,10},{... | collective-permute-start | bytes 294920 | tf_op jit(solution)/shard_map/ppermute | solution.py:111
  6.1 15.2 %collective-permute-start.1 = (bf16[192,256]{1,0:T(8,128)(2,1)}, bf16[192,256]{1,0:T(8,128)(2,1)S(1)}, u32[]{:S(2)}, u32[]{:S(2)}) collective-permute-start(bf16[192,256]{1,0:T(8,128)(2,1)} %get-tuple-element.35), channel_id=1, source_target_pairs={{0,8},{4,12},{8,0},{12,4},{1,9},{5,13},{9,1},{13,5},{2,10},{6,14},... | collective-permute-start | bytes 294920 | tf_op jit(solution)/shard_map/ppermute | solution.py:111
  8.7 14.3 %collective-permute-start.2 = (bf16[192,256]{1,0:T(8,128)(2,1)}, bf16[192,256]{1,0:T(8,128)(2,1)S(1)}, u32[]{:S(2)}, u32[]{:S(2)}) collective-permute-start(bf16[192,256]{1,0:T(8,128)(2,1)} %get-tuple-element.35), channel_id=1, source_target_pairs={{0,12},{4,0},{8,4},{12,8},{1,13},{5,1},{9,5},{13,9},{2,14},{6,2},{... | collective-permute-start | bytes 294920 | tf_op jit(solution)/shard_map/ppermute | solution.py:111
  10.0 16.6 %collective-permute-start.3 = (bf16[192,256]{1,0:T(8,128)(2,1)}, bf16[192,256]{1,0:T(8,128)(2,1)S(1)}, u32[]{:S(2)}, u32[]{:S(2)}) collective-permute-start(bf16[192,256]{1,0:T(8,128)(2,1)} %get-tuple-element.35), channel_id=1, source_target_pairs={{0,2},{1,3},{2,0},{3,1},{4,6},{5,7},{6,4},{7,5},{8,10},{9,11},{10,... | collective-permute-start | bytes 294920 | tf_op jit(solution)/shard_map/ppermute | solution.py:123
  16.0 4.5 %copy-start.1 = (bf16[192,128]{1,0:T(8,128)(2,1)S(1)}, bf16[192,128]{1,0:T(8,128)(2,1)}, u32[]{:S(2)}) copy-start(bf16[192,128]{1,0:T(8,128)(2,1)} %param.9) | copy-start | bytes 147460
  20.5 11.7 %collective-permute-start.4 = (bf16[192,256]{1,0:T(8,128)(2,1)S(1)}, bf16[192,256]{1,0:T(8,128)(2,1)S(1)}, u32[]{:S(2)}, u32[]{:S(2)}) collective-permute-start(bf16[192,256]{1,0:T(8,128)(2,1)S(1)} %collective-permute-done), channel_id=1, source_target_pairs={{0,2},{1,3},{2,0},{3,1},{4,6},{5,7},{6,4},{7,5},{8,10},{9,11},{10,... | collective-permute-start | bytes 294920 | tf_op jit(solution)/shard_map/ppermute | solution.py:123
  21.3 11.6 %collective-permute-start.5 = (bf16[192,256]{1,0:T(8,128)(2,1)S(1)}, bf16[192,256]{1,0:T(8,128)(2,1)S(1)}, u32[]{:S(2)}, u32[]{:S(2)}) collective-permute-start(bf16[192,256]{1,0:T(8,128)(2,1)S(1)} %collective-permute-done.1), channel_id=1, source_target_pairs={{0,2},{1,3},{2,0},{3,1},{4,6},{5,7},{6,4},{7,5},{8,10},{9,11},{10,... | collective-permute-start | bytes 294920 | tf_op jit(solution)/shard_map/ppermute | solution.py:123
  23.1 10.6 %collective-permute-start.6 = (bf16[192,256]{1,0:T(8,128)(2,1)S(1)}, bf16[192,256]{1,0:T(8,128)(2,1)}, u32[]{:S(2)}, u32[]{:S(2)}) collective-permute-start(bf16[192,256]{1,0:T(8,128)(2,1)S(1)} %collective-permute-done.2), channel_id=1, source_target_pairs={{0,2},{1,3},{2,0},{3,1},{4,6},{5,7},{6,4},{7,5},{8,10},{9,11},{10,... | collective-permute-start | bytes 294920 | tf_op jit(solution)/shard_map/ppermute | solution.py:123
  32.2 8.4 %copy-start.2 = (f32[192,128]{1,0:T(8,128)S(1)}, f32[192,128]{1,0:T(8,128)}, u32[]{:S(2)}) copy-start(f32[192,128]{1,0:T(8,128)} %fusion.87) | copy-start | bytes 294916
  33.5 4.2 %collective-permute-start.7 = (bf16[1344,256]{1,0:T(8,128)(2,1)}, bf16[1344,256]{1,0:T(8,128)(2,1)}, u32[]{:S(2)}, u32[]{:S(2)}) collective-permute-start(bf16[1344,256]{1,0:T(8,128)(2,1)} %constant_dynamic-update-slice_fusion), channel_id=1, source_target_pairs={{0,1},{1,0},{2,3},{3,2},{4,5},{5,4},{6,7},{7,6},{8,9},{9,8},{10,11... | collective-permute-start | bytes 2064392 | tf_op jit(solution)/shard_map/ppermute | solution.py:125
  34.6 3.0 %collective-permute-start.8 = (bf16[192,256]{1,0:T(8,128)(2,1)}, bf16[192,256]{1,0:T(8,128)(2,1)S(1)}, u32[]{:S(2)}, u32[]{:S(2)}) collective-permute-start(bf16[192,256]{1,0:T(8,128)(2,1)} %collective-permute-done.6), channel_id=1, source_target_pairs={{0,1},{1,0},{2,3},{3,2},{4,5},{5,4},{6,7},{7,6},{8,9},{9,8},{10,11... | collective-permute-start | bytes 294920 | tf_op jit(solution)/shard_map/ppermute | solution.py:126
  37.6 1.4 %copy-start.5 = (bf16[192,256]{1,0:T(8,128)(2,1)}, bf16[192,256]{1,0:T(8,128)(2,1)S(1)}, u32[]{:S(2)}) copy-start(bf16[192,256]{1,0:T(8,128)(2,1)S(1)} %collective-permute-done.8) | copy-start | bytes 294916
  42.3 29.6 %copy-start.4 = (f32[192,128]{1,0:T(8,128)}, f32[192,128]{1,0:T(8,128)S(1)}, u32[]{:S(2)}) copy-start(f32[192,128]{1,0:T(8,128)S(1)} %get-tuple-element.46) | copy-start | bytes 294916
  43.0 15.0 %collective-permute-start.9 = (bf16[208,128]{1,0:T(8,128)(2,1)S(1)}, bf16[208,128]{1,0:T(8,128)(2,1)}, u32[]{:S(2)}, u32[]{:S(2)}) collective-permute-start(bf16[208,128]{1,0:T(8,128)(2,1)S(1)} %get-tuple-element.38), channel_id=1, source_target_pairs={{0,4},{4,8},{8,12},{12,0},{1,5},{5,9},{9,13},{13,1},{2,6},{6,10},{... | collective-permute-start | bytes 159752 | tf_op jit(solution)/shard_map/ppermute | solution.py:111
  43.8 15.1 %collective-permute-start.10 = (bf16[208,128]{1,0:T(8,128)(2,1)S(1)}, bf16[208,128]{1,0:T(8,128)(2,1)}, u32[]{:S(2)}, u32[]{:S(2)}) collective-permute-start(bf16[208,128]{1,0:T(8,128)(2,1)S(1)} %get-tuple-element.38), channel_id=1, source_target_pairs={{0,8},{4,12},{8,0},{12,4},{1,9},{5,13},{9,1},{13,5},{2,10},{6,14},... | collective-permute-start | bytes 159752 | tf_op jit(solution)/shard_map/ppermute | solution.py:111
  44.1 15.7 %collective-permute-start.11 = (bf16[208,128]{1,0:T(8,128)(2,1)S(1)}, bf16[208,128]{1,0:T(8,128)(2,1)S(1)}, u32[]{:S(2)}, u32[]{:S(2)}) collective-permute-start(bf16[208,128]{1,0:T(8,128)(2,1)S(1)} %get-tuple-element.38), channel_id=1, source_target_pairs={{0,12},{4,0},{8,4},{12,8},{1,13},{5,1},{9,5},{13,9},{2,14},{6,2},{... | collective-permute-start | bytes 159752 | tf_op jit(solution)/shard_map/ppermute | solution.py:111
  46.9 12.9 %collective-permute-start.12 = (bf16[208,128]{1,0:T(8,128)(2,1)S(1)}, bf16[208,128]{1,0:T(8,128)(2,1)S(1)}, u32[]{:S(2)}, u32[]{:S(2)}) collective-permute-start(bf16[208,128]{1,0:T(8,128)(2,1)S(1)} %get-tuple-element.38), channel_id=1, source_target_pairs={{0,2},{1,3},{2,0},{3,1},{4,6},{5,7},{6,4},{7,5},{8,10},{9,11},{10,... | collective-permute-start | bytes 159752 | tf_op jit(solution)/shard_map/ppermute | solution.py:125
  54.3 3.7 %copy-start.6 = (bf16[1040,128]{1,0:T(8,128)(2,1)S(1)}, bf16[1040,128]{1,0:T(8,128)(2,1)}, u32[]{:S(2)}) copy-start(bf16[1040,128]{1,0:T(8,128)(2,1)} %get-tuple-element.27) | copy-start | bytes 798724
  59.8 7.3 %collective-permute-start.14 = (bf16[1040,128]{1,0:T(8,128)(2,1)S(1)}, bf16[1040,128]{1,0:T(8,128)(2,1)S(1)}, u32[]{:S(2)}, u32[]{:S(2)}) collective-permute-start(bf16[1040,128]{1,0:T(8,128)(2,1)S(1)} %constant_dynamic-update-slice_fusion.19), channel_id=1, source_target_pairs={{0,1},{1,0},{2,3},{3,2},{4,5},{5,4},{6,7},{7,6},{8,9},{9,8},{10,11... | collective-permute-start | bytes 798728 | tf_op jit(solution)/shard_map/ppermute | solution.py:125
  59.9 6.5 %collective-permute-start.13 = (bf16[624,128]{1,0:T(8,128)(2,1)S(1)}, bf16[624,128]{1,0:T(8,128)(2,1)S(1)}, u32[]{:S(2)}, u32[]{:S(2)}) collective-permute-start(bf16[624,128]{1,0:T(8,128)(2,1)S(1)} %get-tuple-element.39), channel_id=1, source_target_pairs={{0,2},{1,3},{2,0},{3,1},{4,6},{5,7},{6,4},{7,5},{8,10},{9,11},{10,... | collective-permute-start | bytes 479240 | tf_op jit(solution)/shard_map/ppermute | solution.py:126
  66.4 2.1 %collective-permute-start.15 = (bf16[624,128]{1,0:T(8,128)(2,1)S(1)}, bf16[624,128]{1,0:T(8,128)(2,1)S(1)}, u32[]{:S(2)}, u32[]{:S(2)}) collective-permute-start(bf16[624,128]{1,0:T(8,128)(2,1)S(1)} %collective-permute-done.13), channel_id=1, source_target_pairs={{0,1},{1,0},{2,3},{3,2},{4,5},{5,4},{6,7},{7,6},{8,9},{9,8},{10,11... | collective-permute-start | bytes 479240 | tf_op jit(solution)/shard_map/ppermute | solution.py:126
  67.9 1.8 %copy-start = (bf16[1024,1024]{1,0:T(8,128)(2,1)S(1)}, bf16[1024,1024]{1,0:T(8,128)(2,1)}, u32[]{:S(2)}) copy-start(bf16[1024,1024]{1,0:T(8,128)(2,1)} %get-tuple-element.32) | copy-start | bytes 6291460
  69.7 2.3 %copy-start.3 = (f32[192,128]{1,0:T(8,128)S(1)}, f32[192,128]{1,0:T(8,128)}, u32[]{:S(2)}) copy-start(f32[192,128]{1,0:T(8,128)} %param.10) | copy-start | bytes 294916

commit v5 on v4

--- a/solution.py
+++ b/solution.py
@@ -207,15 +207,11 @@
     tar_sq = norms[1]
     residual_parts = [g[:, :n_local].reshape(-1, width) for g in got_parts]
     projected = projected_all(all_x, all_sq, centers, centers_sq, residual_parts, gamma)
-    w_hi, w_lo = split_bf16(woodbury_inverse)
+    w_hi, w_lo = lax.optimization_barrier(split_bf16(woodbury_inverse))
     p_hi, p_lo = split_bf16(projected)
-    w_both = jnp.concatenate([w_hi, w_lo], axis=1)
-    p_both = jnp.concatenate(
-        [jnp.concatenate([p_hi, p_lo], axis=1), jnp.concatenate([p_hi, jnp.zeros_like(p_lo)], axis=1)], axis=0
-    )
-    both = jnp.dot(w_both, p_both, preferred_element_type=jnp.float32)
+    both = jnp.dot(w_hi, jnp.concatenate([p_hi, p_lo], axis=1), preferred_element_type=jnp.float32)
     r = p_hi.shape[1]
-    weights = both[:, :r] + both[:, r:]
+    weights = both[:, :r] + both[:, r:] + jnp.dot(w_lo, p_hi, preferred_element_type=jnp.float32)
     correction = jnp.dot(cross, weights.astype(jnp.bfloat16), preferred_element_type=jnp.float32)
     new_solution = solution + (residual - correction) / noise_level
     relative_norm = jnp.sqrt(res_sq / (tar_sq + 1e-06))

time: 75.3 us -> 73.3 us (0.973)
  matrix products: 23.7 us -> 20.9 us
    dot_general x1, matrix products: 2.42 us -> 1.22 us  [local(): jnp.dot(cross, weights.astype(jnp.bfloat16), preferred_element_type=jnp.f...]
    dot_general x6, matrix products: 3.15 us -> 2.33 us  [projected_all(): lax.dot_general(piece, r, contract, preferred_element_type=jnp.float32)]
    dot_general x1 -> x2, matrix products: 2.24 us -> 1.46 us  [the longest x1 0.74 us: local(): jnp.dot(w_hi, jnp.concatenate([p_hi, p_lo], axis=1), preferred_element_ty...]
where the time goes in v5:
time: 73.3 us; the launch traced here: 72.3 us
  matrix products  20.9 us (29%)
  starting transfers between devices  17.9 us (24%)
  other arithmetic  14.5 us (20%)
  local copies, waits for them, and re-layouts  12.2 us (17%)
  waiting for transfers between devices  5.65 us (8%)
  between operations  1.1 us (2%)
    dot_general x10, matrix products, piece(): return jnp.dot(k, v, preferred_element_type=jnp.float32)  12.5 us
    ppermute x6, starting transfers between devices, gather_blocks(): lax.ppermute(block, 'rows', [(i, (i + k) % n_rows) for i in range(n_rows)])  10.9 us
    unnamed x31, local copies, waits for them, and re-layouts  7.49 us
    ppermute x3, waiting for transfers between devices, pipelined_xor_gather(): newest = lax.ppermute(parts[-1], axis, perm)  5.62 us
    reduce_sum x12, other arithmetic, square_norms(): return jnp.sum(jnp.square(values.astype(jnp.float32)), axis=1)  4.71 us
    convert_element_type x2, other arithmetic, split_bf16(): return (hi.astype(jnp.bfloat16), lo.astype(jnp.bfloat16))  4.49 us
    ppermute x4, starting transfers between devices, pipelined_xor_gather(): parts = parts + [lax.ppermute(p, axis, perm) for p in parts]  4.25 us
    dot_general x1, matrix products, rbf_tile(): lax.dot_general(left_x, right_x, (((1,), (1,)), ((), ())), preferred_elem...  3.36 us
  transfers between devices with their start and end apart: 16, of which 1 were waited for; matrix products, arithmetic and copies ran while one was open for 49% of the time, Pallas kernels for 0%

profile of v5, /device:TPU:0, one launch (start us, length us, event | category | flops | bytes accessed | tf_op | source)
XLA Modules:
  0.0 72.3 jit_solution(16831046416658052465)
XLA Ops:
  0.6 0.9 %convert_element_type.138 = bf16[192,128]{1,0:T(8,128)(2,1)S(1)} convert(f32[192,128]{1,0:T(8,128)} %param.10) | non-fusion elementwise | flops 24576 | bytes 147456 | tf_op jit(solution)/shard_map/convert_element_type | solution.py:176
  1.5 1.5 %pad_maximum_fusion = (bf16[192,256]{1,0:T(8,128)(2,1)}, bf16[1344,256]{1,0:T(8,128)(2,1)}) fusion(bf16[192,128]{1,0:T(8,128)(2,1)S(1)} %convert_element_type.138, bf16[192,128]{1,0:T(8,128)(2,1)} %param.9), kind=kLoop, calls=%fused_computation.146 | loop fusion | flops 196607 | bytes 294912 | tf_op jit(solution)/shard_map/concatenate | solution.py:177
  3.0 3.1 %collective-permute-start = (bf16[192,256]{1,0:T(8,128)(2,1)}, bf16[192,256]{1,0:T(8,128)(2,1)S(1)}, u32[]{:S(2)}, u32[]{:S(2)}) collective-permute-start(bf16[192,256]{1,0:T(8,128)(2,1)} %get-tuple-element.39), channel_id=1, source_target_pairs={{0,4},{4,8},{8,12},{12,0},{1,5},{5,9},{9,13},{13,1},{2,6},{6,10},{... | collective-permute-start | bytes 294920 | tf_op jit(solution)/shard_map/ppermute | solution.py:111
  6.1 2.6 %collective-permute-start.1 = (bf16[192,256]{1,0:T(8,128)(2,1)}, bf16[192,256]{1,0:T(8,128)(2,1)S(1)}, u32[]{:S(2)}, u32[]{:S(2)}) collective-permute-start(bf16[192,256]{1,0:T(8,128)(2,1)} %get-tuple-element.39), channel_id=1, source_target_pairs={{0,8},{4,12},{8,0},{12,4},{1,9},{5,13},{9,1},{13,5},{2,10},{6,14},... | collective-permute-start | bytes 294920 | tf_op jit(solution)/shard_map/ppermute | solution.py:111
  8.7 1.3 %collective-permute-start.2 = (bf16[192,256]{1,0:T(8,128)(2,1)}, bf16[192,256]{1,0:T(8,128)(2,1)S(1)}, u32[]{:S(2)}, u32[]{:S(2)}) collective-permute-start(bf16[192,256]{1,0:T(8,128)(2,1)} %get-tuple-element.39), channel_id=1, source_target_pairs={{0,12},{4,0},{8,4},{12,8},{1,13},{5,1},{9,5},{13,9},{2,14},{6,2},{... | collective-permute-start | bytes 294920 | tf_op jit(solution)/shard_map/ppermute | solution.py:111
  10.0 1.5 %collective-permute-start.3 = (bf16[192,256]{1,0:T(8,128)(2,1)}, bf16[192,256]{1,0:T(8,128)(2,1)S(1)}, u32[]{:S(2)}, u32[]{:S(2)}) collective-permute-start(bf16[192,256]{1,0:T(8,128)(2,1)} %get-tuple-element.39), channel_id=1, source_target_pairs={{0,2},{1,3},{2,0},{3,1},{4,6},{5,7},{6,4},{7,5},{8,10},{9,11},{10,... | collective-permute-start | bytes 294920 | tf_op jit(solution)/shard_map/ppermute | solution.py:123
  11.5 0.9 %multiply_reduce_fusion.13 = f32[192]{0:T(256)S(1)} fusion(bf16[192,128]{1,0:T(8,128)(2,1)} %param.9), kind=kLoop, calls=%fused_computation.193 | loop fusion | flops 73536 | bytes 49920 | tf_op jit(solution)/shard_map/reduce_sum | solution.py:15
  12.4 1.9 %fusion.86 = f32[192,128]{1,0:T(8,128)} fusion(bf16[192,128]{1,0:T(8,128)(2,1)S(1)} %convert_element_type.138, bf16[192,128]{1,0:T(8,128)(2,1)} %param.9, f32[192]{0:T(256)S(1)} %multiply_reduce_fusion.13), kind=kOutput, calls=%fused_computation.105 | convolution fusion | flops 19058688 | bytes 197376 | tf_op jit(solution)/shard_map/dot_general | solution.py:39
  14.4 0.9 %multiply_reduce_fusion.3 = f32[128]{0:T(128)S(1)} fusion(f32[192,128]{1,0:T(8,128)} %param.11), kind=kLoop, calls=%fused_computation.149 | loop fusion | flops 49024 | bytes 98816 | tf_op jit(solution)/shard_map/reduce_sum | solution.py:195
  15.3 0.7 compare_and_fusion
  16.0 4.5 %fusion = (bf16[1024,1024]{1,0:T(8,128)(2,1)S(1)}, bf16[1024,1024]{1,0:T(8,128)(2,1)}) fusion(f32[1024,1024]{1,0:T(8,128)} %param.13), kind=kLoop, calls=%fused_computation.4 | loop fusion | flops 4194304 | bytes 8388608 | tf_op jit(solution)/shard_map/convert_element_type | solution.py:54
  20.5 0.6 collective-permute-start.4
  21.3 1.6 %collective-permute-start.5 = (bf16[192,256]{1,0:T(8,128)(2,1)S(1)}, bf16[192,256]{1,0:T(8,128)(2,1)S(1)}, u32[]{:S(2)}, u32[]{:S(2)}) collective-permute-start(bf16[192,256]{1,0:T(8,128)(2,1)S(1)} %collective-permute-done.1), channel_id=1, source_target_pairs={{0,2},{1,3},{2,0},{3,1},{4,6},{5,7},{6,4},{7,5},{8,10},{9,11},{10,... | collective-permute-start | bytes 294920 | tf_op jit(solution)/shard_map/ppermute | solution.py:123
  23.1 0.6 collective-permute-start.6
  23.7 0.6 constant_dynamic-update-slice_fusion.5
  24.3 0.6 constant_dynamic-update-slice_fusion.4
  24.9 1.0 %fusion.79 = f32[192,128]{1,0:T(8,128)} fusion(bf16[192,128]{1,0:T(8,128)(2,1)S(1)} %copy-done.1, f32[192]{0:T(256)S(1)} %multiply_reduce_fusion.10, f32[192]{0:T(256)S(1)} %multiply_reduce_fusion.13, bf16[192,256]{1,0:T(8,128)(2,1)S(1)} %collective-permute-done.2), kind=kOutput, calls=%fused_computation.98 | convolution fusion | flops 19058688 | bytes 247296 | tf_op jit(solution)/shard_map/dot_general | solution.py:39
  25.9 0.6 constant_dynamic-update-slice_fusion.3
  26.7 1.0 %fusion.78 = f32[192,128]{1,0:T(8,128)} fusion(bf16[192,128]{1,0:T(8,128)(2,1)S(1)} %copy-done.1, f32[192]{0:T(256)S(1)} %multiply_reduce_fusion.9, f32[192]{0:T(256)S(1)} %multiply_reduce_fusion.13, bf16[192,256]{1,0:T(8,128)(2,1)S(1)} %collective-permute-done.3), kind=kOutput, calls=%fused_computation.97 | convolution fusion | flops 19058688 | bytes 247296 | tf_op jit(solution)/shard_map/dot_general | solution.py:39
  27.7 1.9 %fusion.85 = f32[192,128]{1,0:T(8,128)} fusion(f32[192,128]{1,0:T(8,128)} %fusion.86, bf16[192,128]{1,0:T(8,128)(2,1)S(1)} %copy-done.1, f32[192]{0:T(256)S(1)} %multiply_reduce_fusion.12, f32[192]{0:T(256)S(1)} %multiply_reduce_fusion.13, bf16[192,256]{1,0:T(8,128)(2,1)S(1)} %collective-permute-done), kind=kOutput, calls=%fused_computation.104 | convolution fusion | flops 19083264 | bytes 345600 | tf_op jit(solution)/shard_map/dot_general | solution.py:39
  29.6 2.0 %fusion.83 = f32[192,128]{1,0:T(8,128)} fusion(f32[192,128]{1,0:T(8,128)} %fusion.78, f32[192,128]{1,0:T(8,128)} %fusion.79, f32[192,128]{1,0:T(8,128)} %fusion.85, bf16[192,128]{1,0:T(8,128)(2,1)S(1)} %copy-done.1, f32[192]{0:T(256)S(1)} %multiply_reduce_fusion.11, f32[192]{0:T(256)S(1)} %multiply_reduce_fusion.13, ...), kind=kOutput, calls=%fused_computation.102 | convolution fusion | flops 19132416 | bytes 542208 | tf_op jit(solution)/shard_map/dot_general | solution.py:39
  31.6 0.6 constant_dynamic-update-slice_fusion.2
  32.2 0.6 constant_dynamic-update-slice_fusion.1
  32.9 0.6 constant_dynamic-update-slice_fusion
  33.6 0.9 %multiply_reduce_fusion.6 = f32[192]{0:T(256)S(1)} fusion(bf16[192,256]{1,0:T(8,128)(2,1)} %collective-permute-done.6), kind=kLoop, calls=%fused_computation.154 | loop fusion | flops 73536 | bytes 49920 | tf_op jit(solution)/shard_map/reduce_sum | solution.py:15
  34.5 0.6 collective-permute-start.8
  35.1 1.2 %fusion.71 = f32[192,128]{1,0:T(8,128)S(1)} fusion(bf16[192,128]{1,0:T(8,128)(2,1)S(1)} %copy-done.1, f32[192]{0:T(256)S(1)} %multiply_reduce_fusion.6, f32[192]{0:T(256)S(1)} %multiply_reduce_fusion.13, bf16[192,256]{1,0:T(8,128)(2,1)} %collective-permute-done.6), kind=kOutput, calls=%fused_computation.90 | convolution fusion | flops 19058688 | bytes 247296 | tf_op jit(solution)/shard_map/dot_general | solution.py:39
  36.3 0.8 %constant_dynamic-update-slice_fusion.8 = bf16[3072,128]{1,0:T(8,128)(2,1)S(1)} fusion(bf16[3072,128]{1,0:T(8,128)(2,1)S(1)} %constant_dynamic-update-slice_fusion.9, bf16[192,256]{1,0:T(8,128)(2,1)} %collective-permute-done.6), kind=kLoop, calls=%fused_computation.203 | loop fusion | bytes 98304
  37.7 1.3 %multiply_reduce_fusion.1 = f32[1344]{0:T(1024)S(1)} fusion(bf16[1344,256]{1,0:T(8,128)(2,1)} %collective-permute-done.7), kind=kLoop, calls=%fused_computation.113 | loop fusion | flops 514752 | bytes 349440 | tf_op jit(solution)/shard_map/reduce_sum | solution.py:15
  39.0 1.6 %fusion.13 = f32[192,128]{1,0:T(8,128)S(1)} fusion(bf16[192,128]{1,0:T(8,128)(2,1)S(1)} %copy-done.1, f32[1344]{0:T(1024)S(1)} %multiply_reduce_fusion.1, f32[192]{0:T(256)S(1)} %multiply_reduce_fusion.13, bf16[1344,256]{1,0:T(8,128)(2,1)} %collective-permute-done.7), kind=kOutput, calls=%fused_computation.20 | convolution fusion | flops 133410816 | bytes 841728 | tf_op jit(solution)/shard_map/dot_general | solution.py:39
  41.0 1.4 %multiply_reduce_fusion.4 = (f32[128]{0:T(128)S(1)}, f32[192,128]{1,0:T(8,128)S(1)}) fusion(f32[192,128]{1,0:T(8,128)} %param.10, f32[192,128]{1,0:T(8,128)} %param.11, f32[192,128]{1,0:T(8,128)S(1)} %fusion.77, bf16[192,256]{1,0:T(8,128)(2,1)} %copy-done.5, bf16[192,128]{1,0:T(8,128)(2,1)S(1)} %copy-done.1, f32[192]{0:T(256)S(1)} %multiply_reduce_fusion.5, ...), kind=kOutput, calls=%fused_computation.150 | convolution fusion | flops 19206016 | bytes 542720 | tf_op jit(solution)/shard_map/dot_general | solution.py:39
  42.4 0.6 constant_dynamic-update-slice_fusion.24
  43.0 0.7 %collective-permute-start.9 = (bf16[208,128]{1,0:T(8,128)(2,1)S(1)}, bf16[208,128]{1,0:T(8,128)(2,1)}, u32[]{:S(2)}, u32[]{:S(2)}) collective-permute-start(bf16[208,128]{1,0:T(8,128)(2,1)S(1)} %get-tuple-element.42), channel_id=1, source_target_pairs={{0,4},{4,8},{8,12},{12,0},{1,5},{5,9},{9,13},{13,1},{2,6},{6,10},{... | collective-permute-start | bytes 159752 | tf_op jit(solution)/shard_map/ppermute | solution.py:111
  44.1 2.8 %collective-permute-start.11 = (bf16[208,128]{1,0:T(8,128)(2,1)S(1)}, bf16[208,128]{1,0:T(8,128)(2,1)S(1)}, u32[]{:S(2)}, u32[]{:S(2)}) collective-permute-start(bf16[208,128]{1,0:T(8,128)(2,1)S(1)} %get-tuple-element.42), channel_id=1, source_target_pairs={{0,12},{4,0},{8,4},{12,8},{1,13},{5,1},{9,5},{13,9},{2,14},{6,2},{... | collective-permute-start | bytes 159752 | tf_op jit(solution)/shard_map/ppermute | solution.py:111
  46.9 1.5 %collective-permute-start.12 = (bf16[208,128]{1,0:T(8,128)(2,1)S(1)}, bf16[208,128]{1,0:T(8,128)(2,1)S(1)}, u32[]{:S(2)}, u32[]{:S(2)}) collective-permute-start(bf16[208,128]{1,0:T(8,128)(2,1)S(1)} %get-tuple-element.42), channel_id=1, source_target_pairs={{0,2},{1,3},{2,0},{3,1},{4,6},{5,7},{6,4},{7,5},{8,10},{9,11},{10,... | collective-permute-start | bytes 159752 | tf_op jit(solution)/shard_map/ppermute | solution.py:125
  48.4 1.0 %slice_dynamic-update-slice_fusion = bf16[3072,128]{1,0:T(8,128)(2,1)S(1)} fusion(bf16[3072,128]{1,0:T(8,128)(2,1)S(1)} %constant_dynamic-update-slice_fusion.8, bf16[1344,256]{1,0:T(8,128)(2,1)} %collective-permute-done.7), kind=kLoop, calls=%fused_computation.134 | loop fusion | bytes 688128
  49.4 0.8 %constant_dynamic-update-slice_fusion.7 = bf16[3072,128]{1,0:T(8,128)(2,1)S(1)} fusion(bf16[3072,128]{1,0:T(8,128)(2,1)S(1)} %slice_dynamic-update-slice_fusion, bf16[192,256]{1,0:T(8,128)(2,1)} %copy-done.5), kind=kLoop, calls=%fused_computation.202 | loop fusion | bytes 98304 | tf_op jit(solution)/shard_map/concatenate | solution.py:186
  50.7 3.2 %gather_fusion = bf16[1024,128]{1,0:T(8,128)(2,1)S(1)} fusion(bf16[3072,128]{1,0:T(8,128)(2,1)S(1)} %constant_dynamic-update-slice_fusion.7, s32[1024]{0:T(1024)S(1)} %broadcast_clamp_fusion), kind=kCustom, calls=%fused_computation | custom fusion | bytes 528384 | tf_op jit(solution)/shard_map/jit(_take)/gather | solution.py:190
  54.3 3.4 %exponential_convert_fusion = bf16[3072,1024]{1,0:T(8,128)(2,1)S(1)} fusion(bf16[3072,128]{1,0:T(8,128)(2,1)S(1)} %constant_dynamic-update-slice_fusion.7, f32[1024]{0:T(1024)S(1)} %multiply_reduce_fusion.2, f32[3072]{0:T(1024)S(1)} %multiply_reduce_fusion, bf16[1024,128]{1,0:T(8,128)(2,1)S(1)} %gather_fusion, pred[1024]{0:T(1024)(128)(4,1)S(1)} %get-tuple-element.31), kind=kOutput, calls=%fused_computation.1 | convolution fusion | flops 821166080 | bytes 7357440 | tf_op jit(solution)/shard_map/dot_general | solution.py:19
  58.0 0.8 %constant_dynamic-update-slice_fusion.18 = (bf16[624,128]{1,0:T(8,128)(2,1)S(1)}, bf16[1040,128]{1,0:T(8,128)(2,1)S(1)}) fusion(bf16[208,128]{1,0:T(8,128)(2,1)} %collective-permute-done.9, bf16[1040,128]{1,0:T(8,128)(2,1)S(1)} %constant_dynamic-update-slice_fusion.23), kind=kLoop, calls=%fused_computation.213 | loop fusion | bytes 159744
  58.8 0.8 %constant_dynamic-update-slice_fusion.17 = (bf16[624,128]{1,0:T(8,128)(2,1)S(1)}, bf16[1040,128]{1,0:T(8,128)(2,1)S(1)}) fusion(bf16[624,128]{1,0:T(8,128)(2,1)S(1)} %get-tuple-element.47, bf16[208,128]{1,0:T(8,128)(2,1)} %collective-permute-done.10, bf16[1040,128]{1,0:T(8,128)(2,1)S(1)} %get-tuple-element.48), kind=kLoop, calls=%fused_computation.212 | loop fusion | bytes 159744
  59.8 0.6 collective-permute-start.13
  60.7 5.6 %collective-permute-done.13 = bf16[624,128]{1,0:T(8,128)(2,1)S(1)} collective-permute-done((bf16[624,128]{1,0:T(8,128)(2,1)S(1)}, bf16[624,128]{1,0:T(8,128)(2,1)S(1)}, u32[]{:S(2)}, u32[]{:S(2)}) %collective-permute-start.13) | collective-permute-done | bytes 159776 | tf_op jit(solution)/shard_map/ppermute | solution.py:126
  68.0 0.5 sqrt_bitcast_fusion
  68.9 0.5 copy-done
  69.5 0.7 %fusion.97 = f32[1024,256]{1,0:T(8,128)S(1)} fusion(bf16[1024,1024]{1,0:T(8,128)(2,1)S(1)} %copy-done, bf16[1024,128]{0,1:T(8,128)(2,1)S(1)} %get-tuple-element.37, bf16[1024,128]{0,1:T(8,128)(2,1)S(1)} %get-tuple-element.38), kind=kOutput, calls=%fused_computation.120 | convolution fusion | flops 537919488 | bytes 3670016 | tf_op jit(solution)/shard_map/dot_general | solution.py:212
  70.2 0.7 fusion.18
  71.1 1.2 %fusion.89 = f32[192,128]{1,0:T(8,128)} fusion(f32[192,128]{1,0:T(8,128)S(1)} %copy-done.3, f32[192,128]{1,0:T(8,128)S(1)} %get-tuple-element.50, bf16[1024,128]{1,0:T(8,128)(2,1)S(1)} %fusion.18, bf16[192,128]{1,0:T(8,128)(2,1)S(1)} %copy-done.1, f32[1024]{0:T(1024)S(1)} %multiply_reduce_fusion.2, f32[192]{0:T(256)S(1)} %multiply_reduce_fusion.13, ...), kind=kOutput, calls=%fused_computation.108 | convolution fusion | flops 101851136 | bytes 874240 | tf_op jit(solution)/shard_map/dot_general | solution.py:215
  (73 shorter events, 5.6 us)
Async XLA Ops:
  3.0 17.5 %collective-permute-start = (bf16[192,256]{1,0:T(8,128)(2,1)}, bf16[192,256]{1,0:T(8,128)(2,1)S(1)}, u32[]{:S(2)}, u32[]{:S(2)}) collective-permute-start(bf16[192,256]{1,0:T(8,128)(2,1)} %get-tuple-element.39), channel_id=1, source_target_pairs={{0,4},{4,8},{8,12},{12,0},{1,5},{5,9},{9,13},{13,1},{2,6},{6,10},{... | collective-permute-start | bytes 294920 | tf_op jit(solution)/shard_map/ppermute | solution.py:111
  6.1 15.2 %collective-permute-start.1 = (bf16[192,256]{1,0:T(8,128)(2,1)}, bf16[192,256]{1,0:T(8,128)(2,1)S(1)}, u32[]{:S(2)}, u32[]{:S(2)}) collective-permute-start(bf16[192,256]{1,0:T(8,128)(2,1)} %get-tuple-element.39), channel_id=1, source_target_pairs={{0,8},{4,12},{8,0},{12,4},{1,9},{5,13},{9,1},{13,5},{2,10},{6,14},... | collective-permute-start | bytes 294920 | tf_op jit(solution)/shard_map/ppermute | solution.py:111
  8.7 14.3 %collective-permute-start.2 = (bf16[192,256]{1,0:T(8,128)(2,1)}, bf16[192,256]{1,0:T(8,128)(2,1)S(1)}, u32[]{:S(2)}, u32[]{:S(2)}) collective-permute-start(bf16[192,256]{1,0:T(8,128)(2,1)} %get-tuple-element.39), channel_id=1, source_target_pairs={{0,12},{4,0},{8,4},{12,8},{1,13},{5,1},{9,5},{13,9},{2,14},{6,2},{... | collective-permute-start | bytes 294920 | tf_op jit(solution)/shard_map/ppermute | solution.py:111
  10.0 16.6 %collective-permute-start.3 = (bf16[192,256]{1,0:T(8,128)(2,1)}, bf16[192,256]{1,0:T(8,128)(2,1)S(1)}, u32[]{:S(2)}, u32[]{:S(2)}) collective-permute-start(bf16[192,256]{1,0:T(8,128)(2,1)} %get-tuple-element.39), channel_id=1, source_target_pairs={{0,2},{1,3},{2,0},{3,1},{4,6},{5,7},{6,4},{7,5},{8,10},{9,11},{10,... | collective-permute-start | bytes 294920 | tf_op jit(solution)/shard_map/ppermute | solution.py:123
  16.0 4.5 %copy-start.1 = (bf16[192,128]{1,0:T(8,128)(2,1)S(1)}, bf16[192,128]{1,0:T(8,128)(2,1)}, u32[]{:S(2)}) copy-start(bf16[192,128]{1,0:T(8,128)(2,1)} %param.9) | copy-start | bytes 147460
  20.5 11.7 %collective-permute-start.4 = (bf16[192,256]{1,0:T(8,128)(2,1)S(1)}, bf16[192,256]{1,0:T(8,128)(2,1)S(1)}, u32[]{:S(2)}, u32[]{:S(2)}) collective-permute-start(bf16[192,256]{1,0:T(8,128)(2,1)S(1)} %collective-permute-done), channel_id=1, source_target_pairs={{0,2},{1,3},{2,0},{3,1},{4,6},{5,7},{6,4},{7,5},{8,10},{9,11},{10,... | collective-permute-start | bytes 294920 | tf_op jit(solution)/shard_map/ppermute | solution.py:123
  21.3 11.6 %collective-permute-start.5 = (bf16[192,256]{1,0:T(8,128)(2,1)S(1)}, bf16[192,256]{1,0:T(8,128)(2,1)S(1)}, u32[]{:S(2)}, u32[]{:S(2)}) collective-permute-start(bf16[192,256]{1,0:T(8,128)(2,1)S(1)} %collective-permute-done.1), channel_id=1, source_target_pairs={{0,2},{1,3},{2,0},{3,1},{4,6},{5,7},{6,4},{7,5},{8,10},{9,11},{10,... | collective-permute-start | bytes 294920 | tf_op jit(solution)/shard_map/ppermute | solution.py:123
  23.1 10.6 %collective-permute-start.6 = (bf16[192,256]{1,0:T(8,128)(2,1)S(1)}, bf16[192,256]{1,0:T(8,128)(2,1)}, u32[]{:S(2)}, u32[]{:S(2)}) collective-permute-start(bf16[192,256]{1,0:T(8,128)(2,1)S(1)} %collective-permute-done.2), channel_id=1, source_target_pairs={{0,2},{1,3},{2,0},{3,1},{4,6},{5,7},{6,4},{7,5},{8,10},{9,11},{10,... | collective-permute-start | bytes 294920 | tf_op jit(solution)/shard_map/ppermute | solution.py:123
  33.5 7.1 %copy-start.2 = (f32[192,128]{1,0:T(8,128)S(1)}, f32[192,128]{1,0:T(8,128)}, u32[]{:S(2)}) copy-start(f32[192,128]{1,0:T(8,128)} %fusion.83) | copy-start | bytes 294916
  33.5 4.2 %collective-permute-start.7 = (bf16[1344,256]{1,0:T(8,128)(2,1)}, bf16[1344,256]{1,0:T(8,128)(2,1)}, u32[]{:S(2)}, u32[]{:S(2)}) collective-permute-start(bf16[1344,256]{1,0:T(8,128)(2,1)} %constant_dynamic-update-slice_fusion), channel_id=1, source_target_pairs={{0,1},{1,0},{2,3},{3,2},{4,5},{5,4},{6,7},{7,6},{8,9},{9,8},{10,11... | collective-permute-start | bytes 2064392 | tf_op jit(solution)/shard_map/ppermute | solution.py:125
  34.5 3.0 %collective-permute-start.8 = (bf16[192,256]{1,0:T(8,128)(2,1)}, bf16[192,256]{1,0:T(8,128)(2,1)S(1)}, u32[]{:S(2)}, u32[]{:S(2)}) collective-permute-start(bf16[192,256]{1,0:T(8,128)(2,1)} %collective-permute-done.6), channel_id=1, source_target_pairs={{0,1},{1,0},{2,3},{3,2},{4,5},{5,4},{6,7},{7,6},{8,9},{9,8},{10,11... | collective-permute-start | bytes 294920 | tf_op jit(solution)/shard_map/ppermute | solution.py:126
  37.6 1.4 %copy-start.5 = (bf16[192,256]{1,0:T(8,128)(2,1)}, bf16[192,256]{1,0:T(8,128)(2,1)S(1)}, u32[]{:S(2)}) copy-start(bf16[192,256]{1,0:T(8,128)(2,1)S(1)} %collective-permute-done.8) | copy-start | bytes 294916
  42.3 28.6 %copy-start.4 = (f32[192,128]{1,0:T(8,128)}, f32[192,128]{1,0:T(8,128)S(1)}, u32[]{:S(2)}) copy-start(f32[192,128]{1,0:T(8,128)S(1)} %get-tuple-element.50) | copy-start | bytes 294916
  43.0 14.9 %collective-permute-start.9 = (bf16[208,128]{1,0:T(8,128)(2,1)S(1)}, bf16[208,128]{1,0:T(8,128)(2,1)}, u32[]{:S(2)}, u32[]{:S(2)}) collective-permute-start(bf16[208,128]{1,0:T(8,128)(2,1)S(1)} %get-tuple-element.42), channel_id=1, source_target_pairs={{0,4},{4,8},{8,12},{12,0},{1,5},{5,9},{9,13},{13,1},{2,6},{6,10},{... | collective-permute-start | bytes 159752 | tf_op jit(solution)/shard_map/ppermute | solution.py:111
  43.8 15.1 %collective-permute-start.10 = (bf16[208,128]{1,0:T(8,128)(2,1)S(1)}, bf16[208,128]{1,0:T(8,128)(2,1)}, u32[]{:S(2)}, u32[]{:S(2)}) collective-permute-start(bf16[208,128]{1,0:T(8,128)(2,1)S(1)} %get-tuple-element.42), channel_id=1, source_target_pairs={{0,8},{4,12},{8,0},{12,4},{1,9},{5,13},{9,1},{13,5},{2,10},{6,14},... | collective-permute-start | bytes 159752 | tf_op jit(solution)/shard_map/ppermute | solution.py:111
  44.1 15.6 %collective-permute-start.11 = (bf16[208,128]{1,0:T(8,128)(2,1)S(1)}, bf16[208,128]{1,0:T(8,128)(2,1)S(1)}, u32[]{:S(2)}, u32[]{:S(2)}) collective-permute-start(bf16[208,128]{1,0:T(8,128)(2,1)S(1)} %get-tuple-element.42), channel_id=1, source_target_pairs={{0,12},{4,0},{8,4},{12,8},{1,13},{5,1},{9,5},{13,9},{2,14},{6,2},{... | collective-permute-start | bytes 159752 | tf_op jit(solution)/shard_map/ppermute | solution.py:111
  46.9 12.8 %collective-permute-start.12 = (bf16[208,128]{1,0:T(8,128)(2,1)S(1)}, bf16[208,128]{1,0:T(8,128)(2,1)S(1)}, u32[]{:S(2)}, u32[]{:S(2)}) collective-permute-start(bf16[208,128]{1,0:T(8,128)(2,1)S(1)} %get-tuple-element.42), channel_id=1, source_target_pairs={{0,2},{1,3},{2,0},{3,1},{4,6},{5,7},{6,4},{7,5},{8,10},{9,11},{10,... | collective-permute-start | bytes 159752 | tf_op jit(solution)/shard_map/ppermute | solution.py:125
  54.3 3.6 %copy-start.6 = (bf16[1040,128]{1,0:T(8,128)(2,1)S(1)}, bf16[1040,128]{1,0:T(8,128)(2,1)}, u32[]{:S(2)}) copy-start(bf16[1040,128]{1,0:T(8,128)(2,1)} %get-tuple-element.33) | copy-start | bytes 798724
  59.7 7.1 %collective-permute-start.14 = (bf16[1040,128]{1,0:T(8,128)(2,1)S(1)}, bf16[1040,128]{1,0:T(8,128)(2,1)S(1)}, u32[]{:S(2)}, u32[]{:S(2)}) collective-permute-start(bf16[1040,128]{1,0:T(8,128)(2,1)S(1)} %constant_dynamic-update-slice_fusion.19), channel_id=1, source_target_pairs={{0,1},{1,0},{2,3},{3,2},{4,5},{5,4},{6,7},{7,6},{8,9},{9,8},{10,11... | collective-permute-start | bytes 798728 | tf_op jit(solution)/shard_map/ppermute | solution.py:125
  59.8 6.5 %collective-permute-start.13 = (bf16[624,128]{1,0:T(8,128)(2,1)S(1)}, bf16[624,128]{1,0:T(8,128)(2,1)S(1)}, u32[]{:S(2)}, u32[]{:S(2)}) collective-permute-start(bf16[624,128]{1,0:T(8,128)(2,1)S(1)} %get-tuple-element.43), channel_id=1, source_target_pairs={{0,2},{1,3},{2,0},{3,1},{4,6},{5,7},{6,4},{7,5},{8,10},{9,11},{10,... | collective-permute-start | bytes 479240 | tf_op jit(solution)/shard_map/ppermute | solution.py:126
  66.3 1.5 %collective-permute-start.15 = (bf16[624,128]{1,0:T(8,128)(2,1)S(1)}, bf16[624,128]{1,0:T(8,128)(2,1)S(1)}, u32[]{:S(2)}, u32[]{:S(2)}) collective-permute-start(bf16[624,128]{1,0:T(8,128)(2,1)S(1)} %collective-permute-done.13), channel_id=1, source_target_pairs={{0,1},{1,0},{2,3},{3,2},{4,5},{5,4},{6,7},{7,6},{8,9},{9,8},{10,11... | collective-permute-start | bytes 479240 | tf_op jit(solution)/shard_map/ppermute | solution.py:126
  67.9 1.6 %copy-start = (bf16[1024,1024]{1,0:T(8,128)(2,1)S(1)}, bf16[1024,1024]{1,0:T(8,128)(2,1)}, u32[]{:S(2)}) copy-start(bf16[1024,1024]{1,0:T(8,128)(2,1)} %get-tuple-element.29) | copy-start | bytes 6291460
  70.2 0.9 %copy-start.3 = (f32[192,128]{1,0:T(8,128)S(1)}, f32[192,128]{1,0:T(8,128)}, u32[]{:S(2)}) copy-start(f32[192,128]{1,0:T(8,128)} %param.10) | copy-start | bytes 294916

commit v6 on v5

--- a/solution.py
+++ b/solution.py
@@ -178,17 +178,19 @@
     parts = gather_blocks(packed, split_pieces=True)
     own_sq = square_norms(points)
     kp = None
+    part_sqs = []
     for part in parts:
         part_x = part[:, :F]
-        term = kernel_product(points, own_sq, part_x, square_norms(part_x), part[:, F:], gamma)
+        part_sqs.append(square_norms(part_x))
+        term = kernel_product(points, own_sq, part_x, part_sqs[-1], part[:, F:], gamma)
         kp = term if kp is None else kp + term
     residual = targets - kp - noise_level * solution
     all_x = jnp.concatenate([part[:, :F] for part in parts], axis=0)
-    all_sq = square_norms(all_x)
+    all_sq = jnp.concatenate(part_sqs, axis=0)
     owner = inducing // n_local
     position = relative_order(owner) * n_local + inducing % n_local
     centers = jnp.take(all_x, position, axis=0)
-    centers_sq = square_norms(centers)
+    centers_sq = jnp.take(all_sq, position, axis=0)
     cross = rbf_tile(points, own_sq, centers, centers_sq, gamma)
     residual_b = residual.astype(jnp.bfloat16)
     res_local = jnp.sum(residual * residual, axis=0)
@@ -207,7 +209,7 @@
     tar_sq = norms[1]
     residual_parts = [g[:, :n_local].reshape(-1, width) for g in got_parts]
     projected = projected_all(all_x, all_sq, centers, centers_sq, residual_parts, gamma)
-    w_hi, w_lo = lax.optimization_barrier(split_bf16(woodbury_inverse))
+    w_hi, w_lo = split_bf16(woodbury_inverse)
     p_hi, p_lo = split_bf16(projected)
     both = jnp.dot(w_hi, jnp.concatenate([p_hi, p_lo], axis=1), preferred_element_type=jnp.float32)
     r = p_hi.shape[1]

time: 73.3 us -> 58.4 us (0.80)
  other arithmetic: 14.5 us -> 6.14 us
  matrix products: 20.9 us -> 16.2 us
  starting transfers between devices: 17.9 us -> 16 us
  waiting for transfers between devices: 5.65 us -> 6.9 us
  local copies, waits for them, and re-layouts: 12.2 us -> 11.3 us
    gather x0 -> x1, local copies, waits for them, and re-layouts: none -> 6.14 us  [local(): centers_sq = jnp.take(all_sq, position, axis=0)]
    unnamed x31 -> x27, local copies, waits for them, and re-layouts: 7.49 us -> 1.72 us
    dot_general x10, matrix products: 12.5 us -> 7.75 us  [piece(): return jnp.dot(k, v, preferred_element_type=jnp.float32)]
    convert_element_type x2 -> x1, other arithmetic: 4.49 us -> 0.01 us  [split_bf16(): return (hi.astype(jnp.bfloat16), lo.astype(jnp.bfloat16))]
    ppermute x6, starting transfers between devices: 10.9 us -> 7.4 us  [gather_blocks(): lax.ppermute(block, 'rows', [(i, (i + k) % n_rows) for i in range(n_rows)])]
    reduce_sum x12 -> x10, other arithmetic: 4.71 us -> 2.09 us  [square_norms(): return jnp.sum(jnp.square(values.astype(jnp.float32)), axis=1)]
    ppermute x6, waiting for transfers between devices: 0.02 us -> 1.93 us  [gather_blocks(): lax.ppermute(block, 'rows', [(i, (i + k) % n_rows) for i in range(n_rows)])]
    ppermute x4, starting transfers between devices: 4.25 us -> 5.72 us  [pipelined_xor_gather(): parts = parts + [lax.ppermute(p, axis, perm) for p in parts]]
  transfers between devices with their start and end apart: 16 -> 16, of which waited for: 1 -> 3; matrix products, arithmetic and copies ran while one was open for 49% -> 45% of each run, Pallas kernels for 0% -> 0%
where the time goes in v6:
time: 58.4 us; the launch traced here: 57.7 us
  matrix products  16.2 us (28%)
  starting transfers between devices  16 us (27%)
  local copies, waits for them, and re-layouts  11.3 us (19%)
  waiting for transfers between devices  6.9 us (12%)
  other arithmetic  6.14 us (11%)
  between operations  1.2 us (2%)
    dot_general x10, matrix products, piece(): return jnp.dot(k, v, preferred_element_type=jnp.float32)  7.75 us
    ppermute x6, starting transfers between devices, gather_blocks(): lax.ppermute(block, 'rows', [(i, (i + k) % n_rows) for i in range(n_rows)])  7.4 us
    gather x1, local copies, waits for them, and re-layouts, local(): centers_sq = jnp.take(all_sq, position, axis=0)  6.14 us
    ppermute x4, starting transfers between devices, pipelined_xor_gather(): parts = parts + [lax.ppermute(p, axis, perm) for p in parts]  5.72 us
    ppermute x3, waiting for transfers between devices, pipelined_xor_gather(): newest = lax.ppermute(parts[-1], axis, perm)  4.95 us
    dot_general x1, matrix products, rbf_tile(): lax.dot_general(left_x, right_x, (((1,), (1,)), ((), ())), preferred_elem...  3.38 us
    gather x1, local copies, waits for them, and re-layouts, local(): centers = jnp.take(all_x, position, axis=0)  3.21 us
    dot_general x6, matrix products, projected_all(): lax.dot_general(piece, r, contract, preferred_element_type=jnp.float32)  2.32 us
  transfers between devices with their start and end apart: 16, of which 3 were waited for; matrix products, arithmetic and copies ran while one was open for 45% of the time, Pallas kernels for 0%

profile of v6, /device:TPU:0, one launch (start us, length us, event | category | flops | bytes accessed | tf_op | source)
XLA Modules:
  0.0 57.7 jit_solution(16084840623841550438)
XLA Ops:
  0.6 0.9 %convert_element_type.132 = bf16[192,128]{1,0:T(8,128)(2,1)S(1)} convert(f32[192,128]{1,0:T(8,128)} %param.10) | non-fusion elementwise | flops 24576 | bytes 147456 | tf_op jit(solution)/shard_map/convert_element_type | solution.py:176
  1.6 0.8 %pad_maximum_fusion = (bf16[192,256]{1,0:T(8,128)(2,1)S(1)}, bf16[1344,256]{1,0:T(8,128)(2,1)S(1)}) fusion(bf16[192,128]{1,0:T(8,128)(2,1)S(1)} %convert_element_type.132, bf16[192,128]{1,0:T(8,128)(2,1)} %param.9), kind=kLoop, calls=%fused_computation.147 | loop fusion | flops 196607 | bytes 294912 | tf_op jit(solution)/shard_map/concatenate | solution.py:177
  2.4 3.0 %collective-permute-start.3 = (bf16[192,256]{1,0:T(8,128)(2,1)S(1)}, bf16[192,256]{1,0:T(8,128)(2,1)S(1)}, u32[]{:S(2)}, u32[]{:S(2)}) collective-permute-start(bf16[192,256]{1,0:T(8,128)(2,1)S(1)} %get-tuple-element.35), channel_id=1, source_target_pairs={{0,2},{1,3},{2,0},{3,1},{4,6},{5,7},{6,4},{7,5},{8,10},{9,11},{10,... | collective-permute-start | bytes 294920 | tf_op jit(solution)/shard_map/ppermute | solution.py:123
  5.4 3.6 %collective-permute-start.2 = (bf16[192,256]{1,0:T(8,128)(2,1)S(1)}, bf16[192,256]{1,0:T(8,128)(2,1)S(1)}, u32[]{:S(2)}, u32[]{:S(2)}) collective-permute-start(bf16[192,256]{1,0:T(8,128)(2,1)S(1)} %get-tuple-element.35), channel_id=1, source_target_pairs={{0,12},{4,0},{8,4},{12,8},{1,13},{5,1},{9,5},{13,9},{2,14},{6,2},{... | collective-permute-start | bytes 294920 | tf_op jit(solution)/shard_map/ppermute | solution.py:111
  9.0 1.0 %collective-permute-start = (bf16[192,256]{1,0:T(8,128)(2,1)S(1)}, bf16[192,256]{1,0:T(8,128)(2,1)S(1)}, u32[]{:S(2)}, u32[]{:S(2)}) collective-permute-start(bf16[192,256]{1,0:T(8,128)(2,1)S(1)} %get-tuple-element.35), channel_id=1, source_target_pairs={{0,4},{4,8},{8,12},{12,0},{1,5},{5,9},{9,13},{13,1},{2,6},{6,10},{... | collective-permute-start | bytes 294920 | tf_op jit(solution)/shard_map/ppermute | solution.py:111
  10.0 0.9 %multiply_reduce_fusion.11 = f32[192]{0:T(256)S(1)} fusion(bf16[192,128]{1,0:T(8,128)(2,1)} %param.9), kind=kLoop, calls=%fused_computation.194 | loop fusion | flops 73536 | bytes 49920 | tf_op jit(solution)/shard_map/reduce_sum | solution.py:15
  10.9 0.9 %multiply_reduce_fusion.1 = f32[128]{0:T(128)S(1)} fusion(f32[192,128]{1,0:T(8,128)} %param.11), kind=kLoop, calls=%fused_computation.150 | loop fusion | flops 49024 | bytes 98816 | tf_op jit(solution)/shard_map/reduce_sum | solution.py:197
  11.9 1.3 %fusion.95 = f32[192,128]{1,0:T(8,128)S(1)} fusion(bf16[192,128]{1,0:T(8,128)(2,1)S(1)} %convert_element_type.132, bf16[192,128]{1,0:T(8,128)(2,1)} %param.9, f32[192]{0:T(256)S(1)} %multiply_reduce_fusion.11), kind=kOutput, calls=%fused_computation.108 | convolution fusion | flops 19058688 | bytes 197376 | tf_op jit(solution)/shard_map/dot_general | solution.py:39
  13.2 0.7 %broadcast_clamp_fusion = (s32[1024]{0:T(1024)S(1)}, s32[1024]{0:T(1024)S(1)}) fusion(s32[]{:T(128)S(6)} %axis_index.25, s32[1024]{0:T(1024)} %param.12, s32[]{:T(128)S(6)} %axis_index.22), kind=kLoop, calls=%fused_computation.266 | loop fusion | flops 60416 | bytes 12296 | tf_op jit(solution)/shard_map/jit(_take)/gather | solution.py:193
  13.9 0.8 %constant_dynamic-update-slice_fusion.15 = bf16[3072,128]{1,0:T(8,128)(2,1)S(1)} fusion(bf16[192,128]{1,0:T(8,128)(2,1)} %param.9), kind=kLoop, calls=%fused_computation.211 | loop fusion | bytes 98304
  14.7 0.6 %collective-permute-start.6 = (bf16[192,256]{1,0:T(8,128)(2,1)S(1)}, bf16[192,256]{1,0:T(8,128)(2,1)S(1)}, u32[]{:S(2)}, u32[]{:S(2)}) collective-permute-start(bf16[192,256]{1,0:T(8,128)(2,1)S(1)} %collective-permute-done.2), channel_id=1, source_target_pairs={{0,2},{1,3},{2,0},{3,1},{4,6},{5,7},{6,4},{7,5},{8,10},{9,11},{10,... | collective-permute-start | bytes 294920 | tf_op jit(solution)/shard_map/ppermute | solution.py:123
  15.4 1.9 %collective-permute-done.1 = bf16[192,256]{1,0:T(8,128)(2,1)S(1)} collective-permute-done((bf16[192,256]{1,0:T(8,128)(2,1)S(1)}, bf16[192,256]{1,0:T(8,128)(2,1)S(1)}, u32[]{:S(2)}, u32[]{:S(2)}) %collective-permute-start.1) | collective-permute-done | bytes 98336 | tf_op jit(solution)/shard_map/ppermute | solution.py:111
  17.4 0.5 collective-permute-start.5
  18.0 1.6 %collective-permute-start.4 = (bf16[192,256]{1,0:T(8,128)(2,1)S(1)}, bf16[192,256]{1,0:T(8,128)(2,1)S(1)}, u32[]{:S(2)}, u32[]{:S(2)}) collective-permute-start(bf16[192,256]{1,0:T(8,128)(2,1)S(1)} %collective-permute-done), channel_id=1, source_target_pairs={{0,2},{1,3},{2,0},{3,1},{4,6},{5,7},{6,4},{7,5},{8,10},{9,11},{10,... | collective-permute-start | bytes 294920 | tf_op jit(solution)/shard_map/ppermute | solution.py:123
  19.7 0.1 multiply_reduce_fusion.7
  19.8 1.1 %fusion.87 = f32[192,128]{1,0:T(8,128)S(1)} fusion(bf16[192,128]{1,0:T(8,128)(2,1)} %param.9, f32[192]{0:T(256)S(1)} %multiply_reduce_fusion.7, f32[192]{0:T(256)S(1)} %multiply_reduce_fusion.11, bf16[192,256]{1,0:T(8,128)(2,1)S(1)} %collective-permute-done.3), kind=kOutput, calls=%fused_computation.100 | convolution fusion | flops 19058688 | bytes 247296 | tf_op jit(solution)/shard_map/dot_general | solution.py:39
  21.0 1.1 %fusion.88 = f32[192,128]{1,0:T(8,128)S(1)} fusion(bf16[192,128]{1,0:T(8,128)(2,1)} %param.9, f32[192]{0:T(256)S(1)} %multiply_reduce_fusion.8, f32[192]{0:T(256)S(1)} %multiply_reduce_fusion.11, bf16[192,256]{1,0:T(8,128)(2,1)S(1)} %collective-permute-done.2), kind=kOutput, calls=%fused_computation.101 | convolution fusion | flops 19058688 | bytes 247296 | tf_op jit(solution)/shard_map/dot_general | solution.py:39
  22.2 1.1 %fusion.94 = f32[192,128]{1,0:T(8,128)S(1)} fusion(f32[192,128]{1,0:T(8,128)S(1)} %fusion.95, bf16[192,128]{1,0:T(8,128)(2,1)} %param.9, f32[192]{0:T(256)S(1)} %multiply_reduce_fusion.10, f32[192]{0:T(256)S(1)} %multiply_reduce_fusion.11, bf16[192,256]{1,0:T(8,128)(2,1)S(1)} %collective-permute-done), kind=kOutput, calls=%fused_computation.107 | convolution fusion | flops 19083264 | bytes 345600 | tf_op jit(solution)/shard_map/dot_general | solution.py:39
  23.4 1.1 %fusion.92 = f32[192,128]{1,0:T(8,128)S(1)} fusion(f32[192,128]{1,0:T(8,128)S(1)} %fusion.87, f32[192,128]{1,0:T(8,128)S(1)} %fusion.88, f32[192,128]{1,0:T(8,128)S(1)} %fusion.94, bf16[192,128]{1,0:T(8,128)(2,1)} %param.9, f32[192]{0:T(256)S(1)} %multiply_reduce_fusion.9, f32[192]{0:T(256)S(1)} %multiply_reduce_fusion.11, ...), kind=kOutput, calls=%fused_computation.105 | convolution fusion | flops 19132416 | bytes 542208 | tf_op jit(solution)/shard_map/dot_general | solution.py:39
  24.7 0.1 multiply_reduce_fusion.4
  24.8 0.6 collective-permute-start.8
  25.5 0.3 fusion.80
  25.9 0.3 fusion.81
  26.2 0.1 multiply_reduce_fusion.6
  26.3 0.6 %collective-permute-done.8 = bf16[192,256]{1,0:T(8,128)(2,1)S(1)} collective-permute-done((bf16[192,256]{1,0:T(8,128)(2,1)S(1)}, bf16[192,256]{1,0:T(8,128)(2,1)S(1)}, u32[]{:S(2)}, u32[]{:S(2)}) %collective-permute-start.8) | collective-permute-done | bytes 98336 | tf_op jit(solution)/shard_map/ppermute | solution.py:126
  27.1 0.3 multiply_reduce_fusion
  27.4 0.5 fusion.17
  28.0 0.3 fusion.86
  28.3 0.4 multiply_reduce_fusion.2
  28.8 2.1 %collective-permute-start.11 = (bf16[208,128]{1,0:T(8,128)(2,1)S(1)}, bf16[208,128]{1,0:T(8,128)(2,1)S(1)}, u32[]{:S(2)}, u32[]{:S(2)}) collective-permute-start(bf16[208,128]{1,0:T(8,128)(2,1)S(1)} %get-tuple-element.38), channel_id=1, source_target_pairs={{0,12},{4,0},{8,4},{12,8},{1,13},{5,1},{9,5},{13,9},{2,14},{6,2},{... | collective-permute-start | bytes 159752 | tf_op jit(solution)/shard_map/ppermute | solution.py:111
  30.9 0.6 %collective-permute-start.9 = (bf16[208,128]{1,0:T(8,128)(2,1)S(1)}, bf16[208,128]{1,0:T(8,128)(2,1)S(1)}, u32[]{:S(2)}, u32[]{:S(2)}) collective-permute-start(bf16[208,128]{1,0:T(8,128)(2,1)S(1)} %get-tuple-element.38), channel_id=1, source_target_pairs={{0,4},{4,8},{8,12},{12,0},{1,5},{5,9},{9,13},{13,1},{2,6},{6,10},{... | collective-permute-start | bytes 159752 | tf_op jit(solution)/shard_map/ppermute | solution.py:111
  31.6 1.5 %collective-permute-start.12 = (bf16[208,128]{1,0:T(8,128)(2,1)S(1)}, bf16[208,128]{1,0:T(8,128)(2,1)S(1)}, u32[]{:S(2)}, u32[]{:S(2)}) collective-permute-start(bf16[208,128]{1,0:T(8,128)(2,1)S(1)} %get-tuple-element.38), channel_id=1, source_target_pairs={{0,2},{1,3},{2,0},{3,1},{4,6},{5,7},{6,4},{7,5},{8,10},{9,11},{10,... | collective-permute-start | bytes 159752 | tf_op jit(solution)/shard_map/ppermute | solution.py:125
  33.1 6.1 %gather_fusion = f32[1024]{0:T(1024)S(1)} fusion(f32[3072]{0:T(1024)S(1)} %concatenate.31, s32[1024]{0:T(1024)S(1)} %get-tuple-element.29), kind=kCustom, calls=%fused_computation | custom fusion | bytes 12288 | tf_op jit(solution)/shard_map/jit(_take)/gather | solution.py:193
  39.3 3.2 %gather_fusion.1 = bf16[1024,128]{1,0:T(8,128)(2,1)S(1)} fusion(bf16[3072,128]{1,0:T(8,128)(2,1)S(1)} %constant_dynamic-update-slice_fusion.7, s32[1024]{0:T(1024)S(1)} %get-tuple-element.29), kind=kCustom, calls=%fused_computation.1 | custom fusion | bytes 528384 | tf_op jit(solution)/shard_map/jit(_take)/gather | solution.py:192
  42.5 3.4 %exponential_convert_fusion = bf16[3072,1024]{1,0:T(8,128)(2,1)S(1)} fusion(bf16[3072,128]{1,0:T(8,128)(2,1)S(1)} %constant_dynamic-update-slice_fusion.7, f32[1024]{0:T(1024)S(1)} %get-tuple-element.27, f32[3072]{0:T(1024)S(1)} %concatenate.31, bf16[1024,128]{1,0:T(8,128)(2,1)S(1)} %gather_fusion.1, pred[1024]{0:T(1024)(128)(4,1)S(1)} %get-tuple-element.28), kind=kOutput, calls=%fused_computation.2 | convolution fusion | flops 821166080 | bytes 7357440 | tf_op jit(solution)/shard_map/dot_general | solution.py:19
  45.9 0.3 fusion.111
  46.3 0.6 %collective-permute-start.13 = (bf16[624,128]{1,0:T(8,128)(2,1)S(1)}, bf16[624,128]{1,0:T(8,128)(2,1)S(1)}, u32[]{:S(2)}, u32[]{:S(2)}) collective-permute-start(bf16[624,128]{1,0:T(8,128)(2,1)S(1)} %get-tuple-element.39), channel_id=1, source_target_pairs={{0,2},{1,3},{2,0},{3,1},{4,6},{5,7},{6,4},{7,5},{8,10},{9,11},{10,... | collective-permute-start | bytes 479240 | tf_op jit(solution)/shard_map/ppermute | solution.py:126
  46.9 0.3 fusion.109
  47.3 4.3 %collective-permute-done.13 = bf16[624,128]{1,0:T(8,128)(2,1)S(1)} collective-permute-done((bf16[624,128]{1,0:T(8,128)(2,1)S(1)}, bf16[624,128]{1,0:T(8,128)(2,1)S(1)}, u32[]{:S(2)}, u32[]{:S(2)}) %collective-permute-start.13) | collective-permute-done | bytes 159776 | tf_op jit(solution)/shard_map/ppermute | solution.py:126
  51.8 0.4 fusion.29
  52.2 0.5 fusion.9
  52.7 0.5 fusion.20
  53.3 0.5 sqrt_bitcast_fusion
  53.8 0.4 fusion.105
  54.2 0.7 %copy-done = f32[1024,1024]{1,0:T(8,128)S(1)} copy-done((f32[1024,1024]{1,0:T(8,128)S(1)}, f32[1024,1024]{1,0:T(8,128)}, u32[]{:S(2)}) %copy-start) | copy-done | bytes 4194328
  54.9 0.7 %fusion.11 = f32[1024,256]{0,1:T(8,128)S(1)} fusion(f32[1024,1024]{1,0:T(8,128)S(1)} %copy-done, bf16[1024,128]{0,1:T(8,128)(2,1)S(1)} %get-tuple-element.33, bf16[1024,128]{0,1:T(8,128)(2,1)S(1)} %get-tuple-element.34), kind=kOutput, calls=%fused_computation.16 | convolution fusion | flops 540016640 | bytes 5767168 | tf_op jit(solution)/shard_map/dot_general | solution.py:214
  55.7 0.8 %fusion.25 = bf16[1024,128]{0,1:T(8,128)(2,1)S(1)} fusion(bf16[1024,128]{0,1:T(8,128)(2,1)S(1)} %get-tuple-element.34, f32[1024,1024]{1,0:T(8,128)S(1)} %copy-done, f32[1024,256]{0,1:T(8,128)S(1)} %fusion.11), kind=kOutput, calls=%fused_computation.31 | convolution fusion | flops 271974400 | bytes 5767168 | tf_op jit(solution)/shard_map/dot_general | solution.py:216
  56.5 1.2 %fusion.98 = f32[192,128]{1,0:T(8,128)} fusion(f32[192,128]{1,0:T(8,128)S(1)} %copy-done.3, f32[192,128]{1,0:T(8,128)S(1)} %get-tuple-element.46, bf16[1024,128]{0,1:T(8,128)(2,1)S(1)} %fusion.25, bf16[192,128]{1,0:T(8,128)(2,1)S(1)} %copy-done.1, f32[1024]{0:T(1024)S(1)} %get-tuple-element.27, f32[192]{0:T(256)S(1)} %multiply_reduce_fusion.11, ...), kind=kOutput, calls=%fused_computation.111 | convolution fusion | flops 101851136 | bytes 874240 | tf_op jit(solution)/shard_map/dot_general | solution.py:217
  (68 shorter events, 1.5 us)
Async XLA Ops:
  0.6 24.8 %copy-start.1 = (bf16[192,128]{1,0:T(8,128)(2,1)S(1)}, bf16[192,128]{1,0:T(8,128)(2,1)}, u32[]{:S(2)}) copy-start(bf16[192,128]{1,0:T(8,128)(2,1)} %param.9) | copy-start | bytes 147460
  2.4 17.3 %collective-permute-start.3 = (bf16[192,256]{1,0:T(8,128)(2,1)S(1)}, bf16[192,256]{1,0:T(8,128)(2,1)S(1)}, u32[]{:S(2)}, u32[]{:S(2)}) collective-permute-start(bf16[192,256]{1,0:T(8,128)(2,1)S(1)} %get-tuple-element.35), channel_id=1, source_target_pairs={{0,2},{1,3},{2,0},{3,1},{4,6},{5,7},{6,4},{7,5},{8,10},{9,11},{10,... | collective-permute-start | bytes 294920 | tf_op jit(solution)/shard_map/ppermute | solution.py:123
  5.4 9.3 %collective-permute-start.2 = (bf16[192,256]{1,0:T(8,128)(2,1)S(1)}, bf16[192,256]{1,0:T(8,128)(2,1)S(1)}, u32[]{:S(2)}, u32[]{:S(2)}) collective-permute-start(bf16[192,256]{1,0:T(8,128)(2,1)S(1)} %get-tuple-element.35), channel_id=1, source_target_pairs={{0,12},{4,0},{8,4},{12,8},{1,13},{5,1},{9,5},{13,9},{2,14},{6,2},{... | collective-permute-start | bytes 294920 | tf_op jit(solution)/shard_map/ppermute | solution.py:111
  9.0 8.3 %collective-permute-start.1 = (bf16[192,256]{1,0:T(8,128)(2,1)S(1)}, bf16[192,256]{1,0:T(8,128)(2,1)S(1)}, u32[]{:S(2)}, u32[]{:S(2)}) collective-permute-start(bf16[192,256]{1,0:T(8,128)(2,1)S(1)} %get-tuple-element.35), channel_id=1, source_target_pairs={{0,8},{4,12},{8,0},{12,4},{1,9},{5,13},{9,1},{13,5},{2,10},{6,14},... | collective-permute-start | bytes 294920 | tf_op jit(solution)/shard_map/ppermute | solution.py:111
  9.0 9.0 %collective-permute-start = (bf16[192,256]{1,0:T(8,128)(2,1)S(1)}, bf16[192,256]{1,0:T(8,128)(2,1)S(1)}, u32[]{:S(2)}, u32[]{:S(2)}) collective-permute-start(bf16[192,256]{1,0:T(8,128)(2,1)S(1)} %get-tuple-element.35), channel_id=1, source_target_pairs={{0,4},{4,8},{8,12},{12,0},{1,5},{5,9},{9,13},{13,1},{2,6},{6,10},{... | collective-permute-start | bytes 294920 | tf_op jit(solution)/shard_map/ppermute | solution.py:111
  14.7 13.6 %copy-start.2 = (f32[192,128]{1,0:T(8,128)S(1)}, f32[192,128]{1,0:T(8,128)}, u32[]{:S(2)}) copy-start(f32[192,128]{1,0:T(8,128)} %param.11) | copy-start | bytes 294916
  14.7 13.6 %copy-start.3 = (f32[192,128]{1,0:T(8,128)S(1)}, f32[192,128]{1,0:T(8,128)}, u32[]{:S(2)}) copy-start(f32[192,128]{1,0:T(8,128)} %param.10) | copy-start | bytes 294916
  14.7 9.9 %collective-permute-start.6 = (bf16[192,256]{1,0:T(8,128)(2,1)S(1)}, bf16[192,256]{1,0:T(8,128)(2,1)S(1)}, u32[]{:S(2)}, u32[]{:S(2)}) collective-permute-start(bf16[192,256]{1,0:T(8,128)(2,1)S(1)} %collective-permute-done.2), channel_id=1, source_target_pairs={{0,2},{1,3},{2,0},{3,1},{4,6},{5,7},{6,4},{7,5},{8,10},{9,11},{10,... | collective-permute-start | bytes 294920 | tf_op jit(solution)/shard_map/ppermute | solution.py:123
  17.4 7.2 %collective-permute-start.5 = (bf16[192,256]{1,0:T(8,128)(2,1)S(1)}, bf16[192,256]{1,0:T(8,128)(2,1)S(1)}, u32[]{:S(2)}, u32[]{:S(2)}) collective-permute-start(bf16[192,256]{1,0:T(8,128)(2,1)S(1)} %collective-permute-done.1), channel_id=1, source_target_pairs={{0,2},{1,3},{2,0},{3,1},{4,6},{5,7},{6,4},{7,5},{8,10},{9,11},{10,... | collective-permute-start | bytes 294920 | tf_op jit(solution)/shard_map/ppermute | solution.py:123
  18.0 6.5 %collective-permute-start.4 = (bf16[192,256]{1,0:T(8,128)(2,1)S(1)}, bf16[192,256]{1,0:T(8,128)(2,1)S(1)}, u32[]{:S(2)}, u32[]{:S(2)}) collective-permute-start(bf16[192,256]{1,0:T(8,128)(2,1)S(1)} %collective-permute-done), channel_id=1, source_target_pairs={{0,2},{1,3},{2,0},{3,1},{4,6},{5,7},{6,4},{7,5},{8,10},{9,11},{10,... | collective-permute-start | bytes 294920 | tf_op jit(solution)/shard_map/ppermute | solution.py:123
  24.6 2.5 %collective-permute-start.7 = (bf16[1344,256]{1,0:T(8,128)(2,1)S(1)}, bf16[1344,256]{1,0:T(8,128)(2,1)S(1)}, u32[]{:S(2)}, u32[]{:S(2)}) collective-permute-start(bf16[1344,256]{1,0:T(8,128)(2,1)S(1)} %constant_dynamic-update-slice_fusion), channel_id=1, source_target_pairs={{0,1},{1,0},{2,3},{3,2},{4,5},{5,4},{6,7},{7,6},{8,9},{9,8},{10,11... | collective-permute-start | bytes 2064392 | tf_op jit(solution)/shard_map/ppermute | solution.py:125
  24.8 2.1 %collective-permute-start.8 = (bf16[192,256]{1,0:T(8,128)(2,1)S(1)}, bf16[192,256]{1,0:T(8,128)(2,1)S(1)}, u32[]{:S(2)}, u32[]{:S(2)}) collective-permute-start(bf16[192,256]{1,0:T(8,128)(2,1)S(1)} %collective-permute-done.6), channel_id=1, source_target_pairs={{0,1},{1,0},{2,3},{3,2},{4,5},{5,4},{6,7},{7,6},{8,9},{9,8},{10,11... | collective-permute-start | bytes 294920 | tf_op jit(solution)/shard_map/ppermute | solution.py:126
  28.7 27.8 %copy-start.4 = (f32[192,128]{1,0:T(8,128)}, f32[192,128]{1,0:T(8,128)S(1)}, u32[]{:S(2)}) copy-start(f32[192,128]{1,0:T(8,128)S(1)} %get-tuple-element.46) | copy-start | bytes 294916
  28.8 17.5 %collective-permute-start.11 = (bf16[208,128]{1,0:T(8,128)(2,1)S(1)}, bf16[208,128]{1,0:T(8,128)(2,1)S(1)}, u32[]{:S(2)}, u32[]{:S(2)}) collective-permute-start(bf16[208,128]{1,0:T(8,128)(2,1)S(1)} %get-tuple-element.38), channel_id=1, source_target_pairs={{0,12},{4,0},{8,4},{12,8},{1,13},{5,1},{9,5},{13,9},{2,14},{6,2},{... | collective-permute-start | bytes 159752 | tf_op jit(solution)/shard_map/ppermute | solution.py:111
  30.9 15.4 %collective-permute-start.10 = (bf16[208,128]{1,0:T(8,128)(2,1)S(1)}, bf16[208,128]{1,0:T(8,128)(2,1)S(1)}, u32[]{:S(2)}, u32[]{:S(2)}) collective-permute-start(bf16[208,128]{1,0:T(8,128)(2,1)S(1)} %get-tuple-element.38), channel_id=1, source_target_pairs={{0,8},{4,12},{8,0},{12,4},{1,9},{5,13},{9,1},{13,5},{2,10},{6,14},... | collective-permute-start | bytes 159752 | tf_op jit(solution)/shard_map/ppermute | solution.py:111
  30.9 15.3 %collective-permute-start.9 = (bf16[208,128]{1,0:T(8,128)(2,1)S(1)}, bf16[208,128]{1,0:T(8,128)(2,1)S(1)}, u32[]{:S(2)}, u32[]{:S(2)}) collective-permute-start(bf16[208,128]{1,0:T(8,128)(2,1)S(1)} %get-tuple-element.38), channel_id=1, source_target_pairs={{0,4},{4,8},{8,12},{12,0},{1,5},{5,9},{9,13},{13,1},{2,6},{6,10},{... | collective-permute-start | bytes 159752 | tf_op jit(solution)/shard_map/ppermute | solution.py:111
  31.6 15.3 %collective-permute-start.12 = (bf16[208,128]{1,0:T(8,128)(2,1)S(1)}, bf16[208,128]{1,0:T(8,128)(2,1)S(1)}, u32[]{:S(2)}, u32[]{:S(2)}) collective-permute-start(bf16[208,128]{1,0:T(8,128)(2,1)S(1)} %get-tuple-element.38), channel_id=1, source_target_pairs={{0,2},{1,3},{2,0},{3,1},{4,6},{5,7},{6,4},{7,5},{8,10},{9,11},{10,... | collective-permute-start | bytes 159752 | tf_op jit(solution)/shard_map/ppermute | solution.py:125
  46.3 5.3 %collective-permute-start.13 = (bf16[624,128]{1,0:T(8,128)(2,1)S(1)}, bf16[624,128]{1,0:T(8,128)(2,1)S(1)}, u32[]{:S(2)}, u32[]{:S(2)}) collective-permute-start(bf16[624,128]{1,0:T(8,128)(2,1)S(1)} %get-tuple-element.39), channel_id=1, source_target_pairs={{0,2},{1,3},{2,0},{3,1},{4,6},{5,7},{6,4},{7,5},{8,10},{9,11},{10,... | collective-permute-start | bytes 479240 | tf_op jit(solution)/shard_map/ppermute | solution.py:126
  47.2 5.0 %collective-permute-start.14 = (bf16[1040,128]{1,0:T(8,128)(2,1)S(1)}, bf16[1040,128]{1,0:T(8,128)(2,1)S(1)}, u32[]{:S(2)}, u32[]{:S(2)}) collective-permute-start(bf16[1040,128]{1,0:T(8,128)(2,1)S(1)} %constant_dynamic-update-slice_fusion.19), channel_id=1, source_target_pairs={{0,1},{1,0},{2,3},{3,2},{4,5},{5,4},{6,7},{7,6},{8,9},{9,8},{10,11... | collective-permute-start | bytes 798728 | tf_op jit(solution)/shard_map/ppermute | solution.py:125
  51.7 1.5 %collective-permute-start.15 = (bf16[624,128]{1,0:T(8,128)(2,1)S(1)}, bf16[624,128]{1,0:T(8,128)(2,1)S(1)}, u32[]{:S(2)}, u32[]{:S(2)}) collective-permute-start(bf16[624,128]{1,0:T(8,128)(2,1)S(1)} %collective-permute-done.13), channel_id=1, source_target_pairs={{0,1},{1,0},{2,3},{3,2},{4,5},{5,4},{6,7},{7,6},{8,9},{9,8},{10,11... | collective-permute-start | bytes 479240 | tf_op jit(solution)/shard_map/ppermute | solution.py:126
  52.7 2.2 %copy-start = (f32[1024,1024]{1,0:T(8,128)S(1)}, f32[1024,1024]{1,0:T(8,128)}, u32[]{:S(2)}) copy-start(f32[1024,1024]{1,0:T(8,128)} %param.13) | copy-start | bytes 12582916
